TPU v7x, 32 devices: a whole 2x2x4 slice. The times are simulated.
32 devices in a mesh: bucket: 8 (over z, x), rel: 4 (over y, core).
Axes of the slice: x: 2, y: 2, z: 4, core: 2. Of those that a mesh axis runs over, the one named last changes fastest.
Arguments:
- left_rows: float32 [8192, 512], P(('bucket', 'rel')), may hold values from -1.2 to 1.2
- left_state: float32 [8192], P(('bucket', 'rel')), may hold values from 1e-06 to 0.0001
- right_rows: float32 [8192, 512], P(('bucket', 'rel')), may hold values from -1.2 to 1.2
- right_state: float32 [8192], P(('bucket', 'rel')), may hold values from 1e-06 to 0.0001
- relations: bfloat16 [4, 512, 512], P('rel'), may hold values from -0.25 to 0.25
- fetch_ids: int32 [8, 4, 4], P('bucket', 'rel'), may hold values from 0 to 3
- edge_left: int32 [8, 4, 2, 512], P('bucket', 'rel'), may hold values from 0 to 255
- edge_right: int32 [8, 4, 2, 512], P('bucket', 'rel'), may hold values from 0 to 255
- edge_slot: int32 [8, 4, 2, 512], P('bucket', 'rel'), may hold values from 0 to 1
- edge_weight: int32 [8, 4, 2, 512], P('bucket', 'rel'), may hold values from 1 to 4
- matching: int32 [1], replicated, may hold values from 1 to 7
Outputs:
- left_out: float32 [8192, 512], P(('bucket', 'rel'))
- left_state_out: float32 [8192], P(('bucket', 'rel'))
- right_out: float32 [8192, 512], P(('bucket', 'rel'))
- right_state_out: float32 [8192], P(('bucket', 'rel'))
- rel_grad: float32 [4, 512, 512], P('rel')
Inputs may be any that keep to these rules, and one draw needn't show every extreme that they name: Bucket b is paired with bucket b XOR matching.
All inputs are finite; a program needn't handle non-finite values.
Results may differ from a plain program's by a relative error of at most 0.0015.
The roundings to bfloat16 on the way count: a program that leaves them out, or rounds other values in their place, can miss the bound.
Values may be sent and summed in bfloat16 or wider, within the bound.
No kernel may reach another device: no remote copies, remote signals or barrier semaphores. Data moves between devices by JAX's collectives and lax.ppermute only.
A program may use at most 64 MiB of HBM per device.

v0:
```python
import jax
import jax.numpy as jnp
from jax import lax
from jax.sharding import PartitionSpec as P

learn_rate = 0.1


def edge_targets(edge_left, edge_right, edge_slot, edge_weight, block_len):
    rows = jnp.arange(block_len, dtype=jnp.int32)
    weight = edge_weight.astype(jnp.float32)
    right_hot = (edge_right[:, None] == rows[None, :]).astype(jnp.bfloat16)
    left_hot = edge_left[:, None] == rows[None, :]
    targets = []
    for slot_index in range(2):
        scale = jnp.where(edge_slot == slot_index, weight, jnp.float32(0.0))
        left_w = jnp.where(left_hot, scale[:, None], jnp.float32(0.0)).astype(jnp.bfloat16)
        targets.append(
            lax.dot_general(
                left_w, right_hot, (((0,), (0,)), ((), ())), preferred_element_type=jnp.float32
            )
        )
    return targets


def adagrad(table, state, gradient):
    state_new = state + jnp.mean(gradient * gradient, axis=1)
    return (table - learn_rate * gradient / jnp.sqrt(state_new)[:, None], state_new)


def one_round(
    left_block,
    left_st,
    right_block,
    right_st,
    right_half,
    rel_pair,
    edge_left,
    edge_right,
    edge_slot,
    edge_weight,
):
    block_len = left_block.shape[0]
    left_half = left_block.astype(jnp.bfloat16)
    targets = edge_targets(edge_left, edge_right, edge_slot, edge_weight, block_len)
    grad_left = jnp.zeros(left_block.shape, jnp.float32)
    grad_right = jnp.zeros(right_half.shape, jnp.float32)
    rel_grads = []
    for slot_index in range(2):
        matrix = rel_pair[slot_index]
        projected = jnp.dot(left_half, matrix, preferred_element_type=jnp.float32).astype(
            jnp.bfloat16
        )
        scores = jnp.dot(projected, right_half.T, preferred_element_type=jnp.float32)
        score_grad = ((jax.nn.sigmoid(scores) - targets[slot_index]) / block_len).astype(
            jnp.bfloat16
        )
        carried = jnp.dot(score_grad, right_half, preferred_element_type=jnp.float32).astype(
            jnp.bfloat16
        )
        grad_left = grad_left + jnp.dot(carried, matrix.T, preferred_element_type=jnp.float32)
        grad_right = grad_right + jnp.dot(
            score_grad.T, projected, preferred_element_type=jnp.float32
        )
        rel_grads.append(jnp.dot(left_half.T, carried, preferred_element_type=jnp.float32))
    left_new, left_st_new = adagrad(left_block, left_st, grad_left)
    if right_block is None:
        return (left_new, left_st_new, None, (right_st, grad_right), rel_grads)
    right_new, right_st_new = adagrad(right_block, right_st, grad_right)
    return (left_new, left_st_new, right_new, right_st_new, rel_grads)


def partner_values(values, switch):
    count = lax.axis_size("bucket")

    def exchange(offset):
        pairs = [(b, b ^ offset) for b in range(count)]

        def run(*arrays):
            return tuple(lax.ppermute(array, "bucket", pairs) for array in arrays)

        return run

    branches = [exchange(offset) for offset in range(1, count)]
    return lax.switch(switch - 1, branches, *values)


def axis_bits(axis):
    count = lax.axis_size(axis)
    return [1 << j for j in range(count.bit_length() - 1)]


def halving_sum(chunks, axis, order, done=()):
    count = lax.axis_size(axis)
    index = lax.axis_index(axis)
    current = chunks
    done = list(done)
    for bit in order:
        lower = 1
        for other in axis_bits(axis):
            if other < bit and other not in done:
                lower *= 2
        upper = current.shape[0] // (2 * lower)
        split = current.reshape((upper, 2, lower) + current.shape[1:])
        mine = (index // bit) % 2
        keep = lax.dynamic_index_in_dim(split, mine, axis=1, keepdims=False)
        send = lax.dynamic_index_in_dim(split, 1 - mine, axis=1, keepdims=False)
        got = lax.ppermute(send, axis, [(k, k ^ bit) for k in range(count)])
        current = (keep + got).reshape((upper * lower,) + current.shape[1:])
        done.append(bit)
    return current[0]


def doubling_gather(piece, axis, order):
    count = lax.axis_size(axis)
    index = lax.axis_index(axis)
    current = piece[None]
    done = []
    for bit in order:
        lower = 1
        for other in done:
            if other < bit:
                lower *= 2
        upper = current.shape[0] // lower
        got = lax.ppermute(current, axis, [(k, k ^ bit) for k in range(count)])
        mine = (index // bit) % 2
        ours = current.reshape((upper, 1, lower) + piece.shape)
        theirs = got.reshape((upper, 1, lower) + piece.shape)
        joined = jnp.zeros((upper, 2, lower) + piece.shape, piece.dtype)
        joined = lax.dynamic_update_index_in_dim(joined, ours, mine, axis=1)
        joined = lax.dynamic_update_index_in_dim(joined, theirs, 1 - mine, axis=1)
        current = joined.reshape((upper * 2 * lower,) + piece.shape)
        done.append(bit)
    return current


def selected_term(gradients, rel_ids, devices, per_device, pieces, columns):
    width = gradients[0].shape[0]
    wanted = devices[:, None] * per_device + jnp.arange(per_device, dtype=jnp.int32)[None, :]
    total = jnp.zeros((devices.shape[0], per_device, width, columns.stop - columns.start), jnp.float32)
    for slot_index, gradient in enumerate(gradients):
        hit = (rel_ids[slot_index] == wanted)[:, :, None, None]
        total = total + jnp.where(hit, gradient[None, None, :, columns], jnp.float32(0.0))
    rows = per_device * width
    return total.reshape(devices.shape[0], pieces, rows // pieces, columns.stop - columns.start)


def split_bits(array, axis_names, bits_by_axis, order):
    lead = []
    shape = []
    for name in axis_names:
        bits = bits_by_axis[name]
        for bit in bits[::-1]:
            lead.append((name, bit))
            shape.append(2)
    array = array.reshape(tuple(shape) + array.shape[len(axis_names) :])
    perm = [lead.index(step) for step in order] + list(range(len(lead), array.ndim))
    return jnp.transpose(array, perm)


def halving_steps(current, order):
    for step_index, (name, bit) in enumerate(order):
        count = lax.axis_size(name)
        mine = (lax.axis_index(name) // bit) % 2
        keep = lax.dynamic_index_in_dim(current, mine, axis=0, keepdims=False)
        send = lax.dynamic_index_in_dim(current, 1 - mine, axis=0, keepdims=False)
        got = lax.ppermute(send, name, [(k, k ^ bit) for k in range(count)])
        current = keep + got
    return current


def doubling_steps(piece, name, order):
    count = lax.axis_size(name)
    current = piece
    dims = []
    for bit in order:
        got = lax.ppermute(current, name, [(k, k ^ bit) for k in range(count)])
        mine = (lax.axis_index(name) // bit) % 2
        current = jnp.where(mine == 0, jnp.stack([current, got]), jnp.stack([got, current]))
        dims = [bit] + dims
    natural = sorted(dims, reverse=True)
    current = jnp.transpose(current, [dims.index(bit) for bit in natural] + list(range(len(dims), current.ndim)))
    return current.reshape((-1,) + piece.shape[1:])


def reduce_gradients(gradients, rel_ids, rel_total, width, low, switch):
    rel_count = lax.axis_size("rel")
    bucket_count = lax.axis_size("bucket")
    per_device = rel_total // rel_count
    rel_bits = axis_bits("rel")
    bucket_bits = axis_bits("bucket")
    first = rel_bits[0]
    mine = (lax.axis_index("rel") // first) % 2
    owners = jnp.arange(rel_count, dtype=jnp.int32).reshape(-1, 2, first)
    kept = lax.dynamic_index_in_dim(owners, mine, axis=1, keepdims=False).reshape(-1)
    sent = lax.dynamic_index_in_dim(owners, 1 - mine, axis=1, keepdims=False).reshape(-1)
    rest = rel_bits[1:]
    bits_by_axis = {"rel": rest, "bucket": bucket_bits}
    rel_steps = [("rel", bit) for bit in rest]
    bucket_steps = [("bucket", bit) for bit in bucket_bits]
    streams = [
        (bucket_steps + rel_steps, bucket_bits[::-1]),
        (rel_steps + bucket_steps, bucket_bits[:1] + bucket_bits[1:][::-1]),
    ]
    band = width // len(streams)
    keeps = []
    sends = []
    for stream_index, (order, _) in enumerate(streams):
        columns = slice(stream_index * band, (stream_index + 1) * band)
        keep = selected_term(gradients, rel_ids, kept, per_device, bucket_count, columns)
        send = selected_term(gradients, rel_ids, sent, per_device, bucket_count, columns)
        got = lax.ppermute(send, "rel", [(k, k ^ first) for k in range(rel_count)])
        current = split_bits(keep + got, ("rel", "bucket"), bits_by_axis, order)
        name, bit = order[0]
        side = (lax.axis_index(name) // bit) % 2
        keeps.append(lax.dynamic_index_in_dim(current, side, axis=0, keepdims=False))
        sends.append(lax.dynamic_index_in_dim(current, 1 - side, axis=0, keepdims=False))
    count = lax.axis_size("bucket")

    def first_step(offset):
        pairs = [(b, b ^ offset) for b in range(count)]

        def run(low_part, *parts):
            moved = []
            for (order, _), part in zip(streams, parts):
                name, bit = order[0]
                size = lax.axis_size(name)
                moved.append(lax.ppermute(part, name, [(k, k ^ bit) for k in range(size)]))
            return (lax.ppermute(low_part, "bucket", pairs),) + tuple(moved)

        return run

    results = lax.switch(
        switch - 1, [first_step(offset) for offset in range(1, count)], low, *sends
    )
    block_low = results[0]
    outputs = []
    for (order, gather_order), keep, got in zip(streams, keeps, results[1:]):
        current = halving_steps(keep + got, order[1:])
        outputs.append(doubling_steps(current, "bucket", gather_order))
    return jnp.concatenate(outputs, axis=1), block_low


def on_device(
    left_rows,
    left_state,
    right_rows,
    right_state,
    relations,
    fetch_ids,
    edge_left,
    edge_right,
    edge_slot,
    edge_weight,
    matching,
):
    width = relations.shape[1]
    rel_table = doubling_gather(relations, "rel", axis_bits("rel")[::-1]).reshape(
        -1, width, width
    )
    rel_total = rel_table.shape[0]
    rel_ids = fetch_ids[0, 0]
    switch = matching[0]
    table_left, state_left = (left_rows, left_state)
    row_block, state_block = (right_rows, right_state)
    gradients = []
    right_half = row_block.astype(jnp.bfloat16)
    for round_index in range(2):
        rel_pair = jnp.take(rel_table, rel_ids[2 * round_index : 2 * round_index + 2], axis=0)
        table_left, state_left, row_block, state_block, rel_grads = one_round(
            table_left,
            state_left,
            row_block,
            state_block,
            right_half,
            rel_pair,
            edge_left[0, 0, round_index],
            edge_right[0, 0, round_index],
            edge_slot[0, 0, round_index],
            edge_weight[0, 0, round_index],
        )
        gradients.extend(rel_grads)
        if round_index == 0:
            rounded = lax.reduce_precision(row_block, exponent_bits=8, mantissa_bits=7)
            high = rounded.astype(jnp.bfloat16)
            low = (row_block - rounded).astype(jnp.bfloat16)
            right_half, state_block = partner_values((high, state_block), switch)
            block_high = right_half
            row_block = None

    right_st, grad_right = state_block
    owned, their_low = reduce_gradients(gradients, rel_ids, rel_total, width, low, switch)
    row_block, state_block = adagrad(
        block_high.astype(jnp.float32) + their_low.astype(jnp.float32), right_st, grad_right
    )
    return (table_left, state_left, row_block, state_block, owned.reshape(-1, width, width))


def solution(mesh):
    in_specs = (
        P(("bucket", "rel"), None),
        P(("bucket", "rel")),
        P(("bucket", "rel"), None),
        P(("bucket", "rel")),
        P("rel", None, None),
        P("bucket", "rel", None),
        P("bucket", "rel", None, None),
        P("bucket", "rel", None, None),
        P("bucket", "rel", None, None),
        P("bucket", "rel", None, None),
        P(),
    )
    out_specs = (
        P(("bucket", "rel"), None),
        P(("bucket", "rel")),
        P(("bucket", "rel"), None),
        P(("bucket", "rel")),
        P("rel", None, None),
    )
    return jax.shard_map(
        on_device, mesh=mesh, in_specs=in_specs, out_specs=out_specs, check_vma=False
    )
```

profile of v0, /device:TPU:0, one launch (start us, length us, event | category | flops | bytes accessed | tf_op | source)
XLA Modules:
  0.0 119.9 jit_solution(8266715904664559261)
XLA Ops:
  0.6 3.1 %collective-permute-start.35 = (bf16[1,1,512,512]{3,2,1,0:T(8,128)(2,1)}, bf16[1,1,512,512]{3,2,1,0:T(8,128)(2,1)S(1)}, u32[]{:S(2)}, u32[]{:S(2)}) collective-permute-start(bf16[1,1,512,512]{3,2,1,0:T(8,128)(2,1)} %bitcast.301), channel_id=1, source_target_pairs={{0,2},{1,3},{2,0},{3,1},{4,6},{5,7},{6,4},{7,5},{8,10},{9,11},{10,... | collective-permute-start | bytes 1572872 | tf_op jit(solution)/shard_map/ppermute | solution.py:125
  3.7 0.8 compare_and_fusion
  4.5 1.4 %fusion.56 = (s32[1,1,1]{2,1,0:T(1,128)}, s32[1,1,1]{2,1,0:T(1,128)}, s32[1,1,1]{2,1,0:T(1,128)}, s32[1,1,1]{2,1,0:T(1,128)}) fusion(s32[1,1,4]{2,1,0:T(1,128)} %param.32), kind=kLoop, calls=%fused_computation.182 | loop fusion | bytes 32 | tf_op jit(solution)/shard_map/slice | solution.py:142
  5.9 0.7 compare_bitcast_fusion.7
  6.6 1.9 %compare_bitcast_fusion.2 = (pred[2]{0:T(512)(128)(4,1)S(1)}, pred[2]{0:T(512)(128)(4,1)S(1)}, pred[2]{0:T(512)(128)(4,1)S(1)}) fusion(s32[2,1,1]{0,2,1:T(1,128)S(1)} %get-tuple-element.208, s32[]{:T(128)} %bitcast.41, s32[]{:T(128)} %bitcast.45, s32[]{:T(128)} %bitcast.48), kind=kLoop, calls=%fused_computation.156 | loop fusion | flops 6 | bytes 26 | tf_op jit(solution)/shard_map/eq | solution.py:142
  8.7 1.8 %convert_element_type.111 = bf16[256,512]{1,0:T(8,128)(2,1)} convert(f32[256,512]{1,0:T(8,128)} %param.27) | non-fusion elementwise | flops 131072 | bytes 786432 | tf_op jit(solution)/shard_map/convert_element_type | solution.py:44
  10.5 1.1 convert_element_type.113
  12.3 1.9 %compare_bitcast_fusion.6 = (pred[2]{0:T(512)(128)(4,1)S(1)}, pred[2]{0:T(512)(128)(4,1)S(1)}, pred[2]{0:T(512)(128)(4,1)S(1)}) fusion(s32[2,1,1]{0,2,1:T(1,128)S(1)} %get-tuple-element.172, s32[]{:T(128)} %bitcast.41, s32[]{:T(128)} %bitcast.45, s32[]{:T(128)} %bitcast.48), kind=kLoop, calls=%fused_computation.160 | loop fusion | flops 6 | bytes 26 | tf_op jit(solution)/shard_map/eq | solution.py:142
  14.4 1.5 %collective-permute-done.35 = bf16[1,1,512,512]{3,2,1,0:T(8,128)(2,1)S(1)} collective-permute-done((bf16[1,1,512,512]{3,2,1,0:T(8,128)(2,1)}, bf16[1,1,512,512]{3,2,1,0:T(8,128)(2,1)S(1)}, u32[]{:S(2)}, u32[]{:S(2)}) %collective-permute-start.35) | collective-permute-done | bytes 524320 | tf_op jit(solution)/shard_map/ppermute | solution.py:125
  16.3 2.3 %collective-permute-done.36 = bf16[2,1,512,512]{3,2,0,1:T(8,128)(2,1)S(1)} collective-permute-done((bf16[2,1,512,512]{3,2,0,1:T(8,128)(2,1)S(1)}, bf16[2,1,512,512]{3,2,0,1:T(8,128)(2,1)S(1)}, u32[]{:S(2)}, u32[]{:S(2)}) %collective-permute-start.36) | collective-permute-done | bytes 1048608 | tf_op jit(solution)/shard_map/ppermute | solution.py:125
  18.7 0.6 gather_fusion.1
  19.3 1.6 %gather_fusion = bf16[2,512,512]{2,1,0:T(8,128)(2,1)} fusion(bf16[4,512,512]{2,1,0:T(8,128)(2,1)S(1)} %bitcast.247, s32[1024]{0:T(1024)S(1)} %pad_clamp_fusion.1), kind=kCustom, calls=%fused_computation.clone | custom fusion | bytes 2097160 | tf_op jit(solution)/shard_map/jit(_take)/gather | solution.py:269
  20.9 1.5 %broadcast_select_fusion = (bf16[2,512,512]{2,1,0:T(8,128)(2,1)S(1)}, bf16[2,512,512]{2,1,0:T(8,128)(2,1)S(1)}) fusion(bf16[2,512,512]{2,1,0:T(8,128)(2,1)S(1)} %gather_fusion.1, pred[2]{0:T(512)(128)(4,1)S(1)} %get-tuple-element.179, bf16[2,512,512]{2,1,0:T(8,128)(2,1)} %gather_fusion, pred[2]{0:T(512)(128)(4,1)S(1)} %get-tuple-element.219), kind=kLoop, calls=%fused_computation.65 | loop fusion | flops 1048576 | bytes 4194308 | tf_op jit(solution)/shard_map/jit(_take)/select_n | solution.py:269
  27.5 0.9 fusion.20
  28.4 15.2 %conditional.4 = (bf16[256,512]{1,0:T(8,128)(2,1)}, f32[256]{0:T(256)}) conditional(s32[]{:T(128)} %bitcast.31, (bf16[256,512]{1,0:T(8,128)(2,1)S(1)}, f32[256]{0:T(256)S(1)}) %tuple.95, (bf16[256,512]{1,0:T(8,128)(2,1)S(1)}, f32[256]{0:T(256)S(1)}) %tuple.95, (bf16[256,512]{1,0:T(8,128)(2,1)S(1)}, ...), branch_computations={%region_2.4_spmd, %region_3.5_spmd, %region_4.6_spmd, %region_5.7_... | conditional | bytes 1052768 | solution.py:85
  28.4 2.8 %collective-permute-start.6 = (bf16[256,512]{1,0:T(8,128)(2,1)S(1)}, bf16[256,512]{1,0:T(8,128)(2,1)}, u32[]{:S(2)}, u32[]{:S(2)}) collective-permute-start(bf16[256,512]{1,0:T(8,128)(2,1)S(1)} %get-tuple-element.101), channel_id=1, source_target_pairs={{0,16},{4,20},{8,24},{12,28},{16,0},{20,4},{24,8},{28,12},{1,17},{... | collective-permute-start | bytes 786440 | tf_op jit(solution)/shard_map/cond/branch_3_fun/ppermute | solution.py:80
  31.3 12.3 %collective-permute-done.7 = f32[256]{0:T(256)} collective-permute-done((f32[256]{0:T(256)S(1)}, f32[256]{0:T(256)}, u32[]{:S(2)}, u32[]{:S(2)}) %collective-permute-start.7) | collective-permute-done | bytes 1056 | tf_op jit(solution)/shard_map/cond/branch_3_fun/ppermute | solution.py:80
  43.6 1.3 %fusion.7 = f32[256,256]{1,0:T(8,128)S(1)} fusion(bf16[256,512]{1,0:T(8,128)(2,1)S(1)} %convolution_convert_fusion.3, bf16[256,512]{1,0:T(8,128)(2,1)} %get-tuple-element.140), kind=kOutput, calls=%fused_computation.41 | convolution fusion | flops 67305472 | bytes 786432 | tf_op jit(solution)/shard_map/dot_general | solution.py:54
  45.4 1.2 convolution_convert_fusion.2
  47.5 1.2 %fusion.3 = f32[256,256]{1,0:T(8,128)S(1)} fusion(bf16[256,512]{1,0:T(8,128)(2,1)S(1)} %convolution_convert_fusion.1, bf16[256,512]{1,0:T(8,128)(2,1)} %get-tuple-element.140), kind=kOutput, calls=%fused_computation.35 | convolution fusion | flops 67305472 | bytes 786432 | tf_op jit(solution)/shard_map/dot_general | solution.py:54
  49.3 1.2 convolution_convert_fusion
  52.9 1.2 %fusion.47 = (f32[256]{0:T(256)S(1)}, f32[256]{0:T(256)}) fusion(f32[256]{0:T(256)} %get-tuple-element.142, f32[256]{0:T(256)S(1)} %get-tuple-element.227), kind=kLoop, calls=%fused_computation.173 | loop fusion | flops 512 | bytes 4096 | tf_op jit(solution)/shard_map/sqrt | solution.py:28
  55.4 1.0 divide_subtract_fusion.1
  56.6 0.7 add_add_fusion
  57.4 0.8 copy-done.5
  58.2 18.5 %conditional.5 = (f32[256,512]{1,0:T(8,128)S(1)}, f32[2,2,2,64,256]{4,3,0,1,2:T(8,128)S(1)}, f32[2,2,2,64,256]{4,3,0,1,2:T(8,128)}) conditional(s32[]{:T(128)} %bitcast.31, (f32[1,2,2,2,64,256]{5,4,0,1,2,3:T(8,128)S(1)}, f32[1,2,2,2,64,256]{5,4,1,2,3,0:T(8,128)S(1)}, bf16[256,512]{1,0:T(8,128)(2,1)S(1)}) %tuple.176, ...), branch_computations={%region_10.12_spmd, %region_11.13_spmd, %region_12.14_spmd, %regio... | conditional | flops 131072 | bytes 10223760
  58.3 1.6 %collective-permute-start.23 = (f32[2,2,2,64,256]{4,3,2,1,0:T(8,128)S(1)}, f32[2,2,2,64,256]{4,3,2,1,0:T(8,128)S(1)}, u32[]{:S(2)}, u32[]{:S(2)}) collective-permute-start(f32[2,2,2,64,256]{4,3,2,1,0:T(8,128)S(1)} %bitcast.295), channel_id=1, source_target_pairs={{0,4},{4,0},{8,12},{12,8},{16,20},{20,16},{24,28},{28,24},{1,5},{5... | collective-permute-start | bytes 1572872 | tf_op jit(solution)/shard_map/cond/branch_3_fun/ppermute | solution.py:228
  59.9 1.6 %collective-permute-start.24 = (f32[2,2,2,64,256]{4,3,2,1,0:T(8,128)S(1)}, f32[2,2,2,64,256]{4,3,2,1,0:T(8,128)S(1)}, u32[]{:S(2)}, u32[]{:S(2)}) collective-permute-start(f32[2,2,2,64,256]{4,3,2,1,0:T(8,128)S(1)} %bitcast.288), channel_id=1, source_target_pairs={{0,2},{1,3},{2,0},{3,1},{4,6},{5,7},{6,4},{7,5},{8,10},{9,11},{10,... | collective-permute-start | bytes 1572872 | tf_op jit(solution)/shard_map/cond/branch_3_fun/ppermute | solution.py:228
  61.5 14.3 %collective-permute-done.25 = bf16[256,512]{1,0:T(8,128)(2,1)S(1)} collective-permute-done((bf16[256,512]{1,0:T(8,128)(2,1)S(1)}, bf16[256,512]{1,0:T(8,128)(2,1)S(1)}, u32[]{:S(2)}, u32[]{:S(2)}) %collective-permute-start.25) | collective-permute-done | bytes 262176 | tf_op jit(solution)/shard_map/cond/branch_3_fun/ppermute | solution.py:229
  75.9 0.8 copy.55
  76.8 1.1 bitcast_add_fusion
  78.7 1.9 %divide_subtract_fusion = f32[256,512]{1,0:T(8,128)} fusion(f32[256,512]{1,0:T(8,128)S(1)} %get-tuple-element.228, f32[256,512]{1,0:T(8,128)S(1)} %get-tuple-element.145, bf16[256,512]{1,0:T(8,128)(2,1)} %get-tuple-element.140, f32[256]{0:T(256)S(1)} %get-tuple-element.169), kind=kLoop, calls=%fused_computation.80 | loop fusion | flops 655360 | bytes 1836032 | tf_op jit(solution)/shard_map/sub | solution.py:28
  80.6 4.7 %collective-permute-done.45 = f32[2,2,64,256]{3,2,0,1:T(8,128)S(1)} collective-permute-done((f32[2,2,64,256]{3,2,0,1:T(8,128)S(1)}, f32[2,2,64,256]{3,2,0,1:T(8,128)S(1)}, u32[]{:S(2)}, u32[]{:S(2)}) %collective-permute-start.45) | collective-permute-done | bytes 262176 | tf_op jit(solution)/shard_map/ppermute | solution.py:167
  85.8 2.4 %collective-permute-start.40 = (f32[2,64,256]{2,1,0:T(8,128)S(1)}, f32[2,64,256]{2,1,0:T(8,128)S(1)}, u32[]{:S(2)}, u32[]{:S(2)}) collective-permute-start(f32[2,64,256]{2,1,0:T(8,128)S(1)} %dynamic-slice_bitcast_fusion.5), channel_id=1, source_target_pairs={{0,16},{4,20},{8,24},{12,28},{16,0},{20,4},{24,8},{28,12},{1,17},{... | collective-permute-start | bytes 393224 | tf_op jit(solution)/shard_map/ppermute | solution.py:167
  88.2 2.9 %collective-permute-done.46 = f32[2,64,256]{2,1,0:T(8,128)S(1)} collective-permute-done((f32[2,64,256]{2,1,0:T(8,128)S(1)}, f32[2,64,256]{2,1,0:T(8,128)S(1)}, u32[]{:S(2)}, u32[]{:S(2)}) %collective-permute-start.46) | collective-permute-done | bytes 131104 | tf_op jit(solution)/shard_map/ppermute | solution.py:167
  91.2 1.2 collective-permute-start.47
  92.4 2.8 %collective-permute-done.40 = f32[2,64,256]{2,1,0:T(8,128)S(1)} collective-permute-done((f32[2,64,256]{2,1,0:T(8,128)S(1)}, f32[2,64,256]{2,1,0:T(8,128)S(1)}, u32[]{:S(2)}, u32[]{:S(2)}) %collective-permute-start.40) | collective-permute-done | bytes 131104 | tf_op jit(solution)/shard_map/ppermute | solution.py:167
  95.3 1.6 %collective-permute-done.47 = f32[64,256]{1,0:T(8,128)S(1)} collective-permute-done((f32[64,256]{1,0:T(8,128)S(1)}, f32[64,256]{1,0:T(8,128)S(1)}, u32[]{:S(2)}, u32[]{:S(2)}) %collective-permute-start.47) | collective-permute-done | bytes 65568 | tf_op jit(solution)/shard_map/ppermute | solution.py:167
  96.9 0.8 collective-permute-start.48
  97.8 1.8 %collective-permute-done.41 = f32[64,256]{1,0:T(8,128)S(1)} collective-permute-done((f32[64,256]{1,0:T(8,128)S(1)}, f32[64,256]{1,0:T(8,128)S(1)}, u32[]{:S(2)}, u32[]{:S(2)}) %collective-permute-start.41) | collective-permute-done | bytes 65568 | tf_op jit(solution)/shard_map/ppermute | solution.py:167
  99.6 1.6 %collective-permute-done.48 = f32[64,256]{1,0:T(8,128)S(1)} collective-permute-done((f32[64,256]{1,0:T(8,128)S(1)}, f32[64,256]{1,0:T(8,128)S(1)}, u32[]{:S(2)}, u32[]{:S(2)}) %collective-permute-start.48) | collective-permute-done | bytes 65568 | tf_op jit(solution)/shard_map/ppermute | solution.py:177
  101.3 1.3 %collective-permute-start.49 = (f32[2,64,256]{2,1,0:T(8,128)S(1)}, f32[2,64,256]{2,1,0:T(8,128)S(1)}, u32[]{:S(2)}, u32[]{:S(2)}) collective-permute-start(f32[2,64,256]{2,1,0:T(8,128)S(1)} %maximum_select_fusion.6), channel_id=1, source_target_pairs={{0,16},{4,20},{8,24},{12,28},{16,0},{20,4},{24,8},{28,12},{1,17},{... | collective-permute-start | bytes 393224 | tf_op jit(solution)/shard_map/ppermute | solution.py:177
  102.6 3.2 %collective-permute-done.42 = f32[64,256]{1,0:T(8,128)S(1)} collective-permute-done((f32[64,256]{1,0:T(8,128)S(1)}, f32[64,256]{1,0:T(8,128)S(1)}, u32[]{:S(2)}, u32[]{:S(2)}) %collective-permute-start.42) | collective-permute-done | bytes 65568 | tf_op jit(solution)/shard_map/ppermute | solution.py:177
  106.0 2.7 %collective-permute-done.49 = f32[2,64,256]{2,1,0:T(8,128)S(1)} collective-permute-done((f32[2,64,256]{2,1,0:T(8,128)S(1)}, f32[2,64,256]{2,1,0:T(8,128)S(1)}, u32[]{:S(2)}, u32[]{:S(2)}) %collective-permute-start.49) | collective-permute-done | bytes 131104 | tf_op jit(solution)/shard_map/ppermute | solution.py:177
  109.1 3.2 %collective-permute-done.43 = f32[2,64,256]{2,1,0:T(8,128)S(1)} collective-permute-done((f32[2,64,256]{2,1,0:T(8,128)S(1)}, f32[2,64,256]{2,1,0:T(8,128)S(1)}, u32[]{:S(2)}, u32[]{:S(2)}) %collective-permute-start.43) | collective-permute-done | bytes 131104 | tf_op jit(solution)/shard_map/ppermute | solution.py:177
  112.7 3.0 %collective-permute-done.50 = f32[2,2,64,256]{3,2,1,0:T(8,128)S(1)} collective-permute-done((f32[2,2,64,256]{3,2,1,0:T(8,128)S(1)}, f32[2,2,64,256]{3,2,1,0:T(8,128)S(1)}, u32[]{:S(2)}, u32[]{:S(2)}) %collective-permute-start.50) | collective-permute-done | bytes 262176 | tf_op jit(solution)/shard_map/ppermute | solution.py:177
  115.7 3.0 %collective-permute-done.44 = f32[2,2,64,256]{3,2,0,1:T(8,128)S(1)} collective-permute-done((f32[2,2,64,256]{3,2,0,1:T(8,128)S(1)}, f32[2,2,64,256]{3,2,0,1:T(8,128)S(1)}, u32[]{:S(2)}, u32[]{:S(2)}) %collective-permute-start.44) | collective-permute-done | bytes 262176 | tf_op jit(solution)/shard_map/ppermute | solution.py:177
  118.8 1.1 maximum_bitcast_fusion
  (119 shorter events, 14.1 us)
Async XLA Ops:
  0.6 13.7 %copy-start.4 = (bf16[1,512,512]{2,1,0:T(8,128)(2,1)S(1)}, bf16[1,512,512]{2,1,0:T(8,128)(2,1)}, u32[]{:S(2)}) copy-start(bf16[1,512,512]{2,1,0:T(8,128)(2,1)} %param.31) | copy-start | bytes 1572868
  0.6 15.2 %collective-permute-start.35 = (bf16[1,1,512,512]{3,2,1,0:T(8,128)(2,1)}, bf16[1,1,512,512]{3,2,1,0:T(8,128)(2,1)S(1)}, u32[]{:S(2)}, u32[]{:S(2)}) collective-permute-start(bf16[1,1,512,512]{3,2,1,0:T(8,128)(2,1)} %bitcast.301), channel_id=1, source_target_pairs={{0,2},{1,3},{2,0},{3,1},{4,6},{5,7},{6,4},{7,5},{8,10},{9,11},{10,... | collective-permute-start | bytes 1572872 | tf_op jit(solution)/shard_map/ppermute | solution.py:125
  10.4 5.5 %copy-start.7 = (s32[1,1,2,512]{3,2,1,0:T(2,128)S(1)}, s32[1,1,2,512]{3,2,1,0:T(2,128)}, u32[]{:S(2)}) copy-start(s32[1,1,2,512]{3,2,1,0:T(2,128)} %param.34) | copy-start | bytes 12292
  10.4 5.6 %copy-start.8 = (s32[1,1,2,512]{3,2,1,0:T(2,128)S(1)}, s32[1,1,2,512]{3,2,1,0:T(2,128)}, u32[]{:S(2)}) copy-start(s32[1,1,2,512]{3,2,1,0:T(2,128)} %param.33) | copy-start | bytes 12292
  10.4 5.6 %copy-start.9 = (s32[1,1,2,512]{3,2,1,0:T(2,128)S(1)}, s32[1,1,2,512]{3,2,1,0:T(2,128)}, u32[]{:S(2)}) copy-start(s32[1,1,2,512]{3,2,1,0:T(2,128)} %param.36) | copy-start | bytes 12292
  10.4 5.6 %copy-start.10 = (s32[1,1,2,512]{3,2,1,0:T(2,128)S(1)}, s32[1,1,2,512]{3,2,1,0:T(2,128)}, u32[]{:S(2)}) copy-start(s32[1,1,2,512]{3,2,1,0:T(2,128)} %param.35) | copy-start | bytes 12292
  15.9 2.7 %collective-permute-start.36 = (bf16[2,1,512,512]{3,2,0,1:T(8,128)(2,1)S(1)}, bf16[2,1,512,512]{3,2,0,1:T(8,128)(2,1)S(1)}, u32[]{:S(2)}, u32[]{:S(2)}) collective-permute-start(bf16[2,1,512,512]{3,2,0,1:T(8,128)(2,1)S(1)} %bitcast.268), channel_id=1, source_target_pairs={{0,1},{1,0},{2,3},{3,2},{4,5},{5,4},{6,7},{7,6},{8,9},{9,8},{10,11... | collective-permute-start | bytes 3145736 | tf_op jit(solution)/shard_map/ppermute | solution.py:125
  20.9 1.5 %copy-start.1 = (bf16[256,512]{1,0:T(8,128)(2,1)S(1)}, bf16[256,512]{1,0:T(8,128)(2,1)}, u32[]{:S(2)}) copy-start(bf16[256,512]{1,0:T(8,128)(2,1)} %convert_element_type.111) | copy-start | bytes 786436
  25.1 1.2 copy-start.6
  25.1 1.2 copy-start
  26.4 1.0 copy-start.11
  26.4 1.0 copy-start.3
  28.4 15.2 %collective-permute-start.6 = (bf16[256,512]{1,0:T(8,128)(2,1)S(1)}, bf16[256,512]{1,0:T(8,128)(2,1)}, u32[]{:S(2)}, u32[]{:S(2)}) collective-permute-start(bf16[256,512]{1,0:T(8,128)(2,1)S(1)} %get-tuple-element.101), channel_id=1, source_target_pairs={{0,16},{4,20},{8,24},{12,28},{16,0},{20,4},{24,8},{28,12},{1,17},{... | collective-permute-start | bytes 786440 | tf_op jit(solution)/shard_map/cond/branch_3_fun/ppermute | solution.py:80
  31.2 12.4 %collective-permute-start.7 = (f32[256]{0:T(256)S(1)}, f32[256]{0:T(256)}, u32[]{:S(2)}, u32[]{:S(2)}) collective-permute-start(f32[256]{0:T(256)S(1)} %get-tuple-element.102), channel_id=1, source_target_pairs={{0,16},{4,20},{8,24},{12,28},{16,0},{20,4},{24,8},{28,12},{1,17},{... | collective-permute-start | bytes 3080 | tf_op jit(solution)/shard_map/cond/branch_3_fun/ppermute | solution.py:80
  43.6 3.2 %copy-start.2 = (bf16[256,512]{1,0:T(8,128)(2,1)S(1)}, bf16[256,512]{1,0:T(8,128)(2,1)}, u32[]{:S(2)}) copy-start(bf16[256,512]{1,0:T(8,128)(2,1)} %convert_element_type.111) | copy-start | bytes 786436
  52.3 4.1 %collective-permute-start.38 = (f32[2,8,64,256]{3,2,1,0:T(8,128)S(1)}, f32[2,8,64,256]{3,2,1,0:T(8,128)S(1)}, u32[]{:S(2)}, u32[]{:S(2)}) collective-permute-start(f32[2,8,64,256]{3,2,1,0:T(8,128)S(1)} %get-tuple-element.205), channel_id=1, source_target_pairs={{0,1},{1,0},{2,3},{3,2},{4,5},{5,4},{6,7},{7,6},{8,9},{9,8},{10,11... | collective-permute-start | bytes 3145736 | tf_op jit(solution)/shard_map/ppermute | solution.py:212
  52.4 4.1 %collective-permute-start.37 = (f32[2,8,64,256]{3,2,1,0:T(8,128)S(1)}, f32[2,8,64,256]{3,2,1,0:T(8,128)S(1)}, u32[]{:S(2)}, u32[]{:S(2)}) collective-permute-start(f32[2,8,64,256]{3,2,1,0:T(8,128)S(1)} %get-tuple-element.206), channel_id=1, source_target_pairs={{0,1},{1,0},{2,3},{3,2},{4,5},{5,4},{6,7},{7,6},{8,9},{9,8},{10,11... | collective-permute-start | bytes 3145736 | tf_op jit(solution)/shard_map/ppermute | solution.py:212
  57.3 1.0 copy-start.5
  58.3 17.6 %collective-permute-start.23 = (f32[2,2,2,64,256]{4,3,2,1,0:T(8,128)S(1)}, f32[2,2,2,64,256]{4,3,2,1,0:T(8,128)S(1)}, u32[]{:S(2)}, u32[]{:S(2)}) collective-permute-start(f32[2,2,2,64,256]{4,3,2,1,0:T(8,128)S(1)} %bitcast.295), channel_id=1, source_target_pairs={{0,4},{4,0},{8,12},{12,8},{16,20},{20,16},{24,28},{28,24},{1,5},{5... | collective-permute-start | bytes 1572872 | tf_op jit(solution)/shard_map/cond/branch_3_fun/ppermute | solution.py:228
  59.9 16.0 %collective-permute-start.24 = (f32[2,2,2,64,256]{4,3,2,1,0:T(8,128)S(1)}, f32[2,2,2,64,256]{4,3,2,1,0:T(8,128)S(1)}, u32[]{:S(2)}, u32[]{:S(2)}) collective-permute-start(f32[2,2,2,64,256]{4,3,2,1,0:T(8,128)S(1)} %bitcast.288), channel_id=1, source_target_pairs={{0,2},{1,3},{2,0},{3,1},{4,6},{5,7},{6,4},{7,5},{8,10},{9,11},{10,... | collective-permute-start | bytes 1572872 | tf_op jit(solution)/shard_map/cond/branch_3_fun/ppermute | solution.py:228
  61.5 14.3 %collective-permute-start.25 = (bf16[256,512]{1,0:T(8,128)(2,1)S(1)}, bf16[256,512]{1,0:T(8,128)(2,1)S(1)}, u32[]{:S(2)}, u32[]{:S(2)}) collective-permute-start(bf16[256,512]{1,0:T(8,128)(2,1)S(1)} %get-tuple-element.120), channel_id=1, source_target_pairs={{0,16},{4,20},{8,24},{12,28},{16,0},{20,4},{24,8},{28,12},{1,17},{... | collective-permute-start | bytes 786440 | tf_op jit(solution)/shard_map/cond/branch_3_fun/ppermute | solution.py:229
  77.9 7.4 %collective-permute-start.45 = (f32[2,2,64,256]{3,2,0,1:T(8,128)S(1)}, f32[2,2,64,256]{3,2,0,1:T(8,128)S(1)}, u32[]{:S(2)}, u32[]{:S(2)}) collective-permute-start(f32[2,2,64,256]{3,2,0,1:T(8,128)S(1)} %dynamic-slice_bitcast_fusion.2), channel_id=1, source_target_pairs={{0,4},{4,0},{8,12},{12,8},{16,20},{20,16},{24,28},{28,24},{1,5},{5... | collective-permute-start | bytes 786440 | tf_op jit(solution)/shard_map/ppermute | solution.py:167
  78.6 7.1 %collective-permute-start.39 = (f32[2,2,64,256]{3,2,0,1:T(8,128)S(1)}, f32[2,2,64,256]{3,2,0,1:T(8,128)S(1)}, u32[]{:S(2)}, u32[]{:S(2)}) collective-permute-start(f32[2,2,64,256]{3,2,0,1:T(8,128)S(1)} %dynamic-slice_bitcast_fusion.3), channel_id=1, source_target_pairs={{0,8},{4,12},{8,0},{12,4},{16,24},{20,28},{24,16},{28,20},{1,9},{5... | collective-permute-start | bytes 786440 | tf_op jit(solution)/shard_map/ppermute | solution.py:167
  85.4 5.7 %collective-permute-start.46 = (f32[2,64,256]{2,1,0:T(8,128)S(1)}, f32[2,64,256]{2,1,0:T(8,128)S(1)}, u32[]{:S(2)}, u32[]{:S(2)}) collective-permute-start(f32[2,64,256]{2,1,0:T(8,128)S(1)} %dynamic-slice_bitcast_fusion.4), channel_id=1, source_target_pairs={{0,8},{4,12},{8,0},{12,4},{16,24},{20,28},{24,16},{28,20},{1,9},{5... | collective-permute-start | bytes 393224 | tf_op jit(solution)/shard_map/ppermute | solution.py:167
  85.8 9.3 %collective-permute-start.40 = (f32[2,64,256]{2,1,0:T(8,128)S(1)}, f32[2,64,256]{2,1,0:T(8,128)S(1)}, u32[]{:S(2)}, u32[]{:S(2)}) collective-permute-start(f32[2,64,256]{2,1,0:T(8,128)S(1)} %dynamic-slice_bitcast_fusion.5), channel_id=1, source_target_pairs={{0,16},{4,20},{8,24},{12,28},{16,0},{20,4},{24,8},{28,12},{1,17},{... | collective-permute-start | bytes 393224 | tf_op jit(solution)/shard_map/ppermute | solution.py:167
  91.2 5.7 %collective-permute-start.47 = (f32[64,256]{1,0:T(8,128)S(1)}, f32[64,256]{1,0:T(8,128)S(1)}, u32[]{:S(2)}, u32[]{:S(2)}) collective-permute-start(f32[64,256]{1,0:T(8,128)S(1)} %dynamic-slice_bitcast_fusion.6), channel_id=1, source_target_pairs={{0,16},{4,20},{8,24},{12,28},{16,0},{20,4},{24,8},{28,12},{1,17},{... | collective-permute-start | bytes 196616 | tf_op jit(solution)/shard_map/ppermute | solution.py:167
  95.2 4.3 %collective-permute-start.41 = (f32[64,256]{1,0:T(8,128)S(1)}, f32[64,256]{1,0:T(8,128)S(1)}, u32[]{:S(2)}, u32[]{:S(2)}) collective-permute-start(f32[64,256]{1,0:T(8,128)S(1)} %dynamic-slice_bitcast_fusion.7), channel_id=1, source_target_pairs={{0,2},{1,3},{2,0},{3,1},{4,6},{5,7},{6,4},{7,5},{8,10},{9,11},{10,... | collective-permute-start | bytes 196616 | tf_op jit(solution)/shard_map/ppermute | solution.py:167
  96.9 4.3 %collective-permute-start.48 = (f32[64,256]{1,0:T(8,128)S(1)}, f32[64,256]{1,0:T(8,128)S(1)}, u32[]{:S(2)}, u32[]{:S(2)}) collective-permute-start(f32[64,256]{1,0:T(8,128)S(1)} %bitcast_add_fusion.6), channel_id=1, source_target_pairs={{0,4},{4,0},{8,12},{12,8},{16,20},{20,16},{24,28},{28,24},{1,5},{5... | collective-permute-start | bytes 196616 | tf_op jit(solution)/shard_map/ppermute | solution.py:177
  99.5 6.3 %collective-permute-start.42 = (f32[64,256]{1,0:T(8,128)S(1)}, f32[64,256]{1,0:T(8,128)S(1)}, u32[]{:S(2)}, u32[]{:S(2)}) collective-permute-start(f32[64,256]{1,0:T(8,128)S(1)} %bitcast_add_fusion.7), channel_id=1, source_target_pairs={{0,16},{4,20},{8,24},{12,28},{16,0},{20,4},{24,8},{28,12},{1,17},{... | collective-permute-start | bytes 196616 | tf_op jit(solution)/shard_map/ppermute | solution.py:177
  101.3 7.4 %collective-permute-start.49 = (f32[2,64,256]{2,1,0:T(8,128)S(1)}, f32[2,64,256]{2,1,0:T(8,128)S(1)}, u32[]{:S(2)}, u32[]{:S(2)}) collective-permute-start(f32[2,64,256]{2,1,0:T(8,128)S(1)} %maximum_select_fusion.6), channel_id=1, source_target_pairs={{0,16},{4,20},{8,24},{12,28},{16,0},{20,4},{24,8},{28,12},{1,17},{... | collective-permute-start | bytes 393224 | tf_op jit(solution)/shard_map/ppermute | solution.py:177
  105.9 6.4 %collective-permute-start.43 = (f32[2,64,256]{2,1,0:T(8,128)S(1)}, f32[2,64,256]{2,1,0:T(8,128)S(1)}, u32[]{:S(2)}, u32[]{:S(2)}) collective-permute-start(f32[2,64,256]{2,1,0:T(8,128)S(1)} %maximum_select_fusion.4), channel_id=1, source_target_pairs={{0,8},{4,12},{8,0},{12,4},{16,24},{20,28},{24,16},{28,20},{1,9},{5... | collective-permute-start | bytes 393224 | tf_op jit(solution)/shard_map/ppermute | solution.py:177
  108.7 7.0 %collective-permute-start.50 = (f32[2,2,64,256]{3,2,1,0:T(8,128)S(1)}, f32[2,2,64,256]{3,2,1,0:T(8,128)S(1)}, u32[]{:S(2)}, u32[]{:S(2)}) collective-permute-start(f32[2,2,64,256]{3,2,1,0:T(8,128)S(1)} %maximum_select_fusion.3), channel_id=1, source_target_pairs={{0,8},{4,12},{8,0},{12,4},{16,24},{20,28},{24,16},{28,20},{1,9},{5... | collective-permute-start | bytes 786440 | tf_op jit(solution)/shard_map/ppermute | solution.py:177
  112.3 6.4 %collective-permute-start.44 = (f32[2,2,64,256]{3,2,0,1:T(8,128)S(1)}, f32[2,2,64,256]{3,2,0,1:T(8,128)S(1)}, u32[]{:S(2)}, u32[]{:S(2)}) collective-permute-start(f32[2,2,64,256]{3,2,0,1:T(8,128)S(1)} %maximum_select_fusion.2), channel_id=1, source_target_pairs={{0,4},{4,0},{8,12},{12,8},{16,20},{20,16},{24,28},{28,24},{1,5},{5... | collective-permute-start | bytes 786440 | tf_op jit(solution)/shard_map/ppermute | solution.py:177
where the time goes:
time: 118 us; the launch traced here: 120 us
  waiting for transfers between devices  61.3 us (52%)
  other arithmetic  19.6 us (17%)
  starting transfers between devices  17.1 us (14%)
  matrix products  13.2 us (11%)
  local copies, waits for them, and re-layouts  6.47 us (5%)
  between operations  2.18 us (2%)
    ppermute x6, waiting for transfers between devices, doubling_steps(): got = lax.ppermute(current, name, [(k, k ^ bit) for k in range(count)])  16.8 us
    ppermute x1, waiting for transfers between devices, run(): return (lax.ppermute(low_part, 'bucket', pairs),) + tuple(moved)  14.3 us
    ppermute x6, waiting for transfers between devices, halving_steps(): got = lax.ppermute(send, name, [(k, k ^ bit) for k in range(count)])  14.1 us
    ppermute x2, waiting for transfers between devices, run(): return tuple((lax.ppermute(array, 'bucket', pairs) for array in arrays))  12.3 us
    eq x3, other arithmetic, selected_term(): hit = (rel_ids[slot_index] == wanted)[:, :, None, None]  4.55 us
    ppermute x6, starting transfers between devices, halving_steps(): got = lax.ppermute(send, name, [(k, k ^ bit) for k in range(count)])  4.37 us
    ppermute x2, waiting for transfers between devices, doubling_gather(): got = lax.ppermute(current, axis, [(k, k ^ bit) for k in range(count)])  3.73 us
    ppermute x2, starting transfers between devices, run(): moved.append(lax.ppermute(part, name, [(k, k ^ bit) for k in range(size)]))  3.19 us
  transfers between devices with their start and end apart: 21, of which 17 were waited for; matrix products, arithmetic and copies ran while one was open for 13% of the time, Pallas kernels for 0%

commit v1 on v0

--- a/solution.py
+++ b/solution.py
@@ -203,14 +203,15 @@
         (rel_steps + bucket_steps, bucket_bits[:1] + bucket_bits[1:][::-1]),
     ]
     band = width // len(streams)
+    everything = slice(0, width)
+    keep = selected_term(gradients, rel_ids, kept, per_device, bucket_count, everything)
+    send = selected_term(gradients, rel_ids, sent, per_device, bucket_count, everything)
+    full = keep + lax.ppermute(send, "rel", [(k, k ^ first) for k in range(rel_count)])
     keeps = []
     sends = []
     for stream_index, (order, _) in enumerate(streams):
-        columns = slice(stream_index * band, (stream_index + 1) * band)
-        keep = selected_term(gradients, rel_ids, kept, per_device, bucket_count, columns)
-        send = selected_term(gradients, rel_ids, sent, per_device, bucket_count, columns)
-        got = lax.ppermute(send, "rel", [(k, k ^ first) for k in range(rel_count)])
-        current = split_bits(keep + got, ("rel", "bucket"), bits_by_axis, order)
+        part = full[..., stream_index * band : (stream_index + 1) * band]
+        current = split_bits(part, ("rel", "bucket"), bits_by_axis, order)
         name, bit = order[0]
         side = (lax.axis_index(name) // bit) % 2
         keeps.append(lax.dynamic_index_in_dim(current, side, axis=0, keepdims=False))
@@ -284,7 +285,18 @@
             rounded = lax.reduce_precision(row_block, exponent_bits=8, mantissa_bits=7)
             high = rounded.astype(jnp.bfloat16)
             low = (row_block - rounded).astype(jnp.bfloat16)
-            right_half, state_block = partner_values((high, state_block), switch)
+            state_rounded = lax.reduce_precision(state_block, exponent_bits=8, mantissa_bits=7)
+            state_pair = jnp.concatenate([state_rounded, state_block - state_rounded])
+            block_len, row_width = high.shape
+            state_rows = -(-state_pair.shape[0] // row_width)
+            state_pair = jnp.pad(state_pair, (0, state_rows * row_width - state_pair.shape[0]))
+            packed = jnp.concatenate(
+                [high, state_pair.astype(jnp.bfloat16).reshape(state_rows, row_width)]
+            )
+            (their_packed,) = partner_values((packed,), switch)
+            right_half = their_packed[:block_len]
+            their_state = their_packed[block_len:].reshape(-1).astype(jnp.float32)
+            state_block = their_state[:block_len] + their_state[block_len : 2 * block_len]
             block_high = right_half
             row_block = None
 

time: 118 us -> 119 us (level)
  matrix products: 13.2 us -> 15.4 us
    dot_general x4, matrix products: 1.29 us -> 2.7 us  [one_round(): jnp.dot(left_half, matrix, preferred_element_type=jnp.float32)]
    ppermute x2 -> x1, waiting for transfers between devices: 12.3 us -> 12.7 us  [run(): return tuple((lax.ppermute(array, 'bucket', pairs) for array in arrays))]
    ppermute x2 -> x1, starting transfers between devices: 2.92 us -> 2.88 us  [run(): return tuple((lax.ppermute(array, 'bucket', pairs) for array in arrays))]
  transfers between devices with their start and end apart: 21 -> 19, of which waited for: 17 -> 16; matrix products, arithmetic and copies ran while one was open for 13% -> 15% of each run, Pallas kernels for 0% -> 0%
where the time goes in v1:
time: 119 us; the launch traced here: 121 us
  waiting for transfers between devices  61.9 us (52%)
  other arithmetic  18.9 us (16%)
  starting transfers between devices  16.5 us (14%)
  matrix products  15.4 us (13%)
  local copies, waits for them, and re-layouts  5.73 us (5%)
  between operations  2.19 us (2%)
    ppermute x6, waiting for transfers between devices, doubling_steps(): got = lax.ppermute(current, name, [(k, k ^ bit) for k in range(count)])  16.8 us
    ppermute x1, waiting for transfers between devices, run(): return (lax.ppermute(low_part, 'bucket', pairs),) + tuple(moved)  14.6 us
    ppermute x6, waiting for transfers between devices, halving_steps(): got = lax.ppermute(send, name, [(k, k ^ bit) for k in range(count)])  14.1 us
    ppermute x1, waiting for transfers between devices, run(): return tuple((lax.ppermute(array, 'bucket', pairs) for array in arrays))  12.7 us
    eq x3, other arithmetic, selected_term(): hit = (rel_ids[slot_index] == wanted)[:, :, None, None]  4.55 us
    ppermute x6, starting transfers between devices, halving_steps(): got = lax.ppermute(send, name, [(k, k ^ bit) for k in range(count)])  4.35 us
    ppermute x2, waiting for transfers between devices, doubling_gather(): got = lax.ppermute(current, axis, [(k, k ^ bit) for k in range(count)])  3.73 us
    ppermute x2, starting transfers between devices, run(): moved.append(lax.ppermute(part, name, [(k, k ^ bit) for k in range(size)]))  3.2 us
  transfers between devices with their start and end apart: 19, of which 16 were waited for; matrix products, arithmetic and copies ran while one was open for 15% of the time, Pallas kernels for 0%

profile of v1, /device:TPU:0, one launch (start us, length us, event | category | flops | bytes accessed | tf_op | source)
XLA Modules:
  0.0 120.7 jit_solution(4131355446425266003)
XLA Ops:
  0.6 3.1 %collective-permute-start.28 = (bf16[1,1,512,512]{3,2,1,0:T(8,128)(2,1)}, bf16[1,1,512,512]{3,2,1,0:T(8,128)(2,1)S(1)}, u32[]{:S(2)}, u32[]{:S(2)}) collective-permute-start(bf16[1,1,512,512]{3,2,1,0:T(8,128)(2,1)} %bitcast.286), channel_id=1, source_target_pairs={{0,2},{1,3},{2,0},{3,1},{4,6},{5,7},{6,4},{7,5},{8,10},{9,11},{10,... | collective-permute-start | bytes 1572872 | tf_op jit(solution)/shard_map/ppermute | solution.py:125
  3.7 0.8 compare_and_fusion
  4.5 1.4 %fusion.58 = (s32[1,1,1]{2,1,0:T(1,128)}, s32[1,1,1]{2,1,0:T(1,128)}, s32[1,1,1]{2,1,0:T(1,128)}, s32[1,1,1]{2,1,0:T(1,128)}) fusion(s32[1,1,4]{2,1,0:T(1,128)} %param.32), kind=kLoop, calls=%fused_computation.185 | loop fusion | bytes 32 | tf_op jit(solution)/shard_map/slice | solution.py:142
  5.9 0.7 compare_bitcast_fusion.7
  6.6 1.9 %compare_bitcast_fusion.2 = (pred[2]{0:T(512)(128)(4,1)S(1)}, pred[2]{0:T(512)(128)(4,1)S(1)}, pred[2]{0:T(512)(128)(4,1)S(1)}) fusion(s32[2,1,1]{0,2,1:T(1,128)S(1)} %get-tuple-element.168, s32[]{:T(128)} %bitcast.41, s32[]{:T(128)} %bitcast.45, s32[]{:T(128)} %bitcast.48), kind=kLoop, calls=%fused_computation.158 | loop fusion | flops 6 | bytes 26 | tf_op jit(solution)/shard_map/eq | solution.py:142
  8.7 1.8 %convert_element_type.123 = bf16[256,512]{1,0:T(8,128)(2,1)} convert(f32[256,512]{1,0:T(8,128)} %param.27) | non-fusion elementwise | flops 131072 | bytes 786432 | tf_op jit(solution)/shard_map/convert_element_type | solution.py:44
  10.5 1.1 convert_element_type.125
  12.3 1.9 %compare_bitcast_fusion.6 = (pred[2]{0:T(512)(128)(4,1)S(1)}, pred[2]{0:T(512)(128)(4,1)S(1)}, pred[2]{0:T(512)(128)(4,1)S(1)}) fusion(s32[2,1,1]{0,2,1:T(1,128)S(1)} %get-tuple-element.141, s32[]{:T(128)} %bitcast.41, s32[]{:T(128)} %bitcast.45, s32[]{:T(128)} %bitcast.48), kind=kLoop, calls=%fused_computation.162 | loop fusion | flops 6 | bytes 26 | tf_op jit(solution)/shard_map/eq | solution.py:142
  14.4 1.5 %collective-permute-done.28 = bf16[1,1,512,512]{3,2,1,0:T(8,128)(2,1)S(1)} collective-permute-done((bf16[1,1,512,512]{3,2,1,0:T(8,128)(2,1)}, bf16[1,1,512,512]{3,2,1,0:T(8,128)(2,1)S(1)}, u32[]{:S(2)}, u32[]{:S(2)}) %collective-permute-start.28) | collective-permute-done | bytes 524320 | tf_op jit(solution)/shard_map/ppermute | solution.py:125
  16.3 2.3 %collective-permute-done.29 = bf16[2,1,512,512]{3,2,0,1:T(8,128)(2,1)S(1)} collective-permute-done((bf16[2,1,512,512]{3,2,0,1:T(8,128)(2,1)S(1)}, bf16[2,1,512,512]{3,2,0,1:T(8,128)(2,1)S(1)}, u32[]{:S(2)}, u32[]{:S(2)}) %collective-permute-start.29) | collective-permute-done | bytes 1048608 | tf_op jit(solution)/shard_map/ppermute | solution.py:125
  19.3 1.6 %gather_fusion = bf16[2,512,512]{2,1,0:T(8,128)(2,1)} fusion(bf16[4,512,512]{2,1,0:T(8,128)(2,1)S(1)} %bitcast.248, s32[1024]{0:T(1024)S(1)} %pad_clamp_fusion.1), kind=kCustom, calls=%fused_computation.clone | custom fusion | bytes 2097160 | tf_op jit(solution)/shard_map/jit(_take)/gather | solution.py:270
  20.9 1.5 %broadcast_select_fusion = (bf16[2,512,512]{2,1,0:T(8,128)(2,1)S(1)}, bf16[2,512,512]{2,1,0:T(8,128)(2,1)S(1)}) fusion(bf16[2,512,512]{2,1,0:T(8,128)(2,1)S(1)} %gather_fusion.1, pred[2]{0:T(512)(128)(4,1)S(1)} %get-tuple-element.146, bf16[2,512,512]{2,1,0:T(8,128)(2,1)} %gather_fusion, pred[2]{0:T(512)(128)(4,1)S(1)} %get-tuple-element.179), kind=kLoop, calls=%fused_computation.61 | loop fusion | flops 1048576 | bytes 4194308 | tf_op jit(solution)/shard_map/jit(_take)/select_n | solution.py:270
  26.5 1.0 convolution_convert_fusion.3
  27.5 1.0 convolution_convert_fusion.1
  29.6 0.9 fusion.20
  30.5 15.6 %conditional.4 = (bf16[257,512]{1,0:T(8,128)(2,1)}) conditional(s32[]{:T(128)} %bitcast.31, bf16[257,512]{1,0:T(8,128)(2,1)S(1)} %maximum_maximum_fusion, bf16[257,512]{1,0:T(8,128)(2,1)S(1)} %maximum_maximum_fusion, bf16[257,512]{1,0:T(8,128)(2,1)S(1)} %maximum_maximum_fusion, ...), branch_computations={%region_2.4_spmd, %region_3.5_spmd, %region_4.6_spmd, %region_5.7_... | conditional | bytes 1052720 | solution.py:85
  30.5 2.9 %collective-permute-start.3 = (bf16[257,512]{1,0:T(8,128)(2,1)S(1)}, bf16[257,512]{1,0:T(8,128)(2,1)}, u32[]{:S(2)}, u32[]{:S(2)}) collective-permute-start(bf16[257,512]{1,0:T(8,128)(2,1)S(1)} %param.5), channel_id=1, source_target_pairs={{0,16},{4,20},{8,24},{12,28},{16,0},{20,4},{24,8},{28,12},{1,17},{... | collective-permute-start | bytes 789512 | tf_op jit(solution)/shard_map/cond/branch_3_fun/ppermute | solution.py:80
  33.4 12.7 %collective-permute-done.3 = bf16[257,512]{1,0:T(8,128)(2,1)} collective-permute-done((bf16[257,512]{1,0:T(8,128)(2,1)S(1)}, bf16[257,512]{1,0:T(8,128)(2,1)}, u32[]{:S(2)}, u32[]{:S(2)}) %collective-permute-start.3) | collective-permute-done | bytes 263200 | tf_op jit(solution)/shard_map/cond/branch_3_fun/ppermute | solution.py:80
  46.1 1.3 %fusion.7 = f32[256,256]{1,0:T(8,128)S(1)} fusion(bf16[256,512]{1,0:T(8,128)(2,1)} %convolution_convert_fusion.3, bf16[257,512]{1,0:T(8,128)(2,1)} %get-tuple-element.212), kind=kOutput, calls=%fused_computation.41 | convolution fusion | flops 67305472 | bytes 786432 | tf_op jit(solution)/shard_map/dot_general | solution.py:54
  48.0 1.2 convolution_convert_fusion.2
  49.1 1.2 %fusion.3 = f32[256,256]{1,0:T(8,128)S(1)} fusion(bf16[256,512]{1,0:T(8,128)(2,1)S(1)} %copy-done.7, bf16[257,512]{1,0:T(8,128)(2,1)} %get-tuple-element.212), kind=kOutput, calls=%fused_computation.35 | convolution fusion | flops 67305472 | bytes 786432 | tf_op jit(solution)/shard_map/dot_general | solution.py:54
  50.9 1.2 convolution_convert_fusion
  53.4 0.8 slice_convert_fusion
  54.4 1.0 multiply_reduce_fusion
  57.4 1.0 divide_subtract_fusion.1
  58.4 0.8 add_add_fusion
  59.6 0.8 copy-done.9
  60.5 18.0 %conditional.5 = (f32[256,512]{1,0:T(8,128)S(1)}, f32[2,2,2,64,256]{4,3,0,1,2:T(8,128)S(1)}, f32[2,2,2,64,256]{4,3,0,1,2:T(8,128)S(1)}) conditional(s32[]{:T(128)} %bitcast.31, (f32[1,2,2,2,64,256]{5,4,0,1,2,3:T(8,128)S(1)}, f32[1,2,2,2,64,256]{5,4,1,2,3,0:T(8,128)S(1)}, bf16[256,512]{1,0:T(8,128)(2,1)S(1)}) %tuple.164, ...), branch_computations={%region_10.12_spmd, %region_11.13_spmd, %region_12.14_spmd, %regio... | conditional | flops 131072 | bytes 10223760
  60.5 1.6 %collective-permute-start.16 = (f32[2,2,2,64,256]{4,3,2,1,0:T(8,128)S(1)}, f32[2,2,2,64,256]{4,3,2,1,0:T(8,128)S(1)}, u32[]{:S(2)}, u32[]{:S(2)}) collective-permute-start(f32[2,2,2,64,256]{4,3,2,1,0:T(8,128)S(1)} %bitcast.280), channel_id=1, source_target_pairs={{0,4},{4,0},{8,12},{12,8},{16,20},{20,16},{24,28},{28,24},{1,5},{5... | collective-permute-start | bytes 1572872 | tf_op jit(solution)/shard_map/cond/branch_3_fun/ppermute | solution.py:229
  62.2 1.6 %collective-permute-start.17 = (f32[2,2,2,64,256]{4,3,2,1,0:T(8,128)S(1)}, f32[2,2,2,64,256]{4,3,2,1,0:T(8,128)S(1)}, u32[]{:S(2)}, u32[]{:S(2)}) collective-permute-start(f32[2,2,2,64,256]{4,3,2,1,0:T(8,128)S(1)} %bitcast.273), channel_id=1, source_target_pairs={{0,2},{1,3},{2,0},{3,1},{4,6},{5,7},{6,4},{7,5},{8,10},{9,11},{10,... | collective-permute-start | bytes 1572872 | tf_op jit(solution)/shard_map/cond/branch_3_fun/ppermute | solution.py:229
  63.8 14.6 %collective-permute-done.18 = bf16[256,512]{1,0:T(8,128)(2,1)S(1)} collective-permute-done((bf16[256,512]{1,0:T(8,128)(2,1)S(1)}, bf16[256,512]{1,0:T(8,128)(2,1)S(1)}, u32[]{:S(2)}, u32[]{:S(2)}) %collective-permute-start.18) | collective-permute-done | bytes 262176 | tf_op jit(solution)/shard_map/cond/branch_3_fun/ppermute | solution.py:230
  79.6 1.9 %divide_subtract_fusion = f32[256,512]{1,0:T(8,128)} fusion(f32[256,512]{1,0:T(8,128)S(1)} %copy-done.4, f32[256,512]{1,0:T(8,128)S(1)} %get-tuple-element.114, f32[256]{0:T(256)S(1)} %get-tuple-element.138, bf16[257,512]{1,0:T(8,128)(2,1)} %get-tuple-element.212), kind=kLoop, calls=%fused_computation.76 | loop fusion | flops 655360 | bytes 1836032 | tf_op jit(solution)/shard_map/sub | solution.py:28
  81.5 4.6 %collective-permute-done.37 = f32[2,2,64,256]{3,2,0,1:T(8,128)S(1)} collective-permute-done((f32[2,2,64,256]{3,2,0,1:T(8,128)S(1)}, f32[2,2,64,256]{3,2,0,1:T(8,128)S(1)}, u32[]{:S(2)}, u32[]{:S(2)}) %collective-permute-start.37) | collective-permute-done | bytes 262176 | tf_op jit(solution)/shard_map/ppermute | solution.py:167
  86.6 2.4 %collective-permute-start.32 = (f32[2,64,256]{2,1,0:T(8,128)S(1)}, f32[2,64,256]{2,1,0:T(8,128)S(1)}, u32[]{:S(2)}, u32[]{:S(2)}) collective-permute-start(f32[2,64,256]{2,1,0:T(8,128)S(1)} %dynamic-slice_bitcast_fusion.5), channel_id=1, source_target_pairs={{0,16},{4,20},{8,24},{12,28},{16,0},{20,4},{24,8},{28,12},{1,17},{... | collective-permute-start | bytes 393224 | tf_op jit(solution)/shard_map/ppermute | solution.py:167
  89.0 2.9 %collective-permute-done.38 = f32[2,64,256]{2,1,0:T(8,128)S(1)} collective-permute-done((f32[2,64,256]{2,1,0:T(8,128)S(1)}, f32[2,64,256]{2,1,0:T(8,128)S(1)}, u32[]{:S(2)}, u32[]{:S(2)}) %collective-permute-start.38) | collective-permute-done | bytes 131104 | tf_op jit(solution)/shard_map/ppermute | solution.py:167
  91.9 1.2 collective-permute-start.39
  93.1 2.8 %collective-permute-done.32 = f32[2,64,256]{2,1,0:T(8,128)S(1)} collective-permute-done((f32[2,64,256]{2,1,0:T(8,128)S(1)}, f32[2,64,256]{2,1,0:T(8,128)S(1)}, u32[]{:S(2)}, u32[]{:S(2)}) %collective-permute-start.32) | collective-permute-done | bytes 131104 | tf_op jit(solution)/shard_map/ppermute | solution.py:167
  96.0 1.6 %collective-permute-done.39 = f32[64,256]{1,0:T(8,128)S(1)} collective-permute-done((f32[64,256]{1,0:T(8,128)S(1)}, f32[64,256]{1,0:T(8,128)S(1)}, u32[]{:S(2)}, u32[]{:S(2)}) %collective-permute-start.39) | collective-permute-done | bytes 65568 | tf_op jit(solution)/shard_map/ppermute | solution.py:167
  97.7 0.8 collective-permute-start.40
  98.5 1.8 %collective-permute-done.33 = f32[64,256]{1,0:T(8,128)S(1)} collective-permute-done((f32[64,256]{1,0:T(8,128)S(1)}, f32[64,256]{1,0:T(8,128)S(1)}, u32[]{:S(2)}, u32[]{:S(2)}) %collective-permute-start.33) | collective-permute-done | bytes 65568 | tf_op jit(solution)/shard_map/ppermute | solution.py:167
  100.4 1.6 %collective-permute-done.40 = f32[64,256]{1,0:T(8,128)S(1)} collective-permute-done((f32[64,256]{1,0:T(8,128)S(1)}, f32[64,256]{1,0:T(8,128)S(1)}, u32[]{:S(2)}, u32[]{:S(2)}) %collective-permute-start.40) | collective-permute-done | bytes 65568 | tf_op jit(solution)/shard_map/ppermute | solution.py:177
  102.0 1.3 %collective-permute-start.41 = (f32[2,64,256]{2,1,0:T(8,128)S(1)}, f32[2,64,256]{2,1,0:T(8,128)S(1)}, u32[]{:S(2)}, u32[]{:S(2)}) collective-permute-start(f32[2,64,256]{2,1,0:T(8,128)S(1)} %maximum_select_fusion.6), channel_id=1, source_target_pairs={{0,16},{4,20},{8,24},{12,28},{16,0},{20,4},{24,8},{28,12},{1,17},{... | collective-permute-start | bytes 393224 | tf_op jit(solution)/shard_map/ppermute | solution.py:177
  103.4 3.2 %collective-permute-done.34 = f32[64,256]{1,0:T(8,128)S(1)} collective-permute-done((f32[64,256]{1,0:T(8,128)S(1)}, f32[64,256]{1,0:T(8,128)S(1)}, u32[]{:S(2)}, u32[]{:S(2)}) %collective-permute-start.34) | collective-permute-done | bytes 65568 | tf_op jit(solution)/shard_map/ppermute | solution.py:177
  106.8 2.7 %collective-permute-done.41 = f32[2,64,256]{2,1,0:T(8,128)S(1)} collective-permute-done((f32[2,64,256]{2,1,0:T(8,128)S(1)}, f32[2,64,256]{2,1,0:T(8,128)S(1)}, u32[]{:S(2)}, u32[]{:S(2)}) %collective-permute-start.41) | collective-permute-done | bytes 131104 | tf_op jit(solution)/shard_map/ppermute | solution.py:177
  109.8 3.3 %collective-permute-done.35 = f32[2,64,256]{2,1,0:T(8,128)S(1)} collective-permute-done((f32[2,64,256]{2,1,0:T(8,128)S(1)}, f32[2,64,256]{2,1,0:T(8,128)S(1)}, u32[]{:S(2)}, u32[]{:S(2)}) %collective-permute-start.35) | collective-permute-done | bytes 131104 | tf_op jit(solution)/shard_map/ppermute | solution.py:177
  113.5 3.0 %collective-permute-done.42 = f32[2,2,64,256]{3,2,1,0:T(8,128)S(1)} collective-permute-done((f32[2,2,64,256]{3,2,1,0:T(8,128)S(1)}, f32[2,2,64,256]{3,2,1,0:T(8,128)S(1)}, u32[]{:S(2)}, u32[]{:S(2)}) %collective-permute-start.42) | collective-permute-done | bytes 262176 | tf_op jit(solution)/shard_map/ppermute | solution.py:177
  116.5 3.0 %collective-permute-done.36 = f32[2,2,64,256]{3,2,0,1:T(8,128)S(1)} collective-permute-done((f32[2,2,64,256]{3,2,0,1:T(8,128)S(1)}, f32[2,2,64,256]{3,2,0,1:T(8,128)S(1)}, u32[]{:S(2)}, u32[]{:S(2)}) %collective-permute-start.36) | collective-permute-done | bytes 262176 | tf_op jit(solution)/shard_map/ppermute | solution.py:177
  119.6 1.1 maximum_bitcast_fusion
  (125 shorter events, 13.9 us)
Async XLA Ops:
  0.6 13.7 %copy-start.6 = (bf16[1,512,512]{2,1,0:T(8,128)(2,1)S(1)}, bf16[1,512,512]{2,1,0:T(8,128)(2,1)}, u32[]{:S(2)}) copy-start(bf16[1,512,512]{2,1,0:T(8,128)(2,1)} %param.31) | copy-start | bytes 1572868
  0.6 15.2 %collective-permute-start.28 = (bf16[1,1,512,512]{3,2,1,0:T(8,128)(2,1)}, bf16[1,1,512,512]{3,2,1,0:T(8,128)(2,1)S(1)}, u32[]{:S(2)}, u32[]{:S(2)}) collective-permute-start(bf16[1,1,512,512]{3,2,1,0:T(8,128)(2,1)} %bitcast.286), channel_id=1, source_target_pairs={{0,2},{1,3},{2,0},{3,1},{4,6},{5,7},{6,4},{7,5},{8,10},{9,11},{10,... | collective-permute-start | bytes 1572872 | tf_op jit(solution)/shard_map/ppermute | solution.py:125
  10.4 5.5 %copy-start.11 = (s32[1,1,2,512]{3,2,1,0:T(2,128)S(1)}, s32[1,1,2,512]{3,2,1,0:T(2,128)}, u32[]{:S(2)}) copy-start(s32[1,1,2,512]{3,2,1,0:T(2,128)} %param.34) | copy-start | bytes 12292
  10.4 5.6 %copy-start.12 = (s32[1,1,2,512]{3,2,1,0:T(2,128)S(1)}, s32[1,1,2,512]{3,2,1,0:T(2,128)}, u32[]{:S(2)}) copy-start(s32[1,1,2,512]{3,2,1,0:T(2,128)} %param.33) | copy-start | bytes 12292
  10.4 5.6 %copy-start.13 = (s32[1,1,2,512]{3,2,1,0:T(2,128)S(1)}, s32[1,1,2,512]{3,2,1,0:T(2,128)}, u32[]{:S(2)}) copy-start(s32[1,1,2,512]{3,2,1,0:T(2,128)} %param.36) | copy-start | bytes 12292
  10.4 5.6 %copy-start.14 = (s32[1,1,2,512]{3,2,1,0:T(2,128)S(1)}, s32[1,1,2,512]{3,2,1,0:T(2,128)}, u32[]{:S(2)}) copy-start(s32[1,1,2,512]{3,2,1,0:T(2,128)} %param.35) | copy-start | bytes 12292
  15.9 2.7 %collective-permute-start.29 = (bf16[2,1,512,512]{3,2,0,1:T(8,128)(2,1)S(1)}, bf16[2,1,512,512]{3,2,0,1:T(8,128)(2,1)S(1)}, u32[]{:S(2)}, u32[]{:S(2)}) collective-permute-start(bf16[2,1,512,512]{3,2,0,1:T(8,128)(2,1)S(1)} %bitcast.249), channel_id=1, source_target_pairs={{0,1},{1,0},{2,3},{3,2},{4,5},{5,4},{6,7},{7,6},{8,9},{9,8},{10,11... | collective-permute-start | bytes 3145736 | tf_op jit(solution)/shard_map/ppermute | solution.py:125
  20.9 1.5 %copy-start.3 = (bf16[256,512]{1,0:T(8,128)(2,1)S(1)}, bf16[256,512]{1,0:T(8,128)(2,1)}, u32[]{:S(2)}) copy-start(bf16[256,512]{1,0:T(8,128)(2,1)} %convert_element_type.123) | copy-start | bytes 786436
  22.4 5.0 %copy-start.1 = (bf16[2,512,512]{2,1,0:T(8,128)(2,1)}, bf16[2,512,512]{2,1,0:T(8,128)(2,1)S(1)}, u32[]{:S(2)}) copy-start(bf16[2,512,512]{2,1,0:T(8,128)(2,1)S(1)} %get-tuple-element.189) | copy-start | bytes 3145732
  25.1 1.2 copy-start.10
  25.1 1.2 copy-start
  28.5 1.1 copy-start.15
  28.5 1.1 copy-start.5
  30.5 15.6 %collective-permute-start.3 = (bf16[257,512]{1,0:T(8,128)(2,1)S(1)}, bf16[257,512]{1,0:T(8,128)(2,1)}, u32[]{:S(2)}, u32[]{:S(2)}) collective-permute-start(bf16[257,512]{1,0:T(8,128)(2,1)S(1)} %param.5), channel_id=1, source_target_pairs={{0,16},{4,20},{8,24},{12,28},{16,0},{20,4},{24,8},{28,12},{1,17},{... | collective-permute-start | bytes 789512 | tf_op jit(solution)/shard_map/cond/branch_3_fun/ppermute | solution.py:80
  46.1 3.0 %copy-start.7 = (bf16[256,512]{1,0:T(8,128)(2,1)S(1)}, bf16[256,512]{1,0:T(8,128)(2,1)}, u32[]{:S(2)}) copy-start(bf16[256,512]{1,0:T(8,128)(2,1)} %convolution_convert_fusion.1) | copy-start | bytes 786436
  52.7 1.5 %copy-start.8 = (bf16[256,512]{1,0:T(8,128)(2,1)S(1)}, bf16[256,512]{1,0:T(8,128)(2,1)}, u32[]{:S(2)}) copy-start(bf16[256,512]{1,0:T(8,128)(2,1)} %convolution_convert_fusion.3) | copy-start | bytes 786436
  53.3 2.7 %copy-start.2 = (bf16[2,512,512]{2,1,0:T(8,128)(2,1)S(1)}, bf16[2,512,512]{2,1,0:T(8,128)(2,1)}, u32[]{:S(2)}) copy-start(bf16[2,512,512]{2,1,0:T(8,128)(2,1)} %copy-done.1) | copy-start | bytes 3145732
  53.3 5.1 %collective-permute-start.30 = (f32[2,8,64,512]{3,2,1,0:T(8,128)S(1)}, f32[2,8,64,512]{3,2,1,0:T(8,128)S(1)}, u32[]{:S(2)}, u32[]{:S(2)}) collective-permute-start(f32[2,8,64,512]{3,2,1,0:T(8,128)S(1)} %select_add_fusion), channel_id=1, source_target_pairs={{0,1},{1,0},{2,3},{3,2},{4,5},{5,4},{6,7},{7,6},{8,9},{9,8},{10,11... | collective-permute-start | bytes 6291464 | tf_op jit(solution)/shard_map/ppermute | solution.py:209
  59.5 1.0 copy-start.9
  60.5 17.9 %collective-permute-start.16 = (f32[2,2,2,64,256]{4,3,2,1,0:T(8,128)S(1)}, f32[2,2,2,64,256]{4,3,2,1,0:T(8,128)S(1)}, u32[]{:S(2)}, u32[]{:S(2)}) collective-permute-start(f32[2,2,2,64,256]{4,3,2,1,0:T(8,128)S(1)} %bitcast.280), channel_id=1, source_target_pairs={{0,4},{4,0},{8,12},{12,8},{16,20},{20,16},{24,28},{28,24},{1,5},{5... | collective-permute-start | bytes 1572872 | tf_op jit(solution)/shard_map/cond/branch_3_fun/ppermute | solution.py:229
  62.2 16.3 %collective-permute-start.17 = (f32[2,2,2,64,256]{4,3,2,1,0:T(8,128)S(1)}, f32[2,2,2,64,256]{4,3,2,1,0:T(8,128)S(1)}, u32[]{:S(2)}, u32[]{:S(2)}) collective-permute-start(f32[2,2,2,64,256]{4,3,2,1,0:T(8,128)S(1)} %bitcast.273), channel_id=1, source_target_pairs={{0,2},{1,3},{2,0},{3,1},{4,6},{5,7},{6,4},{7,5},{8,10},{9,11},{10,... | collective-permute-start | bytes 1572872 | tf_op jit(solution)/shard_map/cond/branch_3_fun/ppermute | solution.py:229
  63.7 14.6 %collective-permute-start.18 = (bf16[256,512]{1,0:T(8,128)(2,1)S(1)}, bf16[256,512]{1,0:T(8,128)(2,1)S(1)}, u32[]{:S(2)}, u32[]{:S(2)}) collective-permute-start(bf16[256,512]{1,0:T(8,128)(2,1)S(1)} %get-tuple-element.93), channel_id=1, source_target_pairs={{0,16},{4,20},{8,24},{12,28},{16,0},{20,4},{24,8},{28,12},{1,17},{... | collective-permute-start | bytes 786440 | tf_op jit(solution)/shard_map/cond/branch_3_fun/ppermute | solution.py:230
  78.5 1.0 copy-start.4
  78.7 7.5 %collective-permute-start.37 = (f32[2,2,64,256]{3,2,0,1:T(8,128)S(1)}, f32[2,2,64,256]{3,2,0,1:T(8,128)S(1)}, u32[]{:S(2)}, u32[]{:S(2)}) collective-permute-start(f32[2,2,64,256]{3,2,0,1:T(8,128)S(1)} %dynamic-slice_bitcast_fusion.2), channel_id=1, source_target_pairs={{0,4},{4,0},{8,12},{12,8},{16,20},{20,16},{24,28},{28,24},{1,5},{5... | collective-permute-start | bytes 786440 | tf_op jit(solution)/shard_map/ppermute | solution.py:167
  79.4 7.2 %collective-permute-start.31 = (f32[2,2,64,256]{3,2,0,1:T(8,128)S(1)}, f32[2,2,64,256]{3,2,0,1:T(8,128)S(1)}, u32[]{:S(2)}, u32[]{:S(2)}) collective-permute-start(f32[2,2,64,256]{3,2,0,1:T(8,128)S(1)} %dynamic-slice_bitcast_fusion.3), channel_id=1, source_target_pairs={{0,8},{4,12},{8,0},{12,4},{16,24},{20,28},{24,16},{28,20},{1,9},{5... | collective-permute-start | bytes 786440 | tf_op jit(solution)/shard_map/ppermute | solution.py:167
  86.2 5.7 %collective-permute-start.38 = (f32[2,64,256]{2,1,0:T(8,128)S(1)}, f32[2,64,256]{2,1,0:T(8,128)S(1)}, u32[]{:S(2)}, u32[]{:S(2)}) collective-permute-start(f32[2,64,256]{2,1,0:T(8,128)S(1)} %dynamic-slice_bitcast_fusion.4), channel_id=1, source_target_pairs={{0,8},{4,12},{8,0},{12,4},{16,24},{20,28},{24,16},{28,20},{1,9},{5... | collective-permute-start | bytes 393224 | tf_op jit(solution)/shard_map/ppermute | solution.py:167
  86.6 9.3 %collective-permute-start.32 = (f32[2,64,256]{2,1,0:T(8,128)S(1)}, f32[2,64,256]{2,1,0:T(8,128)S(1)}, u32[]{:S(2)}, u32[]{:S(2)}) collective-permute-start(f32[2,64,256]{2,1,0:T(8,128)S(1)} %dynamic-slice_bitcast_fusion.5), channel_id=1, source_target_pairs={{0,16},{4,20},{8,24},{12,28},{16,0},{20,4},{24,8},{28,12},{1,17},{... | collective-permute-start | bytes 393224 | tf_op jit(solution)/shard_map/ppermute | solution.py:167
  91.9 5.7 %collective-permute-start.39 = (f32[64,256]{1,0:T(8,128)S(1)}, f32[64,256]{1,0:T(8,128)S(1)}, u32[]{:S(2)}, u32[]{:S(2)}) collective-permute-start(f32[64,256]{1,0:T(8,128)S(1)} %dynamic-slice_bitcast_fusion.6), channel_id=1, source_target_pairs={{0,16},{4,20},{8,24},{12,28},{16,0},{20,4},{24,8},{28,12},{1,17},{... | collective-permute-start | bytes 196616 | tf_op jit(solution)/shard_map/ppermute | solution.py:167
  96.0 4.3 %collective-permute-start.33 = (f32[64,256]{1,0:T(8,128)S(1)}, f32[64,256]{1,0:T(8,128)S(1)}, u32[]{:S(2)}, u32[]{:S(2)}) collective-permute-start(f32[64,256]{1,0:T(8,128)S(1)} %dynamic-slice_bitcast_fusion.7), channel_id=1, source_target_pairs={{0,2},{1,3},{2,0},{3,1},{4,6},{5,7},{6,4},{7,5},{8,10},{9,11},{10,... | collective-permute-start | bytes 196616 | tf_op jit(solution)/shard_map/ppermute | solution.py:167
  97.7 4.3 %collective-permute-start.40 = (f32[64,256]{1,0:T(8,128)S(1)}, f32[64,256]{1,0:T(8,128)S(1)}, u32[]{:S(2)}, u32[]{:S(2)}) collective-permute-start(f32[64,256]{1,0:T(8,128)S(1)} %bitcast_add_fusion.6), channel_id=1, source_target_pairs={{0,4},{4,0},{8,12},{12,8},{16,20},{20,16},{24,28},{28,24},{1,5},{5... | collective-permute-start | bytes 196616 | tf_op jit(solution)/shard_map/ppermute | solution.py:177
  100.3 6.3 %collective-permute-start.34 = (f32[64,256]{1,0:T(8,128)S(1)}, f32[64,256]{1,0:T(8,128)S(1)}, u32[]{:S(2)}, u32[]{:S(2)}) collective-permute-start(f32[64,256]{1,0:T(8,128)S(1)} %bitcast_add_fusion.7), channel_id=1, source_target_pairs={{0,16},{4,20},{8,24},{12,28},{16,0},{20,4},{24,8},{28,12},{1,17},{... | collective-permute-start | bytes 196616 | tf_op jit(solution)/shard_map/ppermute | solution.py:177
  102.0 7.4 %collective-permute-start.41 = (f32[2,64,256]{2,1,0:T(8,128)S(1)}, f32[2,64,256]{2,1,0:T(8,128)S(1)}, u32[]{:S(2)}, u32[]{:S(2)}) collective-permute-start(f32[2,64,256]{2,1,0:T(8,128)S(1)} %maximum_select_fusion.6), channel_id=1, source_target_pairs={{0,16},{4,20},{8,24},{12,28},{16,0},{20,4},{24,8},{28,12},{1,17},{... | collective-permute-start | bytes 393224 | tf_op jit(solution)/shard_map/ppermute | solution.py:177
  106.6 6.4 %collective-permute-start.35 = (f32[2,64,256]{2,1,0:T(8,128)S(1)}, f32[2,64,256]{2,1,0:T(8,128)S(1)}, u32[]{:S(2)}, u32[]{:S(2)}) collective-permute-start(f32[2,64,256]{2,1,0:T(8,128)S(1)} %maximum_select_fusion.4), channel_id=1, source_target_pairs={{0,8},{4,12},{8,0},{12,4},{16,24},{20,28},{24,16},{28,20},{1,9},{5... | collective-permute-start | bytes 393224 | tf_op jit(solution)/shard_map/ppermute | solution.py:177
  109.5 7.0 %collective-permute-start.42 = (f32[2,2,64,256]{3,2,1,0:T(8,128)S(1)}, f32[2,2,64,256]{3,2,1,0:T(8,128)S(1)}, u32[]{:S(2)}, u32[]{:S(2)}) collective-permute-start(f32[2,2,64,256]{3,2,1,0:T(8,128)S(1)} %maximum_select_fusion.3), channel_id=1, source_target_pairs={{0,8},{4,12},{8,0},{12,4},{16,24},{20,28},{24,16},{28,20},{1,9},{5... | collective-permute-start | bytes 786440 | tf_op jit(solution)/shard_map/ppermute | solution.py:177
  113.1 6.4 %collective-permute-start.36 = (f32[2,2,64,256]{3,2,0,1:T(8,128)S(1)}, f32[2,2,64,256]{3,2,0,1:T(8,128)S(1)}, u32[]{:S(2)}, u32[]{:S(2)}) collective-permute-start(f32[2,2,64,256]{3,2,0,1:T(8,128)S(1)} %maximum_select_fusion.2), channel_id=1, source_target_pairs={{0,4},{4,0},{8,12},{12,8},{16,20},{20,16},{24,28},{28,24},{1,5},{5... | collective-permute-start | bytes 786440 | tf_op jit(solution)/shard_map/ppermute | solution.py:177

commit v2 on v1

--- a/solution.py
+++ b/solution.py
@@ -267,7 +267,10 @@
     gradients = []
     right_half = row_block.astype(jnp.bfloat16)
     for round_index in range(2):
-        rel_pair = jnp.take(rel_table, rel_ids[2 * round_index : 2 * round_index + 2], axis=0)
+        rel_pair = [
+            lax.dynamic_index_in_dim(rel_table, rel_ids[2 * round_index + slot], 0, keepdims=False)
+            for slot in range(2)
+        ]
         table_left, state_left, row_block, state_block, rel_grads = one_round(
             table_left,
             state_left,

time: 119 us -> 132 us (1.11)
  starting transfers between devices: 16.5 us -> 38.5 us
  waiting for transfers between devices: 61.9 us -> 48.8 us
  between operations: 2.19 us -> 10 us
  other arithmetic: 18.9 us -> 14 us
    ppermute x6, starting transfers between devices: 4.35 us -> 18.1 us  [halving_steps(): got = lax.ppermute(send, name, [(k, k ^ bit) for k in range(count)])]
    ppermute x6, waiting for transfers between devices: 14.1 us -> 4.95 us  [halving_steps(): got = lax.ppermute(send, name, [(k, k ^ bit) for k in range(count)])]
    ppermute x1, waiting for transfers between devices: 14.6 us -> 7.37 us  [run(): return (lax.ppermute(low_part, 'bucket', pairs),) + tuple(moved)]
    ppermute x2, waiting for transfers between devices: 0.01 us -> 5.91 us  [run(): moved.append(lax.ppermute(part, name, [(k, k ^ bit) for k in range(size)]))]
    ppermute x1, waiting for transfers between devices: 12.7 us -> 7.35 us  [run(): return tuple((lax.ppermute(array, 'bucket', pairs) for array in arrays))]
    ppermute x2, waiting for transfers between devices: 3.73 us -> 8.79 us  [doubling_gather(): got = lax.ppermute(current, axis, [(k, k ^ bit) for k in range(count)])]
    ppermute x1, starting transfers between devices: 0.01 us -> 3.57 us  [run(): return (lax.ppermute(low_part, 'bucket', pairs),) + tuple(moved)]
    ppermute x6, starting transfers between devices: 2.9 us -> 5.79 us  [doubling_steps(): got = lax.ppermute(current, name, [(k, k ^ bit) for k in range(count)])]
  transfers between devices with their start and end apart: 19 -> 19, of which waited for: 16 -> 13; matrix products, arithmetic and copies ran while one was open for 15% -> 12% of each run, Pallas kernels for 0% -> 0%
where the time goes in v2:
time: 132 us; the launch traced here: 133 us
  waiting for transfers between devices  48.8 us (37%)
  starting transfers between devices  38.5 us (29%)
  matrix products  15.8 us (12%)
  other arithmetic  14 us (11%)
  between operations  10 us (8%)
  local copies, waits for them, and re-layouts  5.83 us (4%)
    ppermute x6, starting transfers between devices, halving_steps(): got = lax.ppermute(send, name, [(k, k ^ bit) for k in range(count)])  18.1 us
    ppermute x6, waiting for transfers between devices, doubling_steps(): got = lax.ppermute(current, name, [(k, k ^ bit) for k in range(count)])  14.4 us
    ppermute x2, waiting for transfers between devices, doubling_gather(): got = lax.ppermute(current, axis, [(k, k ^ bit) for k in range(count)])  8.79 us
    ppermute x1, waiting for transfers between devices, run(): return (lax.ppermute(low_part, 'bucket', pairs),) + tuple(moved)  7.37 us
    ppermute x1, waiting for transfers between devices, run(): return tuple((lax.ppermute(array, 'bucket', pairs) for array in arrays))  7.35 us
    ppermute x2, waiting for transfers between devices, run(): moved.append(lax.ppermute(part, name, [(k, k ^ bit) for k in range(size)]))  5.91 us
    ppermute x6, starting transfers between devices, doubling_steps(): got = lax.ppermute(current, name, [(k, k ^ bit) for k in range(count)])  5.79 us
    ppermute x6, waiting for transfers between devices, halving_steps(): got = lax.ppermute(send, name, [(k, k ^ bit) for k in range(count)])  4.95 us
  transfers between devices with their start and end apart: 19, of which 13 were waited for; matrix products, arithmetic and copies ran while one was open for 12% of the time, Pallas kernels for 0%

profile of v2, /device:TPU:0, one launch (start us, length us, event | category | flops | bytes accessed | tf_op | source)
XLA Modules:
  0.0 132.9 jit_solution(7155789300999299767)
XLA Ops:
  0.6 3.1 %collective-permute-start.28 = (bf16[1,1,512,512]{3,2,1,0:T(8,128)(2,1)}, bf16[1,1,512,512]{3,2,1,0:T(8,128)(2,1)S(1)}, u32[]{:S(2)}, u32[]{:S(2)}) collective-permute-start(bf16[1,1,512,512]{3,2,1,0:T(8,128)(2,1)} %bitcast.290), channel_id=1, source_target_pairs={{0,2},{1,3},{2,0},{3,1},{4,6},{5,7},{6,4},{7,5},{8,10},{9,11},{10,... | collective-permute-start | bytes 1572872 | tf_op jit(solution)/shard_map/ppermute | solution.py:125
  3.7 1.5 %fusion.82 = (s32[1,1,1]{2,1,0:T(1,128)}, s32[1,1,1]{2,1,0:T(1,128)}, s32[1,1,1]{2,1,0:T(1,128)}, s32[1,1,1]{2,1,0:T(1,128)}) fusion(s32[1,1,4]{2,1,0:T(1,128)} %param.30), kind=kLoop, calls=%fused_computation.195 | loop fusion | bytes 32 | tf_op jit(solution)/shard_map/slice | solution.py:271
  6.0 1.1 bitcast_dynamic-update-slice_fusion.3
  7.1 8.8 %collective-permute-done.28 = bf16[1,1,512,512]{3,2,1,0:T(8,128)(2,1)S(1)} collective-permute-done((bf16[1,1,512,512]{3,2,1,0:T(8,128)(2,1)}, bf16[1,1,512,512]{3,2,1,0:T(8,128)(2,1)S(1)}, u32[]{:S(2)}, u32[]{:S(2)}) %collective-permute-start.28) | collective-permute-done | bytes 524320 | tf_op jit(solution)/shard_map/ppermute | solution.py:125
  16.0 2.0 %compare_bitcast_fusion.2 = (pred[2]{0:T(512)(128)(4,1)S(1)}, pred[2]{0:T(512)(128)(4,1)S(1)}, pred[2]{0:T(512)(128)(4,1)S(1)}) fusion(s32[2,1,1]{0,2,1:T(1,128)S(1)} %get-tuple-element.163, s32[]{:T(128)} %bitcast.27, s32[]{:T(128)} %bitcast.30, s32[]{:T(128)} %bitcast.36), kind=kLoop, calls=%fused_computation.168 | loop fusion | flops 6 | bytes 26 | tf_op jit(solution)/shard_map/eq | solution.py:142
  23.3 0.7 convert_element_type.125
  27.8 1.4 %bitcast_dynamic-update-slice_fusion.1 = bf16[2,2,1,1,512,512]{5,4,1,0,3,2:T(8,128)(2,1)S(1)} fusion(bf16[2,2,1,1,512,512]{5,4,1,0,3,2:T(8,128)(2,1)S(1)} %bitcast_dynamic-update-slice_fusion, s32[]{:T(128)S(6)} %select_n.346, bf16[2,1,512,512]{3,2,0,1:T(8,128)(2,1)} %collective-permute-done.29), kind=kLoop, calls=%fused_computation.58 | loop fusion | bytes 2097156 | tf_op jit(solution)/shard_map/jit(dynamic_update_index_in_dim)/dynamic_update_slice | solution.py:131
  32.9 1.3 fusion.85
  35.3 1.0 convolution_convert_fusion.3
  36.3 0.9 fusion.20
  37.2 12.2 %conditional.4 = (bf16[257,512]{1,0:T(8,128)(2,1)}) conditional(s32[]{:T(128)} %bitcast.32, bf16[257,512]{1,0:T(8,128)(2,1)S(1)} %maximum_maximum_fusion, bf16[257,512]{1,0:T(8,128)(2,1)S(1)} %maximum_maximum_fusion, bf16[257,512]{1,0:T(8,128)(2,1)S(1)} %maximum_maximum_fusion, ...), branch_computations={%region_2.3_spmd, %region_3.4_spmd, %region_4.5_spmd, %region_5.6_... | conditional | bytes 1052720 | solution.py:85
  37.2 4.8 %collective-permute-start.6 = (bf16[257,512]{1,0:T(8,128)(2,1)S(1)}, bf16[257,512]{1,0:T(8,128)(2,1)}, u32[]{:S(2)}, u32[]{:S(2)}) collective-permute-start(bf16[257,512]{1,0:T(8,128)(2,1)S(1)} %param.6), channel_id=1, source_target_pairs={{0,28},{4,24},{8,20},{12,16},{16,12},{20,8},{24,4},{28,0},{1,29},{... | collective-permute-start | bytes 789512 | tf_op jit(solution)/shard_map/cond/branch_6_fun/ppermute | solution.py:80
  42.0 7.3 %collective-permute-done.6 = bf16[257,512]{1,0:T(8,128)(2,1)} collective-permute-done((bf16[257,512]{1,0:T(8,128)(2,1)S(1)}, bf16[257,512]{1,0:T(8,128)(2,1)}, u32[]{:S(2)}, u32[]{:S(2)}) %collective-permute-start.6) | collective-permute-done | bytes 263200 | tf_op jit(solution)/shard_map/cond/branch_6_fun/ppermute | solution.py:80
  49.4 1.3 fusion.7
  51.2 1.2 convolution_convert_fusion.2
  52.7 1.2 fusion.3
  54.4 1.3 convolution_convert_fusion
  57.1 2.0 %compare_bitcast_fusion.6 = (pred[2]{0:T(512)(128)(4,1)S(1)}, pred[2]{0:T(512)(128)(4,1)S(1)}, pred[2]{0:T(512)(128)(4,1)S(1)}) fusion(s32[2,1,1]{0,2,1:T(1,128)S(1)} %get-tuple-element.140, s32[]{:T(128)} %bitcast.27, s32[]{:T(128)} %bitcast.30, s32[]{:T(128)} %bitcast.36), kind=kLoop, calls=%fused_computation.172 | loop fusion | flops 6 | bytes 26 | tf_op jit(solution)/shard_map/eq | solution.py:142
  60.8 1.0 multiply_reduce_fusion
  62.4 1.0 divide_subtract_fusion.1
  63.5 0.8 add_add_fusion
  64.7 0.8 copy-done.12
  65.5 20.1 %conditional.5 = (f32[256,512]{1,0:T(8,128)S(1)}, f32[2,2,2,64,256]{4,3,0,1,2:T(8,128)S(1)}, f32[2,2,2,64,256]{4,3,0,1,2:T(8,128)S(1)}) conditional(s32[]{:T(128)} %bitcast.32, (f32[1,2,2,2,64,256]{5,4,0,1,2,3:T(8,128)S(1)}, f32[1,2,2,2,64,256]{5,4,1,2,3,0:T(8,128)S(1)}, bf16[256,512]{1,0:T(8,128)(2,1)S(1)}) %tuple.160, ...), branch_computations={%region_10.11_spmd, %region_11.12_spmd, %region_12.13_spmd, %regio... | conditional | flops 131072 | bytes 10223760
  65.5 1.5 %collective-permute-start.25 = (f32[2,2,2,64,256]{4,3,2,1,0:T(8,128)S(1)}, f32[2,2,2,64,256]{4,3,2,1,0:T(8,128)S(1)}, u32[]{:S(2)}, u32[]{:S(2)}) collective-permute-start(f32[2,2,2,64,256]{4,3,2,1,0:T(8,128)S(1)} %bitcast.287), channel_id=1, source_target_pairs={{0,4},{4,0},{8,12},{12,8},{16,20},{20,16},{24,28},{28,24},{1,5},{5... | collective-permute-start | bytes 1572872 | tf_op jit(solution)/shard_map/cond/branch_6_fun/ppermute | solution.py:229
  67.0 1.6 %collective-permute-start.26 = (f32[2,2,2,64,256]{4,3,2,1,0:T(8,128)S(1)}, f32[2,2,2,64,256]{4,3,2,1,0:T(8,128)S(1)}, u32[]{:S(2)}, u32[]{:S(2)}) collective-permute-start(f32[2,2,2,64,256]{4,3,2,1,0:T(8,128)S(1)} %bitcast.280), channel_id=1, source_target_pairs={{0,2},{1,3},{2,0},{3,1},{4,6},{5,7},{6,4},{7,5},{8,10},{9,11},{10,... | collective-permute-start | bytes 1572872 | tf_op jit(solution)/shard_map/cond/branch_6_fun/ppermute | solution.py:229
  68.6 3.6 %collective-permute-start.27 = (bf16[256,512]{1,0:T(8,128)(2,1)S(1)}, bf16[256,512]{1,0:T(8,128)(2,1)S(1)}, u32[]{:S(2)}, u32[]{:S(2)}) collective-permute-start(bf16[256,512]{1,0:T(8,128)(2,1)S(1)} %get-tuple-element.101), channel_id=1, source_target_pairs={{0,28},{4,24},{8,20},{12,16},{16,12},{20,8},{24,4},{28,0},{1,29},{... | collective-permute-start | bytes 786440 | tf_op jit(solution)/shard_map/cond/branch_6_fun/ppermute | solution.py:230
  72.2 7.4 %collective-permute-done.27 = bf16[256,512]{1,0:T(8,128)(2,1)S(1)} collective-permute-done((bf16[256,512]{1,0:T(8,128)(2,1)S(1)}, bf16[256,512]{1,0:T(8,128)(2,1)S(1)}, u32[]{:S(2)}, u32[]{:S(2)}) %collective-permute-start.27) | collective-permute-done | bytes 262176 | tf_op jit(solution)/shard_map/cond/branch_6_fun/ppermute | solution.py:230
  79.6 5.9 %collective-permute-done.25 = f32[2,2,2,64,256]{4,3,2,1,0:T(8,128)S(1)} collective-permute-done((f32[2,2,2,64,256]{4,3,2,1,0:T(8,128)S(1)}, f32[2,2,2,64,256]{4,3,2,1,0:T(8,128)S(1)}, u32[]{:S(2)}, u32[]{:S(2)}) %collective-permute-start.25) | collective-permute-done | bytes 524320 | tf_op jit(solution)/shard_map/cond/branch_6_fun/ppermute | solution.py:229
  85.8 1.5 %collective-permute-start.37 = (f32[2,2,64,256]{3,2,0,1:T(8,128)S(1)}, f32[2,2,64,256]{3,2,0,1:T(8,128)S(1)}, u32[]{:S(2)}, u32[]{:S(2)}) collective-permute-start(f32[2,2,64,256]{3,2,0,1:T(8,128)S(1)} %dynamic-slice_bitcast_fusion.2), channel_id=1, source_target_pairs={{0,4},{4,0},{8,12},{12,8},{16,20},{20,16},{24,28},{28,24},{1,5},{5... | collective-permute-start | bytes 786440 | tf_op jit(solution)/shard_map/ppermute | solution.py:167
  87.4 5.5 %collective-permute-start.31 = (f32[2,2,64,256]{3,2,0,1:T(8,128)S(1)}, f32[2,2,64,256]{3,2,0,1:T(8,128)S(1)}, u32[]{:S(2)}, u32[]{:S(2)}) collective-permute-start(f32[2,2,64,256]{3,2,0,1:T(8,128)S(1)} %dynamic-slice_bitcast_fusion.3), channel_id=1, source_target_pairs={{0,8},{4,12},{8,0},{12,4},{16,24},{20,28},{24,16},{28,20},{1,9},{5... | collective-permute-start | bytes 786440 | tf_op jit(solution)/shard_map/ppermute | solution.py:167
  92.9 2.1 %divide_subtract_fusion = f32[256,512]{1,0:T(8,128)} fusion(f32[256,512]{1,0:T(8,128)S(1)} %copy-done.7, f32[256,512]{1,0:T(8,128)} %copy-done.8, f32[256]{0:T(256)S(1)} %get-tuple-element.137, bf16[257,512]{1,0:T(8,128)(2,1)} %get-tuple-element.205), kind=kLoop, calls=%fused_computation.78 | loop fusion | flops 655360 | bytes 1836032 | tf_op jit(solution)/shard_map/sub | solution.py:28
  95.0 4.2 %collective-permute-start.38 = (f32[2,64,256]{2,1,0:T(8,128)S(1)}, f32[2,64,256]{2,1,0:T(8,128)S(1)}, u32[]{:S(2)}, u32[]{:S(2)}) collective-permute-start(f32[2,64,256]{2,1,0:T(8,128)S(1)} %dynamic-slice_bitcast_fusion.4), channel_id=1, source_target_pairs={{0,8},{4,12},{8,0},{12,4},{16,24},{20,28},{24,16},{28,20},{1,9},{5... | collective-permute-start | bytes 393224 | tf_op jit(solution)/shard_map/ppermute | solution.py:167
  99.3 2.3 %collective-permute-start.32 = (f32[2,64,256]{2,1,0:T(8,128)S(1)}, f32[2,64,256]{2,1,0:T(8,128)S(1)}, u32[]{:S(2)}, u32[]{:S(2)}) collective-permute-start(f32[2,64,256]{2,1,0:T(8,128)S(1)} %dynamic-slice_bitcast_fusion.5), channel_id=1, source_target_pairs={{0,16},{4,20},{8,24},{12,28},{16,0},{20,4},{24,8},{28,12},{1,17},{... | collective-permute-start | bytes 393224 | tf_op jit(solution)/shard_map/ppermute | solution.py:167
  101.6 1.7 %collective-permute-done.38 = f32[2,64,256]{2,1,0:T(8,128)S(1)} collective-permute-done((f32[2,64,256]{2,1,0:T(8,128)S(1)}, f32[2,64,256]{2,1,0:T(8,128)S(1)}, u32[]{:S(2)}, u32[]{:S(2)}) %collective-permute-start.38) | collective-permute-done | bytes 131104 | tf_op jit(solution)/shard_map/ppermute | solution.py:167
  103.4 3.0 %collective-permute-start.39 = (f32[64,256]{1,0:T(8,128)S(1)}, f32[64,256]{1,0:T(8,128)S(1)}, u32[]{:S(2)}, u32[]{:S(2)}) collective-permute-start(f32[64,256]{1,0:T(8,128)S(1)} %dynamic-slice_bitcast_fusion.6), channel_id=1, source_target_pairs={{0,16},{4,20},{8,24},{12,28},{16,0},{20,4},{24,8},{28,12},{1,17},{... | collective-permute-start | bytes 196616 | tf_op jit(solution)/shard_map/ppermute | solution.py:167
  106.3 2.1 %collective-permute-done.32 = f32[2,64,256]{2,1,0:T(8,128)S(1)} collective-permute-done((f32[2,64,256]{2,1,0:T(8,128)S(1)}, f32[2,64,256]{2,1,0:T(8,128)S(1)}, u32[]{:S(2)}, u32[]{:S(2)}) %collective-permute-start.32) | collective-permute-done | bytes 131104 | tf_op jit(solution)/shard_map/ppermute | solution.py:167
  108.4 1.6 %collective-permute-start.33 = (f32[64,256]{1,0:T(8,128)S(1)}, f32[64,256]{1,0:T(8,128)S(1)}, u32[]{:S(2)}, u32[]{:S(2)}) collective-permute-start(f32[64,256]{1,0:T(8,128)S(1)} %dynamic-slice_bitcast_fusion.7), channel_id=1, source_target_pairs={{0,2},{1,3},{2,0},{3,1},{4,6},{5,7},{6,4},{7,5},{8,10},{9,11},{10,... | collective-permute-start | bytes 196616 | tf_op jit(solution)/shard_map/ppermute | solution.py:167
  110.0 1.6 %collective-permute-start.40 = (f32[64,256]{1,0:T(8,128)S(1)}, f32[64,256]{1,0:T(8,128)S(1)}, u32[]{:S(2)}, u32[]{:S(2)}) collective-permute-start(f32[64,256]{1,0:T(8,128)S(1)} %bitcast_add_fusion.6), channel_id=1, source_target_pairs={{0,4},{4,0},{8,12},{12,8},{16,20},{20,16},{24,28},{28,24},{1,5},{5... | collective-permute-start | bytes 196616 | tf_op jit(solution)/shard_map/ppermute | solution.py:177
  111.6 1.2 collective-permute-done.33
  113.1 1.2 collective-permute-done.40
  114.4 1.5 %collective-permute-start.41 = (f32[2,64,256]{2,1,0:T(8,128)S(1)}, f32[2,64,256]{2,1,0:T(8,128)S(1)}, u32[]{:S(2)}, u32[]{:S(2)}) collective-permute-start(f32[2,64,256]{2,1,0:T(8,128)S(1)} %maximum_select_fusion.6), channel_id=1, source_target_pairs={{0,16},{4,20},{8,24},{12,28},{16,0},{20,4},{24,8},{28,12},{1,17},{... | collective-permute-start | bytes 393224 | tf_op jit(solution)/shard_map/ppermute | solution.py:177
  115.9 2.9 %collective-permute-done.34 = f32[64,256]{1,0:T(8,128)S(1)} collective-permute-done((f32[64,256]{1,0:T(8,128)S(1)}, f32[64,256]{1,0:T(8,128)S(1)}, u32[]{:S(2)}, u32[]{:S(2)}) %collective-permute-start.34) | collective-permute-done | bytes 65568 | tf_op jit(solution)/shard_map/ppermute | solution.py:177
  119.0 2.7 %collective-permute-done.41 = f32[2,64,256]{2,1,0:T(8,128)S(1)} collective-permute-done((f32[2,64,256]{2,1,0:T(8,128)S(1)}, f32[2,64,256]{2,1,0:T(8,128)S(1)}, u32[]{:S(2)}, u32[]{:S(2)}) %collective-permute-start.41) | collective-permute-done | bytes 131104 | tf_op jit(solution)/shard_map/ppermute | solution.py:177
  122.4 2.9 %collective-permute-done.35 = f32[2,64,256]{2,1,0:T(8,128)S(1)} collective-permute-done((f32[2,64,256]{2,1,0:T(8,128)S(1)}, f32[2,64,256]{2,1,0:T(8,128)S(1)}, u32[]{:S(2)}, u32[]{:S(2)}) %collective-permute-start.35) | collective-permute-done | bytes 131104 | tf_op jit(solution)/shard_map/ppermute | solution.py:177
  125.3 1.6 %collective-permute-start.36 = (f32[2,2,64,256]{3,2,0,1:T(8,128)S(1)}, f32[2,2,64,256]{3,2,0,1:T(8,128)S(1)}, u32[]{:S(2)}, u32[]{:S(2)}) collective-permute-start(f32[2,2,64,256]{3,2,0,1:T(8,128)S(1)} %maximum_select_fusion.2), channel_id=1, source_target_pairs={{0,4},{4,0},{8,12},{12,8},{16,20},{20,16},{24,28},{28,24},{1,5},{5... | collective-permute-start | bytes 786440 | tf_op jit(solution)/shard_map/ppermute | solution.py:177
  127.0 1.5 %collective-permute-done.42 = f32[2,2,64,256]{3,2,1,0:T(8,128)S(1)} collective-permute-done((f32[2,2,64,256]{3,2,1,0:T(8,128)S(1)}, f32[2,2,64,256]{3,2,1,0:T(8,128)S(1)}, u32[]{:S(2)}, u32[]{:S(2)}) %collective-permute-start.42) | collective-permute-done | bytes 262176 | tf_op jit(solution)/shard_map/ppermute | solution.py:177
  128.5 3.2 %collective-permute-done.36 = f32[2,2,64,256]{3,2,0,1:T(8,128)S(1)} collective-permute-done((f32[2,2,64,256]{3,2,0,1:T(8,128)S(1)}, f32[2,2,64,256]{3,2,0,1:T(8,128)S(1)}, u32[]{:S(2)}, u32[]{:S(2)}) %collective-permute-start.36) | collective-permute-done | bytes 262176 | tf_op jit(solution)/shard_map/ppermute | solution.py:177
  131.8 1.1 maximum_bitcast_fusion
  (124 shorter events, 13.2 us)
Async XLA Ops:
  0.6 22.6 %copy-start.1 = (f32[256,512]{1,0:T(8,128)S(1)}, f32[256,512]{1,0:T(8,128)}, u32[]{:S(2)}) copy-start(f32[256,512]{1,0:T(8,128)} %param.25) | copy-start | bytes 1572868
  0.6 15.2 %collective-permute-start.28 = (bf16[1,1,512,512]{3,2,1,0:T(8,128)(2,1)}, bf16[1,1,512,512]{3,2,1,0:T(8,128)(2,1)S(1)}, u32[]{:S(2)}, u32[]{:S(2)}) collective-permute-start(bf16[1,1,512,512]{3,2,1,0:T(8,128)(2,1)} %bitcast.290), channel_id=1, source_target_pairs={{0,2},{1,3},{2,0},{3,1},{4,6},{5,7},{6,4},{7,5},{8,10},{9,11},{10,... | collective-permute-start | bytes 1572872 | tf_op jit(solution)/shard_map/ppermute | solution.py:125
  3.7 19.6 %copy-start.9 = (f32[256,512]{1,0:T(8,128)S(1)}, f32[256,512]{1,0:T(8,128)}, u32[]{:S(2)}) copy-start(f32[256,512]{1,0:T(8,128)} %param.27) | copy-start | bytes 1572868
  5.9 21.5 %copy-start.14 = (s32[1,1,2,512]{3,2,1,0:T(2,128)S(1)}, s32[1,1,2,512]{3,2,1,0:T(2,128)}, u32[]{:S(2)}) copy-start(s32[1,1,2,512]{3,2,1,0:T(2,128)} %param.32) | copy-start | bytes 12292
  5.9 21.5 %copy-start.15 = (s32[1,1,2,512]{3,2,1,0:T(2,128)S(1)}, s32[1,1,2,512]{3,2,1,0:T(2,128)}, u32[]{:S(2)}) copy-start(s32[1,1,2,512]{3,2,1,0:T(2,128)} %param.31) | copy-start | bytes 12292
  5.9 21.5 %copy-start.16 = (s32[1,1,2,512]{3,2,1,0:T(2,128)S(1)}, s32[1,1,2,512]{3,2,1,0:T(2,128)}, u32[]{:S(2)}) copy-start(s32[1,1,2,512]{3,2,1,0:T(2,128)} %param.34) | copy-start | bytes 12292
  5.9 21.5 %copy-start.17 = (s32[1,1,2,512]{3,2,1,0:T(2,128)S(1)}, s32[1,1,2,512]{3,2,1,0:T(2,128)}, u32[]{:S(2)}) copy-start(s32[1,1,2,512]{3,2,1,0:T(2,128)} %param.33) | copy-start | bytes 12292
  15.9 11.9 %collective-permute-start.29 = (bf16[2,1,512,512]{3,2,0,1:T(8,128)(2,1)S(1)}, bf16[2,1,512,512]{3,2,0,1:T(8,128)(2,1)}, u32[]{:S(2)}, u32[]{:S(2)}) collective-permute-start(bf16[2,1,512,512]{3,2,0,1:T(8,128)(2,1)S(1)} %bitcast.253), channel_id=1, source_target_pairs={{0,1},{1,0},{2,3},{3,2},{4,5},{5,4},{6,7},{7,6},{8,9},{9,8},{10,11... | collective-permute-start | bytes 3145736 | tf_op jit(solution)/shard_map/ppermute | solution.py:125
  27.7 1.8 %copy-start.6 = (bf16[256,512]{1,0:T(8,128)(2,1)S(1)}, bf16[256,512]{1,0:T(8,128)(2,1)}, u32[]{:S(2)}) copy-start(bf16[256,512]{1,0:T(8,128)(2,1)} %convert_element_type.125) | copy-start | bytes 786436
  32.9 2.1 %copy-start.18 = (f32[256]{0:T(256)S(1)}, f32[256]{0:T(256)}, u32[]{:S(2)}) copy-start(f32[256]{0:T(256)} %param.28) | copy-start | bytes 3076
  32.9 2.2 %copy-start.13 = (f32[256]{0:T(256)S(1)}, f32[256]{0:T(256)}, u32[]{:S(2)}) copy-start(f32[256]{0:T(256)} %param.26) | copy-start | bytes 3076
  32.9 2.2 %copy-start.2 = (f32[256,512]{1,0:T(8,128)S(1)}, f32[256,512]{1,0:T(8,128)}, u32[]{:S(2)}) copy-start(f32[256,512]{1,0:T(8,128)} %param.25) | copy-start | bytes 1572868
  34.7 2.5 %copy-start.4 = (f32[256,512]{1,0:T(8,128)}, f32[256,512]{1,0:T(8,128)S(1)}, u32[]{:S(2)}) copy-start(f32[256,512]{1,0:T(8,128)S(1)} %get-tuple-element.175) | copy-start | bytes 1572868
  34.7 1.6 %copy-start.10 = (f32[256,512]{1,0:T(8,128)S(1)}, f32[256,512]{1,0:T(8,128)}, u32[]{:S(2)}) copy-start(f32[256,512]{1,0:T(8,128)} %param.27) | copy-start | bytes 1572868
  37.2 12.2 %collective-permute-start.6 = (bf16[257,512]{1,0:T(8,128)(2,1)S(1)}, bf16[257,512]{1,0:T(8,128)(2,1)}, u32[]{:S(2)}, u32[]{:S(2)}) collective-permute-start(bf16[257,512]{1,0:T(8,128)(2,1)S(1)} %param.6), channel_id=1, source_target_pairs={{0,28},{4,24},{8,20},{12,16},{16,12},{20,8},{24,4},{28,0},{1,29},{... | collective-permute-start | bytes 789512 | tf_op jit(solution)/shard_map/cond/branch_6_fun/ppermute | solution.py:80
  54.4 1.9 %copy-start = (f32[512,512]{0,1:T(8,128)S(1)}, f32[512,512]{0,1:T(8,128)}, u32[]{:S(2)}) copy-start(f32[512,512]{0,1:T(8,128)} %fusion.85) | copy-start | bytes 3145732
  56.4 3.7 %copy-start.11 = (bf16[256,512]{1,0:T(8,128)(2,1)S(1)}, bf16[256,512]{1,0:T(8,128)(2,1)}, u32[]{:S(2)}) copy-start(bf16[256,512]{1,0:T(8,128)(2,1)} %convolution_convert_fusion.3) | copy-start | bytes 786436
  57.0 6.5 %collective-permute-start.30 = (f32[2,8,64,512]{3,2,1,0:T(8,128)S(1)}, f32[2,8,64,512]{3,2,1,0:T(8,128)S(1)}, u32[]{:S(2)}, u32[]{:S(2)}) collective-permute-start(f32[2,8,64,512]{3,2,1,0:T(8,128)S(1)} %select_add_fusion), channel_id=1, source_target_pairs={{0,1},{1,0},{2,3},{3,2},{4,5},{5,4},{6,7},{7,6},{8,9},{9,8},{10,11... | collective-permute-start | bytes 6291464 | tf_op jit(solution)/shard_map/ppermute | solution.py:209
  60.1 2.3 %copy-start.3 = (f32[256,512]{1,0:T(8,128)S(1)}, f32[256,512]{1,0:T(8,128)}, u32[]{:S(2)}) copy-start(f32[256,512]{1,0:T(8,128)} %param.25) | copy-start | bytes 1572868
  60.1 2.3 %copy-start.5 = (f32[256,512]{1,0:T(8,128)S(1)}, f32[256,512]{1,0:T(8,128)}, u32[]{:S(2)}) copy-start(f32[256,512]{1,0:T(8,128)} %copy-done.4) | copy-start | bytes 1572868
  64.5 1.0 copy-start.12
  65.5 20.0 %collective-permute-start.25 = (f32[2,2,2,64,256]{4,3,2,1,0:T(8,128)S(1)}, f32[2,2,2,64,256]{4,3,2,1,0:T(8,128)S(1)}, u32[]{:S(2)}, u32[]{:S(2)}) collective-permute-start(f32[2,2,2,64,256]{4,3,2,1,0:T(8,128)S(1)} %bitcast.287), channel_id=1, source_target_pairs={{0,4},{4,0},{8,12},{12,8},{16,20},{20,16},{24,28},{28,24},{1,5},{5... | collective-permute-start | bytes 1572872 | tf_op jit(solution)/shard_map/cond/branch_6_fun/ppermute | solution.py:229
  67.0 18.5 %collective-permute-start.26 = (f32[2,2,2,64,256]{4,3,2,1,0:T(8,128)S(1)}, f32[2,2,2,64,256]{4,3,2,1,0:T(8,128)S(1)}, u32[]{:S(2)}, u32[]{:S(2)}) collective-permute-start(f32[2,2,2,64,256]{4,3,2,1,0:T(8,128)S(1)} %bitcast.280), channel_id=1, source_target_pairs={{0,2},{1,3},{2,0},{3,1},{4,6},{5,7},{6,4},{7,5},{8,10},{9,11},{10,... | collective-permute-start | bytes 1572872 | tf_op jit(solution)/shard_map/cond/branch_6_fun/ppermute | solution.py:229
  68.6 10.9 %collective-permute-start.27 = (bf16[256,512]{1,0:T(8,128)(2,1)S(1)}, bf16[256,512]{1,0:T(8,128)(2,1)S(1)}, u32[]{:S(2)}, u32[]{:S(2)}) collective-permute-start(bf16[256,512]{1,0:T(8,128)(2,1)S(1)} %get-tuple-element.101), channel_id=1, source_target_pairs={{0,28},{4,24},{8,20},{12,16},{16,12},{20,8},{24,4},{28,0},{1,29},{... | collective-permute-start | bytes 786440 | tf_op jit(solution)/shard_map/cond/branch_6_fun/ppermute | solution.py:230
  85.6 1.7 %copy-start.8 = (f32[256,512]{1,0:T(8,128)}, f32[256,512]{1,0:T(8,128)S(1)}, u32[]{:S(2)}) copy-start(f32[256,512]{1,0:T(8,128)S(1)} %get-tuple-element.113) | copy-start | bytes 1572868
  85.6 7.3 %copy-start.7 = (f32[256,512]{1,0:T(8,128)S(1)}, f32[256,512]{1,0:T(8,128)}, u32[]{:S(2)}) copy-start(f32[256,512]{1,0:T(8,128)} %get-tuple-element.181) | copy-start | bytes 1572868
  85.8 9.2 %collective-permute-start.37 = (f32[2,2,64,256]{3,2,0,1:T(8,128)S(1)}, f32[2,2,64,256]{3,2,0,1:T(8,128)S(1)}, u32[]{:S(2)}, u32[]{:S(2)}) collective-permute-start(f32[2,2,64,256]{3,2,0,1:T(8,128)S(1)} %dynamic-slice_bitcast_fusion.2), channel_id=1, source_target_pairs={{0,4},{4,0},{8,12},{12,8},{16,20},{20,16},{24,28},{28,24},{1,5},{5... | collective-permute-start | bytes 786440 | tf_op jit(solution)/shard_map/ppermute | solution.py:167
  87.4 11.8 %collective-permute-start.31 = (f32[2,2,64,256]{3,2,0,1:T(8,128)S(1)}, f32[2,2,64,256]{3,2,0,1:T(8,128)S(1)}, u32[]{:S(2)}, u32[]{:S(2)}) collective-permute-start(f32[2,2,64,256]{3,2,0,1:T(8,128)S(1)} %dynamic-slice_bitcast_fusion.3), channel_id=1, source_target_pairs={{0,8},{4,12},{8,0},{12,4},{16,24},{20,28},{24,16},{28,20},{1,9},{5... | collective-permute-start | bytes 786440 | tf_op jit(solution)/shard_map/ppermute | solution.py:167
  95.0 8.3 %collective-permute-start.38 = (f32[2,64,256]{2,1,0:T(8,128)S(1)}, f32[2,64,256]{2,1,0:T(8,128)S(1)}, u32[]{:S(2)}, u32[]{:S(2)}) collective-permute-start(f32[2,64,256]{2,1,0:T(8,128)S(1)} %dynamic-slice_bitcast_fusion.4), channel_id=1, source_target_pairs={{0,8},{4,12},{8,0},{12,4},{16,24},{20,28},{24,16},{28,20},{1,9},{5... | collective-permute-start | bytes 393224 | tf_op jit(solution)/shard_map/ppermute | solution.py:167
  99.3 9.1 %collective-permute-start.32 = (f32[2,64,256]{2,1,0:T(8,128)S(1)}, f32[2,64,256]{2,1,0:T(8,128)S(1)}, u32[]{:S(2)}, u32[]{:S(2)}) collective-permute-start(f32[2,64,256]{2,1,0:T(8,128)S(1)} %dynamic-slice_bitcast_fusion.5), channel_id=1, source_target_pairs={{0,16},{4,20},{8,24},{12,28},{16,0},{20,4},{24,8},{28,12},{1,17},{... | collective-permute-start | bytes 393224 | tf_op jit(solution)/shard_map/ppermute | solution.py:167
  103.4 6.7 %collective-permute-start.39 = (f32[64,256]{1,0:T(8,128)S(1)}, f32[64,256]{1,0:T(8,128)S(1)}, u32[]{:S(2)}, u32[]{:S(2)}) collective-permute-start(f32[64,256]{1,0:T(8,128)S(1)} %dynamic-slice_bitcast_fusion.6), channel_id=1, source_target_pairs={{0,16},{4,20},{8,24},{12,28},{16,0},{20,4},{24,8},{28,12},{1,17},{... | collective-permute-start | bytes 196616 | tf_op jit(solution)/shard_map/ppermute | solution.py:167
  108.4 4.3 %collective-permute-start.33 = (f32[64,256]{1,0:T(8,128)S(1)}, f32[64,256]{1,0:T(8,128)S(1)}, u32[]{:S(2)}, u32[]{:S(2)}) collective-permute-start(f32[64,256]{1,0:T(8,128)S(1)} %dynamic-slice_bitcast_fusion.7), channel_id=1, source_target_pairs={{0,2},{1,3},{2,0},{3,1},{4,6},{5,7},{6,4},{7,5},{8,10},{9,11},{10,... | collective-permute-start | bytes 196616 | tf_op jit(solution)/shard_map/ppermute | solution.py:167
  110.0 4.3 %collective-permute-start.40 = (f32[64,256]{1,0:T(8,128)S(1)}, f32[64,256]{1,0:T(8,128)S(1)}, u32[]{:S(2)}, u32[]{:S(2)}) collective-permute-start(f32[64,256]{1,0:T(8,128)S(1)} %bitcast_add_fusion.6), channel_id=1, source_target_pairs={{0,4},{4,0},{8,12},{12,8},{16,20},{20,16},{24,28},{28,24},{1,5},{5... | collective-permute-start | bytes 196616 | tf_op jit(solution)/shard_map/ppermute | solution.py:177
  112.8 6.1 %collective-permute-start.34 = (f32[64,256]{1,0:T(8,128)S(1)}, f32[64,256]{1,0:T(8,128)S(1)}, u32[]{:S(2)}, u32[]{:S(2)}) collective-permute-start(f32[64,256]{1,0:T(8,128)S(1)} %bitcast_add_fusion.7), channel_id=1, source_target_pairs={{0,16},{4,20},{8,24},{12,28},{16,0},{20,4},{24,8},{28,12},{1,17},{... | collective-permute-start | bytes 196616 | tf_op jit(solution)/shard_map/ppermute | solution.py:177
  114.4 7.3 %collective-permute-start.41 = (f32[2,64,256]{2,1,0:T(8,128)S(1)}, f32[2,64,256]{2,1,0:T(8,128)S(1)}, u32[]{:S(2)}, u32[]{:S(2)}) collective-permute-start(f32[2,64,256]{2,1,0:T(8,128)S(1)} %maximum_select_fusion.6), channel_id=1, source_target_pairs={{0,16},{4,20},{8,24},{12,28},{16,0},{20,4},{24,8},{28,12},{1,17},{... | collective-permute-start | bytes 393224 | tf_op jit(solution)/shard_map/ppermute | solution.py:177
  118.8 6.4 %collective-permute-start.35 = (f32[2,64,256]{2,1,0:T(8,128)S(1)}, f32[2,64,256]{2,1,0:T(8,128)S(1)}, u32[]{:S(2)}, u32[]{:S(2)}) collective-permute-start(f32[2,64,256]{2,1,0:T(8,128)S(1)} %maximum_select_fusion.4), channel_id=1, source_target_pairs={{0,8},{4,12},{8,0},{12,4},{16,24},{20,28},{24,16},{28,20},{1,9},{5... | collective-permute-start | bytes 393224 | tf_op jit(solution)/shard_map/ppermute | solution.py:177
  121.7 6.8 %collective-permute-start.42 = (f32[2,2,64,256]{3,2,1,0:T(8,128)S(1)}, f32[2,2,64,256]{3,2,1,0:T(8,128)S(1)}, u32[]{:S(2)}, u32[]{:S(2)}) collective-permute-start(f32[2,2,64,256]{3,2,1,0:T(8,128)S(1)} %maximum_select_fusion.3), channel_id=1, source_target_pairs={{0,8},{4,12},{8,0},{12,4},{16,24},{20,28},{24,16},{28,20},{1,9},{5... | collective-permute-start | bytes 786440 | tf_op jit(solution)/shard_map/ppermute | solution.py:177
  125.3 6.4 %collective-permute-start.36 = (f32[2,2,64,256]{3,2,0,1:T(8,128)S(1)}, f32[2,2,64,256]{3,2,0,1:T(8,128)S(1)}, u32[]{:S(2)}, u32[]{:S(2)}) collective-permute-start(f32[2,2,64,256]{3,2,0,1:T(8,128)S(1)} %maximum_select_fusion.2), channel_id=1, source_target_pairs={{0,4},{4,0},{8,12},{12,8},{16,20},{20,16},{24,28},{28,24},{1,5},{5... | collective-permute-start | bytes 786440 | tf_op jit(solution)/shard_map/ppermute | solution.py:177

commit v3 on v1

--- a/solution.py
+++ b/solution.py
@@ -68,6 +68,13 @@
         return (left_new, left_st_new, None, (right_st, grad_right), rel_grads)
     right_new, right_st_new = adagrad(right_block, right_st, grad_right)
     return (left_new, left_st_new, right_new, right_st_new, rel_grads)
+
+
+def scored(left_half, right_half, matrix, target, block_len):
+    projected = jnp.dot(left_half, matrix, preferred_element_type=jnp.float32).astype(jnp.bfloat16)
+    scores = jnp.dot(projected, right_half.T, preferred_element_type=jnp.float32)
+    score_grad = ((jax.nn.sigmoid(scores) - target) / block_len).astype(jnp.bfloat16)
+    return projected, score_grad
 
 
 def partner_values(values, switch):
@@ -264,42 +271,87 @@
     switch = matching[0]
     table_left, state_left = (left_rows, left_state)
     row_block, state_block = (right_rows, right_state)
-    gradients = []
-    right_half = row_block.astype(jnp.bfloat16)
-    for round_index in range(2):
-        rel_pair = jnp.take(rel_table, rel_ids[2 * round_index : 2 * round_index + 2], axis=0)
-        table_left, state_left, row_block, state_block, rel_grads = one_round(
-            table_left,
-            state_left,
-            row_block,
-            state_block,
-            right_half,
-            rel_pair,
-            edge_left[0, 0, round_index],
-            edge_right[0, 0, round_index],
-            edge_slot[0, 0, round_index],
-            edge_weight[0, 0, round_index],
-        )
-        gradients.extend(rel_grads)
-        if round_index == 0:
-            rounded = lax.reduce_precision(row_block, exponent_bits=8, mantissa_bits=7)
-            high = rounded.astype(jnp.bfloat16)
-            low = (row_block - rounded).astype(jnp.bfloat16)
-            state_rounded = lax.reduce_precision(state_block, exponent_bits=8, mantissa_bits=7)
-            state_pair = jnp.concatenate([state_rounded, state_block - state_rounded])
-            block_len, row_width = high.shape
-            state_rows = -(-state_pair.shape[0] // row_width)
-            state_pair = jnp.pad(state_pair, (0, state_rows * row_width - state_pair.shape[0]))
-            packed = jnp.concatenate(
-                [high, state_pair.astype(jnp.bfloat16).reshape(state_rows, row_width)]
+    block_len, row_width = right_rows.shape
+    own_half = right_rows.astype(jnp.bfloat16)
+    left_half = left_rows.astype(jnp.bfloat16)
+    first_pair = jnp.take(rel_table, rel_ids[0:2], axis=0)
+    targets = edge_targets(
+        edge_left[0, 0, 0], edge_right[0, 0, 0], edge_slot[0, 0, 0], edge_weight[0, 0, 0], block_len
+    )
+    grad_right = jnp.zeros(right_rows.shape, jnp.float32)
+    score_grads = []
+    for slot_index in range(2):
+        projected, score_grad = scored(
+            left_half, own_half, first_pair[slot_index], targets[slot_index], block_len
+        )
+        score_grads.append(score_grad)
+        grad_right = grad_right + jnp.dot(
+            score_grad.T, projected, preferred_element_type=jnp.float32
+        )
+    right_new, right_st_new = adagrad(right_rows, right_state, grad_right)
+    rounded = lax.reduce_precision(right_new, exponent_bits=8, mantissa_bits=7)
+    high = rounded.astype(jnp.bfloat16)
+    low = (right_new - rounded).astype(jnp.bfloat16)
+    state_rounded = lax.reduce_precision(right_st_new, exponent_bits=8, mantissa_bits=7)
+    state_pair = jnp.concatenate([state_rounded, right_st_new - state_rounded])
+    state_rows = -(-state_pair.shape[0] // row_width)
+    state_pair = jnp.pad(state_pair, (0, state_rows * row_width - state_pair.shape[0]))
+    packed = jnp.concatenate([high, state_pair.astype(jnp.bfloat16).reshape(state_rows, row_width)])
+
+    def left_side(left_block, left_st, matrices, grads_of_scores):
+        grad_left = jnp.zeros(left_block.shape, jnp.float32)
+        rel_grads = []
+        for slot_index in range(2):
+            carried = jnp.dot(
+                grads_of_scores[slot_index], own_half, preferred_element_type=jnp.float32
+            ).astype(jnp.bfloat16)
+            grad_left = grad_left + jnp.dot(
+                carried, matrices[slot_index].T, preferred_element_type=jnp.float32
             )
-            (their_packed,) = partner_values((packed,), switch)
-            right_half = their_packed[:block_len]
-            their_state = their_packed[block_len:].reshape(-1).astype(jnp.float32)
-            state_block = their_state[:block_len] + their_state[block_len : 2 * block_len]
-            block_high = right_half
-            row_block = None
-
+            rel_grads.append(jnp.dot(left_half.T, carried, preferred_element_type=jnp.float32))
+        left_new, left_st_new = adagrad(left_block, left_st, grad_left)
+        return (left_new, left_st_new) + tuple(rel_grads)
+
+    count = lax.axis_size("bucket")
+
+    def swap_and_update(offset):
+        pairs = [(b, b ^ offset) for b in range(count)]
+
+        def run(values, left_block, left_st, matrices, grads_of_scores):
+            moved = lax.ppermute(values, "bucket", pairs)
+            return (moved,) + left_side(left_block, left_st, matrices, grads_of_scores)
+
+        return run
+
+    outcome = lax.switch(
+        switch - 1,
+        [swap_and_update(offset) for offset in range(1, count)],
+        packed,
+        left_rows,
+        left_state,
+        first_pair,
+        tuple(score_grads),
+    )
+    their_packed, table_left, state_left = outcome[:3]
+    gradients = list(outcome[3:])
+    right_half = their_packed[:block_len]
+    their_state = their_packed[block_len:].reshape(-1).astype(jnp.float32)
+    state_block = their_state[:block_len] + their_state[block_len : 2 * block_len]
+    block_high = right_half
+    rel_pair = jnp.take(rel_table, rel_ids[2:4], axis=0)
+    table_left, state_left, _, state_block, rel_grads = one_round(
+        table_left,
+        state_left,
+        None,
+        state_block,
+        right_half,
+        rel_pair,
+        edge_left[0, 0, 1],
+        edge_right[0, 0, 1],
+        edge_slot[0, 0, 1],
+        edge_weight[0, 0, 1],
+    )
+    gradients.extend(rel_grads)
     right_st, grad_right = state_block
     owned, their_low = reduce_gradients(gradients, rel_ids, rel_total, width, low, switch)
     row_block, state_block = adagrad(

time: 119 us -> 126 us (1.059); the launches traced: 121 us -> 124 us
  waiting for transfers between devices: 61.9 us -> 40.6 us
  starting transfers between devices: 16.5 us -> 31.6 us
  local copies, waits for them, and re-layouts: 5.73 us -> 12.5 us
  other arithmetic: 18.9 us -> 22.6 us
  matrix products: 15.4 us -> 14.1 us
    ppermute x1, waiting for transfers between devices: 12.7 us -> 4.09 us  [run(): moved = lax.ppermute(values, 'bucket', pairs)]
    ppermute x2, waiting for transfers between devices: 0.01 us -> 7.5 us  [run(): moved.append(lax.ppermute(part, name, [(k, k ^ bit) for k in range(size)]))]
    ppermute x6, starting transfers between devices: 4.35 us -> 11.7 us  [halving_steps(): got = lax.ppermute(send, name, [(k, k ^ bit) for k in range(count)])]
    ppermute x1, waiting for transfers between devices: 14.6 us -> 7.52 us  [run(): return (lax.ppermute(low_part, 'bucket', pairs),) + tuple(moved)]
    ppermute x6, waiting for transfers between devices: 14.1 us -> 7.65 us  [halving_steps(): got = lax.ppermute(send, name, [(k, k ^ bit) for k in range(count)])]
    ppermute x6, waiting for transfers between devices: 16.8 us -> 10.4 us  [doubling_steps(): got = lax.ppermute(current, name, [(k, k ^ bit) for k in range(count)])]
    ppermute x6, starting transfers between devices: 2.9 us -> 9.07 us  [doubling_steps(): got = lax.ppermute(current, name, [(k, k ^ bit) for k in range(count)])]
    another operation x4 -> x6, local copies, waits for them, and re-layouts: 0.14 us -> 4.25 us
  transfers between devices with their start and end apart: 19 -> 19, of which waited for: 16 -> 15; matrix products, arithmetic and copies ran while one was open for 15% -> 17% of each run, Pallas kernels for 0% -> 0%
where the time goes in v3:
time: 126 us; the launch traced here: 124 us
  waiting for transfers between devices  40.6 us (32%)
  starting transfers between devices  31.6 us (25%)
  other arithmetic  22.6 us (18%)
  matrix products  14.1 us (11%)
  local copies, waits for them, and re-layouts  12.5 us (10%)
  between operations  2.19 us (2%)
    ppermute x6, starting transfers between devices, halving_steps(): got = lax.ppermute(send, name, [(k, k ^ bit) for k in range(count)])  11.7 us
    ppermute x6, waiting for transfers between devices, doubling_steps(): got = lax.ppermute(current, name, [(k, k ^ bit) for k in range(count)])  10.4 us
    ppermute x6, starting transfers between devices, doubling_steps(): got = lax.ppermute(current, name, [(k, k ^ bit) for k in range(count)])  9.07 us
    ppermute x6, waiting for transfers between devices, halving_steps(): got = lax.ppermute(send, name, [(k, k ^ bit) for k in range(count)])  7.65 us
    ppermute x1, waiting for transfers between devices, run(): return (lax.ppermute(low_part, 'bucket', pairs),) + tuple(moved)  7.52 us
    ppermute x2, waiting for transfers between devices, run(): moved.append(lax.ppermute(part, name, [(k, k ^ bit) for k in range(size)]))  7.5 us
    eq x3, other arithmetic, selected_term(): hit = (rel_ids[slot_index] == wanted)[:, :, None, None]  5.65 us
    sub x3, other arithmetic, adagrad(): table - learn_rate * gradient / jnp.sqrt(state_new)[:, None]  4.8 us
  transfers between devices with their start and end apart: 19, of which 15 were waited for; matrix products, arithmetic and copies ran while one was open for 17% of the time, Pallas kernels for 0%

profile of v3, /device:TPU:0, one launch (start us, length us, event | category | flops | bytes accessed | tf_op | source)
XLA Modules:
  0.0 123.7 jit_solution(15437136459638962207)
XLA Ops:
  0.6 3.1 %collective-permute-start.28 = (bf16[1,1,512,512]{3,2,1,0:T(8,128)(2,1)}, bf16[1,1,512,512]{3,2,1,0:T(8,128)(2,1)S(1)}, u32[]{:S(2)}, u32[]{:S(2)}) collective-permute-start(bf16[1,1,512,512]{3,2,1,0:T(8,128)(2,1)} %bitcast.422), channel_id=1, source_target_pairs={{0,2},{1,3},{2,0},{3,1},{4,6},{5,7},{6,4},{7,5},{8,10},{9,11},{10,... | collective-permute-start | bytes 1572872 | tf_op jit(solution)/shard_map/ppermute | solution.py:132
  4.5 1.4 %fusion.97 = (s32[1,1,1]{2,1,0:T(1,128)}, s32[1,1,1]{2,1,0:T(1,128)}, s32[1,1,1]{2,1,0:T(1,128)}, s32[1,1,1]{2,1,0:T(1,128)}) fusion(s32[1,1,4]{2,1,0:T(1,128)} %param.32), kind=kLoop, calls=%fused_computation.274 | loop fusion | bytes 32 | tf_op jit(solution)/shard_map/slice | solution.py:149
  6.6 2.5 %compare_bitcast_fusion.2 = (pred[2]{0:T(512)(128)(4,1)S(1)}, pred[2]{0:T(512)(128)(4,1)}, pred[2]{0:T(512)(128)(4,1)}) fusion(s32[2,1,1]{0,2,1:T(1,128)S(1)} %get-tuple-element.399, s32[]{:T(128)} %bitcast.68, s32[]{:T(128)} %bitcast.71, s32[]{:T(128)} %bitcast.74), kind=kLoop, calls=%fused_computation.243 | loop fusion | flops 6 | bytes 26 | tf_op jit(solution)/shard_map/eq | solution.py:149
  10.9 1.1 convert_element_type.177
  12.0 2.5 %compare_bitcast_fusion.6 = (pred[2]{0:T(512)(128)(4,1)}, pred[2]{0:T(512)(128)(4,1)}, pred[2]{0:T(512)(128)(4,1)}) fusion(s32[2,1,1]{0,2,1:T(1,128)S(1)} %get-tuple-element.358, s32[]{:T(128)} %bitcast.68, s32[]{:T(128)} %bitcast.71, s32[]{:T(128)} %bitcast.74), kind=kLoop, calls=%fused_computation.247 | loop fusion | flops 6 | bytes 26 | tf_op jit(solution)/shard_map/eq | solution.py:149
  14.6 1.2 collective-permute-done.28
  16.3 2.3 %collective-permute-done.29 = bf16[2,1,512,512]{3,2,0,1:T(8,128)(2,1)S(1)} collective-permute-done((bf16[2,1,512,512]{3,2,0,1:T(8,128)(2,1)S(1)}, bf16[2,1,512,512]{3,2,0,1:T(8,128)(2,1)S(1)}, u32[]{:S(2)}, u32[]{:S(2)}) %collective-permute-start.29) | collective-permute-done | bytes 1048608 | tf_op jit(solution)/shard_map/ppermute | solution.py:132
  18.7 1.6 %gather_fusion.1 = bf16[2,512,512]{2,1,0:T(8,128)(2,1)} fusion(bf16[4,512,512]{2,1,0:T(8,128)(2,1)S(1)} %bitcast.383, s32[1024]{0:T(1024)S(1)} %pad_clamp_fusion), kind=kCustom, calls=%fused_computation.1.clone | custom fusion | bytes 2097160 | tf_op jit(solution)/shard_map/jit(_take)/gather | solution.py:341
  20.3 1.6 %gather_fusion = bf16[2,512,512]{2,1,0:T(8,128)(2,1)} fusion(bf16[4,512,512]{2,1,0:T(8,128)(2,1)S(1)} %bitcast.384, s32[1024]{0:T(1024)S(1)} %pad_clamp_fusion.1), kind=kCustom, calls=%fused_computation.clone | custom fusion | bytes 2097160 | tf_op jit(solution)/shard_map/jit(_take)/gather | solution.py:277
  21.9 1.8 %broadcast_select_fusion = (bf16[2,512,512]{2,1,0:T(8,128)(2,1)S(1)}, bf16[2,512,512]{2,1,0:T(8,128)(2,1)S(1)}) fusion(bf16[2,512,512]{2,1,0:T(8,128)(2,1)} %gather_fusion.1, pred[2]{0:T(512)(128)(4,1)S(1)} %get-tuple-element.363, bf16[2,512,512]{2,1,0:T(8,128)(2,1)} %gather_fusion, pred[2]{0:T(512)(128)(4,1)S(1)} %get-tuple-element.410), kind=kLoop, calls=%fused_computation.149 | loop fusion | flops 1048576 | bytes 4194308 | tf_op jit(solution)/shard_map/jit(_take)/select_n | solution.py:341
  27.7 10.8 %conditional.8 = (bf16[257,512]{1,0:T(8,128)(2,1)}, f32[256,512]{1,0:T(8,128)}, f32[256]{0:T(256)S(1)}, f32[512,512]{0,1:T(8,128)S(1)}, f32[512,512]{0,1:T(8,128)S(1)}, /*index=5*/f32[256,512]{1,0:T(8,128)S(1)}) conditional(s32[]{:T(128)} %bitcast.42, (bf16[257,512]{1,0:T(8,128)(2,1)S(1)}, ...), branch_computations={%region_1.4_spmd, %region_3.6_spmd, %region_5.8_spmd, %region_7.10... | conditional | flops 672137472 | bytes 11282520
  27.7 2.8 %collective-permute-start.23 = (bf16[257,512]{1,0:T(8,128)(2,1)S(1)}, bf16[257,512]{1,0:T(8,128)(2,1)}, u32[]{:S(2)}, u32[]{:S(2)}) collective-permute-start(bf16[257,512]{1,0:T(8,128)(2,1)S(1)} %get-tuple-element.211), channel_id=1, source_target_pairs={{0,12},{4,8},{8,4},{12,0},{16,28},{20,24},{24,20},{28,16},{1,13},{... | collective-permute-start | bytes 789512 | tf_op jit(solution)/shard_map/cond/branch_2_fun/ppermute | solution.py:321
  33.3 4.1 %collective-permute-done.23 = bf16[257,512]{1,0:T(8,128)(2,1)} collective-permute-done((bf16[257,512]{1,0:T(8,128)(2,1)S(1)}, bf16[257,512]{1,0:T(8,128)(2,1)}, u32[]{:S(2)}, u32[]{:S(2)}) %collective-permute-start.23) | collective-permute-done | bytes 263200 | tf_op jit(solution)/shard_map/cond/branch_2_fun/ppermute | solution.py:321
  39.1 1.4 %fusion.42 = f32[256,256]{1,0:T(8,128)S(1)} fusion(bf16[256,512]{1,0:T(8,128)(2,1)S(1)} %convolution_convert_fusion.17, bf16[257,512]{1,0:T(8,128)(2,1)} %get-tuple-element.288), kind=kOutput, calls=%fused_computation.129 | convolution fusion | flops 67305472 | bytes 786432 | tf_op jit(solution)/shard_map/dot_general | solution.py:54
  41.1 1.2 convolution_convert_fusion.16
  42.3 1.2 fusion.38
  44.0 1.2 convolution_convert_fusion.14
  46.6 1.6 %copy.33 = f32[512,512]{1,0:T(8,128)S(1)} copy(f32[512,512]{0,1:T(8,128)} %copy-done.5) | data formatting | bytes 2097152 | tf_op jit(solution)/shard_map/conditional.2
  48.2 2.6 %copy.32 = f32[512,512]{1,0:T(8,128)} copy(f32[512,512]{0,1:T(8,128)} %copy-done.4) | data formatting | bytes 2097152 | tf_op jit(solution)/shard_map/conditional.2
  50.7 1.9 %select_add_fusion = f32[2,8,64,512]{3,2,1,0:T(8,128)S(1)} fusion(f32[8,64,512]{2,1,0:T(8,128)S(1)} %bitcast.375, f32[8,64,512]{2,1,0:T(8,128)S(1)} %bitcast.377, f32[8,64,512]{2,1,0:T(8,128)S(1)} %bitcast.379, f32[8,64,512]{2,1,0:T(8,128)} %bitcast.381, pred[2]{0:T(512)(128)(4,1)} %get-tuple-element.405, pred[2]{0:T(512)(128)(4,1)} %get-tuple-element.404, ...), kind=kLoop, calls=%fused_computation.107 | loop fusion | flops 3670016 | bytes 6291464 | tf_op jit(solution)/shard_map/add | solution.py:150
  56.8 2.0 %divide_subtract_fusion.8 = f32[256,512]{1,0:T(8,128)} fusion(f32[256,512]{1,0:T(8,128)} %get-tuple-element.286, f32[256,512]{1,0:T(8,128)S(1)} %get-tuple-element.415, f32[256]{0:T(256)S(1)} %get-tuple-element.361), kind=kLoop, calls=%fused_computation.168 | loop fusion | flops 393216 | bytes 1573888 | tf_op jit(solution)/shard_map/sub | solution.py:28
  60.9 20.1 %conditional.7 = (f32[256,512]{1,0:T(8,128)S(1)}, f32[2,2,2,64,256]{4,3,0,1,2:T(8,128)S(1)}, f32[2,2,2,64,256]{4,3,0,1,2:T(8,128)S(1)}) conditional(s32[]{:T(128)} %bitcast.42, (f32[1,2,2,2,64,256]{5,4,0,1,2,3:T(8,128)S(1)}, f32[1,2,2,2,64,256]{5,4,1,2,3,0:T(8,128)S(1)}, bf16[256,512]{1,0:T(8,128)(2,1)S(1)}) %tuple.251, ...), branch_computations={%region_16.18_spmd, %region_17.19_spmd, %region_18.20_spmd, %regio... | conditional | flops 131072 | bytes 10223760
  60.9 1.7 %collective-permute-start.6 = (f32[2,2,2,64,256]{4,3,2,1,0:T(8,128)S(1)}, f32[2,2,2,64,256]{4,3,2,1,0:T(8,128)S(1)}, u32[]{:S(2)}, u32[]{:S(2)}) collective-permute-start(f32[2,2,2,64,256]{4,3,2,1,0:T(8,128)S(1)} %bitcast.415), channel_id=1, source_target_pairs={{0,4},{4,0},{8,12},{12,8},{16,20},{20,16},{24,28},{28,24},{1,5},{5... | collective-permute-start | bytes 1572872 | tf_op jit(solution)/shard_map/cond/branch_2_fun/ppermute | solution.py:236
  62.6 1.6 %collective-permute-start.7 = (f32[2,2,2,64,256]{4,3,2,1,0:T(8,128)S(1)}, f32[2,2,2,64,256]{4,3,2,1,0:T(8,128)S(1)}, u32[]{:S(2)}, u32[]{:S(2)}) collective-permute-start(f32[2,2,2,64,256]{4,3,2,1,0:T(8,128)S(1)} %bitcast.408), channel_id=1, source_target_pairs={{0,2},{1,3},{2,0},{3,1},{4,6},{5,7},{6,4},{7,5},{8,10},{9,11},{10,... | collective-permute-start | bytes 1572872 | tf_op jit(solution)/shard_map/cond/branch_2_fun/ppermute | solution.py:236
  64.2 1.6 %collective-permute-start.8 = (bf16[256,512]{1,0:T(8,128)(2,1)S(1)}, bf16[256,512]{1,0:T(8,128)(2,1)S(1)}, u32[]{:S(2)}, u32[]{:S(2)}) collective-permute-start(bf16[256,512]{1,0:T(8,128)(2,1)S(1)} %get-tuple-element.259), channel_id=1, source_target_pairs={{0,12},{4,8},{8,4},{12,0},{16,28},{20,24},{24,20},{28,16},{1,13},{... | collective-permute-start | bytes 786440 | tf_op jit(solution)/shard_map/cond/branch_2_fun/ppermute | solution.py:237
  65.8 7.5 %collective-permute-done.8 = bf16[256,512]{1,0:T(8,128)(2,1)S(1)} collective-permute-done((bf16[256,512]{1,0:T(8,128)(2,1)S(1)}, bf16[256,512]{1,0:T(8,128)(2,1)S(1)}, u32[]{:S(2)}, u32[]{:S(2)}) %collective-permute-start.8) | collective-permute-done | bytes 262176 | tf_op jit(solution)/shard_map/cond/branch_2_fun/ppermute | solution.py:237
  73.3 7.5 %collective-permute-done.6 = f32[2,2,2,64,256]{4,3,2,1,0:T(8,128)S(1)} collective-permute-done((f32[2,2,2,64,256]{4,3,2,1,0:T(8,128)S(1)}, f32[2,2,2,64,256]{4,3,2,1,0:T(8,128)S(1)}, u32[]{:S(2)}, u32[]{:S(2)}) %collective-permute-start.6) | collective-permute-done | bytes 524320 | tf_op jit(solution)/shard_map/cond/branch_2_fun/ppermute | solution.py:236
  81.1 1.7 %collective-permute-start.37 = (f32[2,2,64,256]{3,2,0,1:T(8,128)S(1)}, f32[2,2,64,256]{3,2,0,1:T(8,128)S(1)}, u32[]{:S(2)}, u32[]{:S(2)}) collective-permute-start(f32[2,2,64,256]{3,2,0,1:T(8,128)S(1)} %dynamic-slice_bitcast_fusion.2), channel_id=1, source_target_pairs={{0,4},{4,0},{8,12},{12,8},{16,20},{20,16},{24,28},{28,24},{1,5},{5... | collective-permute-start | bytes 786440 | tf_op jit(solution)/shard_map/ppermute | solution.py:174
  82.9 1.6 %collective-permute-start.31 = (f32[2,2,64,256]{3,2,0,1:T(8,128)S(1)}, f32[2,2,64,256]{3,2,0,1:T(8,128)S(1)}, u32[]{:S(2)}, u32[]{:S(2)}) collective-permute-start(f32[2,2,64,256]{3,2,0,1:T(8,128)S(1)} %dynamic-slice_bitcast_fusion.3), channel_id=1, source_target_pairs={{0,8},{4,12},{8,0},{12,4},{16,24},{20,28},{24,16},{28,20},{1,9},{5... | collective-permute-start | bytes 786440 | tf_op jit(solution)/shard_map/ppermute | solution.py:174
  84.5 1.9 %divide_subtract_fusion.7 = f32[256,512]{1,0:T(8,128)} fusion(f32[256,512]{1,0:T(8,128)S(1)} %copy-done.8, f32[256,512]{1,0:T(8,128)S(1)} %get-tuple-element.310, f32[256]{0:T(256)S(1)} %get-tuple-element.355, bf16[257,512]{1,0:T(8,128)(2,1)} %get-tuple-element.288), kind=kLoop, calls=%fused_computation.164 | loop fusion | flops 655360 | bytes 1836032 | tf_op jit(solution)/shard_map/sub | solution.py:28
  86.4 2.5 %collective-permute-done.37 = f32[2,2,64,256]{3,2,0,1:T(8,128)S(1)} collective-permute-done((f32[2,2,64,256]{3,2,0,1:T(8,128)S(1)}, f32[2,2,64,256]{3,2,0,1:T(8,128)S(1)}, u32[]{:S(2)}, u32[]{:S(2)}) %collective-permute-start.37) | collective-permute-done | bytes 262176 | tf_op jit(solution)/shard_map/ppermute | solution.py:174
  89.0 1.8 %collective-permute-start.38 = (f32[2,64,256]{2,1,0:T(8,128)S(1)}, f32[2,64,256]{2,1,0:T(8,128)S(1)}, u32[]{:S(2)}, u32[]{:S(2)}) collective-permute-start(f32[2,64,256]{2,1,0:T(8,128)S(1)} %dynamic-slice_bitcast_fusion.4), channel_id=1, source_target_pairs={{0,8},{4,12},{8,0},{12,4},{16,24},{20,28},{24,16},{28,20},{1,9},{5... | collective-permute-start | bytes 393224 | tf_op jit(solution)/shard_map/ppermute | solution.py:174
  90.8 2.7 %collective-permute-start.32 = (f32[2,64,256]{2,1,0:T(8,128)S(1)}, f32[2,64,256]{2,1,0:T(8,128)S(1)}, u32[]{:S(2)}, u32[]{:S(2)}) collective-permute-start(f32[2,64,256]{2,1,0:T(8,128)S(1)} %dynamic-slice_bitcast_fusion.5), channel_id=1, source_target_pairs={{0,16},{4,20},{8,24},{12,28},{16,0},{20,4},{24,8},{28,12},{1,17},{... | collective-permute-start | bytes 393224 | tf_op jit(solution)/shard_map/ppermute | solution.py:174
  93.5 1.9 %collective-permute-done.38 = f32[2,64,256]{2,1,0:T(8,128)S(1)} collective-permute-done((f32[2,64,256]{2,1,0:T(8,128)S(1)}, f32[2,64,256]{2,1,0:T(8,128)S(1)}, u32[]{:S(2)}, u32[]{:S(2)}) %collective-permute-start.38) | collective-permute-done | bytes 131104 | tf_op jit(solution)/shard_map/ppermute | solution.py:174
  95.4 2.4 %collective-permute-start.39 = (f32[64,256]{1,0:T(8,128)S(1)}, f32[64,256]{1,0:T(8,128)S(1)}, u32[]{:S(2)}, u32[]{:S(2)}) collective-permute-start(f32[64,256]{1,0:T(8,128)S(1)} %dynamic-slice_bitcast_fusion.6), channel_id=1, source_target_pairs={{0,16},{4,20},{8,24},{12,28},{16,0},{20,4},{24,8},{28,12},{1,17},{... | collective-permute-start | bytes 196616 | tf_op jit(solution)/shard_map/ppermute | solution.py:174
  97.8 2.1 %collective-permute-done.32 = f32[2,64,256]{2,1,0:T(8,128)S(1)} collective-permute-done((f32[2,64,256]{2,1,0:T(8,128)S(1)}, f32[2,64,256]{2,1,0:T(8,128)S(1)}, u32[]{:S(2)}, u32[]{:S(2)}) %collective-permute-start.32) | collective-permute-done | bytes 131104 | tf_op jit(solution)/shard_map/ppermute | solution.py:174
  99.9 1.6 %collective-permute-start.33 = (f32[64,256]{1,0:T(8,128)S(1)}, f32[64,256]{1,0:T(8,128)S(1)}, u32[]{:S(2)}, u32[]{:S(2)}) collective-permute-start(f32[64,256]{1,0:T(8,128)S(1)} %dynamic-slice_bitcast_fusion.7), channel_id=1, source_target_pairs={{0,2},{1,3},{2,0},{3,1},{4,6},{5,7},{6,4},{7,5},{8,10},{9,11},{10,... | collective-permute-start | bytes 196616 | tf_op jit(solution)/shard_map/ppermute | solution.py:174
  101.5 1.6 %collective-permute-start.40 = (f32[64,256]{1,0:T(8,128)S(1)}, f32[64,256]{1,0:T(8,128)S(1)}, u32[]{:S(2)}, u32[]{:S(2)}) collective-permute-start(f32[64,256]{1,0:T(8,128)S(1)} %bitcast_add_fusion.6), channel_id=1, source_target_pairs={{0,4},{4,0},{8,12},{12,8},{16,20},{20,16},{24,28},{28,24},{1,5},{5... | collective-permute-start | bytes 196616 | tf_op jit(solution)/shard_map/ppermute | solution.py:184
  103.1 1.2 collective-permute-done.33
  104.7 1.2 collective-permute-done.40
  105.9 1.5 %collective-permute-start.41 = (f32[2,64,256]{2,1,0:T(8,128)S(1)}, f32[2,64,256]{2,1,0:T(8,128)S(1)}, u32[]{:S(2)}, u32[]{:S(2)}) collective-permute-start(f32[2,64,256]{2,1,0:T(8,128)S(1)} %maximum_select_fusion.6), channel_id=1, source_target_pairs={{0,16},{4,20},{8,24},{12,28},{16,0},{20,4},{24,8},{28,12},{1,17},{... | collective-permute-start | bytes 393224 | tf_op jit(solution)/shard_map/ppermute | solution.py:184
  107.4 2.9 %collective-permute-done.34 = f32[64,256]{1,0:T(8,128)S(1)} collective-permute-done((f32[64,256]{1,0:T(8,128)S(1)}, f32[64,256]{1,0:T(8,128)S(1)}, u32[]{:S(2)}, u32[]{:S(2)}) %collective-permute-start.34) | collective-permute-done | bytes 65568 | tf_op jit(solution)/shard_map/ppermute | solution.py:184
  110.5 1.3 %collective-permute-done.41 = f32[2,64,256]{2,1,0:T(8,128)S(1)} collective-permute-done((f32[2,64,256]{2,1,0:T(8,128)S(1)}, f32[2,64,256]{2,1,0:T(8,128)S(1)}, u32[]{:S(2)}, u32[]{:S(2)}) %collective-permute-start.41) | collective-permute-done | bytes 131104 | tf_op jit(solution)/shard_map/ppermute | solution.py:184
  111.8 3.4 %collective-permute-start.42 = (f32[2,2,64,256]{3,2,1,0:T(8,128)S(1)}, f32[2,2,64,256]{3,2,1,0:T(8,128)S(1)}, u32[]{:S(2)}, u32[]{:S(2)}) collective-permute-start(f32[2,2,64,256]{3,2,1,0:T(8,128)S(1)} %maximum_select_fusion.3), channel_id=1, source_target_pairs={{0,8},{4,12},{8,0},{12,4},{16,24},{20,28},{24,16},{28,20},{1,9},{5... | collective-permute-start | bytes 786440 | tf_op jit(solution)/shard_map/ppermute | solution.py:184
  116.1 2.1 %collective-permute-start.36 = (f32[2,2,64,256]{3,2,0,1:T(8,128)S(1)}, f32[2,2,64,256]{3,2,0,1:T(8,128)S(1)}, u32[]{:S(2)}, u32[]{:S(2)}) collective-permute-start(f32[2,2,64,256]{3,2,0,1:T(8,128)S(1)} %maximum_select_fusion.2), channel_id=1, source_target_pairs={{0,4},{4,0},{8,12},{12,8},{16,20},{20,16},{24,28},{28,24},{1,5},{5... | collective-permute-start | bytes 786440 | tf_op jit(solution)/shard_map/ppermute | solution.py:184
  118.3 1.3 %collective-permute-done.42 = f32[2,2,64,256]{3,2,1,0:T(8,128)S(1)} collective-permute-done((f32[2,2,64,256]{3,2,1,0:T(8,128)S(1)}, f32[2,2,64,256]{3,2,1,0:T(8,128)S(1)}, u32[]{:S(2)}, u32[]{:S(2)}) %collective-permute-start.42) | collective-permute-done | bytes 262176 | tf_op jit(solution)/shard_map/ppermute | solution.py:184
  119.6 2.9 %collective-permute-done.36 = f32[2,2,64,256]{3,2,0,1:T(8,128)S(1)} collective-permute-done((f32[2,2,64,256]{3,2,0,1:T(8,128)S(1)}, f32[2,2,64,256]{3,2,0,1:T(8,128)S(1)}, u32[]{:S(2)}, u32[]{:S(2)}) %collective-permute-start.36) | collective-permute-done | bytes 262176 | tf_op jit(solution)/shard_map/ppermute | solution.py:184
  122.5 1.1 maximum_bitcast_fusion
  (151 shorter events, 22.2 us)
Async XLA Ops:
  0.6 14.0 %copy-start.12 = (bf16[1,512,512]{2,1,0:T(8,128)(2,1)S(1)}, bf16[1,512,512]{2,1,0:T(8,128)(2,1)}, u32[]{:S(2)}) copy-start(bf16[1,512,512]{2,1,0:T(8,128)(2,1)} %param.31) | copy-start | bytes 1572868
  0.6 15.2 %collective-permute-start.28 = (bf16[1,1,512,512]{3,2,1,0:T(8,128)(2,1)}, bf16[1,1,512,512]{3,2,1,0:T(8,128)(2,1)S(1)}, u32[]{:S(2)}, u32[]{:S(2)}) collective-permute-start(bf16[1,1,512,512]{3,2,1,0:T(8,128)(2,1)} %bitcast.422), channel_id=1, source_target_pairs={{0,2},{1,3},{2,0},{3,1},{4,6},{5,7},{6,4},{7,5},{8,10},{9,11},{10,... | collective-permute-start | bytes 1572872 | tf_op jit(solution)/shard_map/ppermute | solution.py:132
  10.8 5.2 %copy-start.19 = (s32[1,1,2,512]{3,2,1,0:T(2,128)S(1)}, s32[1,1,2,512]{3,2,1,0:T(2,128)}, u32[]{:S(2)}) copy-start(s32[1,1,2,512]{3,2,1,0:T(2,128)} %param.34) | copy-start | bytes 12292
  10.8 5.2 %copy-start.20 = (s32[1,1,2,512]{3,2,1,0:T(2,128)S(1)}, s32[1,1,2,512]{3,2,1,0:T(2,128)}, u32[]{:S(2)}) copy-start(s32[1,1,2,512]{3,2,1,0:T(2,128)} %param.33) | copy-start | bytes 12292
  10.8 5.2 %copy-start.21 = (s32[1,1,2,512]{3,2,1,0:T(2,128)S(1)}, s32[1,1,2,512]{3,2,1,0:T(2,128)}, u32[]{:S(2)}) copy-start(s32[1,1,2,512]{3,2,1,0:T(2,128)} %param.36) | copy-start | bytes 12292
  10.8 5.2 %copy-start.22 = (s32[1,1,2,512]{3,2,1,0:T(2,128)S(1)}, s32[1,1,2,512]{3,2,1,0:T(2,128)}, u32[]{:S(2)}) copy-start(s32[1,1,2,512]{3,2,1,0:T(2,128)} %param.35) | copy-start | bytes 12292
  15.9 2.7 %collective-permute-start.29 = (bf16[2,1,512,512]{3,2,0,1:T(8,128)(2,1)S(1)}, bf16[2,1,512,512]{3,2,0,1:T(8,128)(2,1)S(1)}, u32[]{:S(2)}, u32[]{:S(2)}) collective-permute-start(bf16[2,1,512,512]{3,2,0,1:T(8,128)(2,1)S(1)} %bitcast.385), channel_id=1, source_target_pairs={{0,1},{1,0},{2,3},{3,2},{4,5},{5,4},{6,7},{7,6},{8,9},{9,8},{10,11... | collective-permute-start | bytes 3145736 | tf_op jit(solution)/shard_map/ppermute | solution.py:132
  23.7 15.1 %copy-start.2 = (bf16[2,512,512]{2,1,0:T(8,128)(2,1)}, bf16[2,512,512]{2,1,0:T(8,128)(2,1)S(1)}, u32[]{:S(2)}) copy-start(bf16[2,512,512]{2,1,0:T(8,128)(2,1)S(1)} %get-tuple-element.418) | copy-start | bytes 3145732
  25.5 1.2 copy-start.26
  25.5 1.3 %copy-start.9 = (f32[256,512]{1,0:T(8,128)S(1)}, f32[256,512]{1,0:T(8,128)}, u32[]{:S(2)}) copy-start(f32[256,512]{1,0:T(8,128)} %param.29) | copy-start | bytes 1572868
  25.8 1.9 %copy-start = (f32[256,512]{1,0:T(8,128)S(1)}, f32[256,512]{1,0:T(8,128)}, u32[]{:S(2)}) copy-start(f32[256,512]{1,0:T(8,128)} %param.27) | copy-start | bytes 1572868
  25.8 1.9 %copy-start.18 = (f32[256]{0:T(256)S(1)}, f32[256]{0:T(256)}, u32[]{:S(2)}) copy-start(f32[256]{0:T(256)} %param.28) | copy-start | bytes 3076
  27.7 9.7 %collective-permute-start.23 = (bf16[257,512]{1,0:T(8,128)(2,1)S(1)}, bf16[257,512]{1,0:T(8,128)(2,1)}, u32[]{:S(2)}, u32[]{:S(2)}) collective-permute-start(bf16[257,512]{1,0:T(8,128)(2,1)S(1)} %get-tuple-element.211), channel_id=1, source_target_pairs={{0,12},{4,8},{8,4},{12,0},{16,28},{20,24},{24,20},{28,16},{1,13},{... | collective-permute-start | bytes 789512 | tf_op jit(solution)/shard_map/cond/branch_2_fun/ppermute | solution.py:321
  38.4 2.1 %copy-start.4 = (f32[512,512]{0,1:T(8,128)}, f32[512,512]{0,1:T(8,128)S(1)}, u32[]{:S(2)}) copy-start(f32[512,512]{0,1:T(8,128)S(1)} %get-tuple-element.290) | copy-start | bytes 3145732
  38.4 2.1 %copy-start.5 = (f32[512,512]{0,1:T(8,128)}, f32[512,512]{0,1:T(8,128)S(1)}, u32[]{:S(2)}) copy-start(f32[512,512]{0,1:T(8,128)S(1)} %get-tuple-element.291) | copy-start | bytes 3145732
  38.8 3.5 %copy-start.15 = (bf16[256,512]{1,0:T(8,128)(2,1)}, bf16[256,512]{1,0:T(8,128)(2,1)S(1)}, u32[]{:S(2)}) copy-start(bf16[256,512]{1,0:T(8,128)(2,1)S(1)} %convolution_convert_fusion.17) | copy-start | bytes 786436
  39.1 4.4 %copy-start.13 = (bf16[256,512]{1,0:T(8,128)(2,1)}, bf16[256,512]{1,0:T(8,128)(2,1)S(1)}, u32[]{:S(2)}) copy-start(bf16[256,512]{1,0:T(8,128)(2,1)S(1)} %convolution_convert_fusion.15) | copy-start | bytes 786436
  44.0 1.2 copy-start.10
  45.3 0.7 copy-start.6
  50.7 2.8 %copy-start.3 = (bf16[2,512,512]{2,1,0:T(8,128)(2,1)S(1)}, bf16[2,512,512]{2,1,0:T(8,128)(2,1)}, u32[]{:S(2)}) copy-start(bf16[2,512,512]{2,1,0:T(8,128)(2,1)} %copy-done.2) | copy-start | bytes 3145732
  50.7 3.2 %copy-start.7 = (bf16[256,512]{1,0:T(8,128)(2,1)S(1)}, bf16[256,512]{1,0:T(8,128)(2,1)}, u32[]{:S(2)}) copy-start(bf16[256,512]{1,0:T(8,128)(2,1)} %copy-done.6) | copy-start | bytes 786436
  52.7 2.3 %copy-start.16 = (bf16[256,512]{1,0:T(8,128)(2,1)S(1)}, bf16[256,512]{1,0:T(8,128)(2,1)}, u32[]{:S(2)}) copy-start(bf16[256,512]{1,0:T(8,128)(2,1)} %copy-done.15) | copy-start | bytes 786436
  52.7 2.5 %copy-start.11 = (bf16[256,256]{1,0:T(8,128)(2,1)S(1)}, bf16[256,256]{1,0:T(8,128)(2,1)}, u32[]{:S(2)}) copy-start(bf16[256,256]{1,0:T(8,128)(2,1)} %copy-done.10) | copy-start | bytes 393220
  52.7 2.5 %copy-start.14 = (bf16[256,512]{1,0:T(8,128)(2,1)S(1)}, bf16[256,512]{1,0:T(8,128)(2,1)}, u32[]{:S(2)}) copy-start(bf16[256,512]{1,0:T(8,128)(2,1)} %copy-done.13) | copy-start | bytes 786436
  52.7 6.1 %collective-permute-start.30 = (f32[2,8,64,512]{3,2,1,0:T(8,128)S(1)}, f32[2,8,64,512]{3,2,1,0:T(8,128)S(1)}, u32[]{:S(2)}, u32[]{:S(2)}) collective-permute-start(f32[2,8,64,512]{3,2,1,0:T(8,128)S(1)} %select_add_fusion), channel_id=1, source_target_pairs={{0,1},{1,0},{2,3},{3,2},{4,5},{5,4},{6,7},{7,6},{8,9},{9,8},{10,11... | collective-permute-start | bytes 6291464 | tf_op jit(solution)/shard_map/ppermute | solution.py:216
  54.3 4.5 %copy-start.1 = (f32[512,512]{1,0:T(8,128)S(1)}, f32[512,512]{1,0:T(8,128)}, u32[]{:S(2)}) copy-start(f32[512,512]{1,0:T(8,128)} %copy.32) | copy-start | bytes 3145732
  54.3 4.4 %copy-start.23 = (pred[2]{0:T(512)(128)(4,1)S(1)}, pred[2]{0:T(512)(128)(4,1)}, u32[]{:S(2)}) copy-start(pred[2]{0:T(512)(128)(4,1)} %get-tuple-element.400) | copy-start | bytes 10
  54.3 4.4 %copy-start.24 = (pred[2]{0:T(512)(128)(4,1)S(1)}, pred[2]{0:T(512)(128)(4,1)}, u32[]{:S(2)}) copy-start(pred[2]{0:T(512)(128)(4,1)} %get-tuple-element.401) | copy-start | bytes 10
  54.4 4.4 %copy-start.25 = (pred[2]{0:T(512)(128)(4,1)S(1)}, pred[2]{0:T(512)(128)(4,1)}, u32[]{:S(2)}) copy-start(pred[2]{0:T(512)(128)(4,1)} %get-tuple-element.402) | copy-start | bytes 10
  59.9 1.0 copy-start.17
  60.9 19.9 %collective-permute-start.6 = (f32[2,2,2,64,256]{4,3,2,1,0:T(8,128)S(1)}, f32[2,2,2,64,256]{4,3,2,1,0:T(8,128)S(1)}, u32[]{:S(2)}, u32[]{:S(2)}) collective-permute-start(f32[2,2,2,64,256]{4,3,2,1,0:T(8,128)S(1)} %bitcast.415), channel_id=1, source_target_pairs={{0,4},{4,0},{8,12},{12,8},{16,20},{20,16},{24,28},{28,24},{1,5},{5... | collective-permute-start | bytes 1572872 | tf_op jit(solution)/shard_map/cond/branch_2_fun/ppermute | solution.py:236
  62.6 18.3 %collective-permute-start.7 = (f32[2,2,2,64,256]{4,3,2,1,0:T(8,128)S(1)}, f32[2,2,2,64,256]{4,3,2,1,0:T(8,128)S(1)}, u32[]{:S(2)}, u32[]{:S(2)}) collective-permute-start(f32[2,2,2,64,256]{4,3,2,1,0:T(8,128)S(1)} %bitcast.408), channel_id=1, source_target_pairs={{0,2},{1,3},{2,0},{3,1},{4,6},{5,7},{6,4},{7,5},{8,10},{9,11},{10,... | collective-permute-start | bytes 1572872 | tf_op jit(solution)/shard_map/cond/branch_2_fun/ppermute | solution.py:236
  64.2 9.1 %collective-permute-start.8 = (bf16[256,512]{1,0:T(8,128)(2,1)S(1)}, bf16[256,512]{1,0:T(8,128)(2,1)S(1)}, u32[]{:S(2)}, u32[]{:S(2)}) collective-permute-start(bf16[256,512]{1,0:T(8,128)(2,1)S(1)} %get-tuple-element.259), channel_id=1, source_target_pairs={{0,12},{4,8},{8,4},{12,0},{16,28},{20,24},{24,20},{28,16},{1,13},{... | collective-permute-start | bytes 786440 | tf_op jit(solution)/shard_map/cond/branch_2_fun/ppermute | solution.py:237
  80.9 3.6 %copy-start.8 = (f32[256,512]{1,0:T(8,128)S(1)}, f32[256,512]{1,0:T(8,128)}, u32[]{:S(2)}) copy-start(f32[256,512]{1,0:T(8,128)} %get-tuple-element.417) | copy-start | bytes 1572868
  81.1 7.8 %collective-permute-start.37 = (f32[2,2,64,256]{3,2,0,1:T(8,128)S(1)}, f32[2,2,64,256]{3,2,0,1:T(8,128)S(1)}, u32[]{:S(2)}, u32[]{:S(2)}) collective-permute-start(f32[2,2,64,256]{3,2,0,1:T(8,128)S(1)} %dynamic-slice_bitcast_fusion.2), channel_id=1, source_target_pairs={{0,4},{4,0},{8,12},{12,8},{16,20},{20,16},{24,28},{28,24},{1,5},{5... | collective-permute-start | bytes 786440 | tf_op jit(solution)/shard_map/ppermute | solution.py:174
  82.9 7.9 %collective-permute-start.31 = (f32[2,2,64,256]{3,2,0,1:T(8,128)S(1)}, f32[2,2,64,256]{3,2,0,1:T(8,128)S(1)}, u32[]{:S(2)}, u32[]{:S(2)}) collective-permute-start(f32[2,2,64,256]{3,2,0,1:T(8,128)S(1)} %dynamic-slice_bitcast_fusion.3), channel_id=1, source_target_pairs={{0,8},{4,12},{8,0},{12,4},{16,24},{20,28},{24,16},{28,20},{1,9},{5... | collective-permute-start | bytes 786440 | tf_op jit(solution)/shard_map/ppermute | solution.py:174
  89.0 6.4 %collective-permute-start.38 = (f32[2,64,256]{2,1,0:T(8,128)S(1)}, f32[2,64,256]{2,1,0:T(8,128)S(1)}, u32[]{:S(2)}, u32[]{:S(2)}) collective-permute-start(f32[2,64,256]{2,1,0:T(8,128)S(1)} %dynamic-slice_bitcast_fusion.4), channel_id=1, source_target_pairs={{0,8},{4,12},{8,0},{12,4},{16,24},{20,28},{24,16},{28,20},{1,9},{5... | collective-permute-start | bytes 393224 | tf_op jit(solution)/shard_map/ppermute | solution.py:174
  90.8 9.1 %collective-permute-start.32 = (f32[2,64,256]{2,1,0:T(8,128)S(1)}, f32[2,64,256]{2,1,0:T(8,128)S(1)}, u32[]{:S(2)}, u32[]{:S(2)}) collective-permute-start(f32[2,64,256]{2,1,0:T(8,128)S(1)} %dynamic-slice_bitcast_fusion.5), channel_id=1, source_target_pairs={{0,16},{4,20},{8,24},{12,28},{16,0},{20,4},{24,8},{28,12},{1,17},{... | collective-permute-start | bytes 393224 | tf_op jit(solution)/shard_map/ppermute | solution.py:174
  95.4 6.1 %collective-permute-start.39 = (f32[64,256]{1,0:T(8,128)S(1)}, f32[64,256]{1,0:T(8,128)S(1)}, u32[]{:S(2)}, u32[]{:S(2)}) collective-permute-start(f32[64,256]{1,0:T(8,128)S(1)} %dynamic-slice_bitcast_fusion.6), channel_id=1, source_target_pairs={{0,16},{4,20},{8,24},{12,28},{16,0},{20,4},{24,8},{28,12},{1,17},{... | collective-permute-start | bytes 196616 | tf_op jit(solution)/shard_map/ppermute | solution.py:174
  99.9 4.3 %collective-permute-start.33 = (f32[64,256]{1,0:T(8,128)S(1)}, f32[64,256]{1,0:T(8,128)S(1)}, u32[]{:S(2)}, u32[]{:S(2)}) collective-permute-start(f32[64,256]{1,0:T(8,128)S(1)} %dynamic-slice_bitcast_fusion.7), channel_id=1, source_target_pairs={{0,2},{1,3},{2,0},{3,1},{4,6},{5,7},{6,4},{7,5},{8,10},{9,11},{10,... | collective-permute-start | bytes 196616 | tf_op jit(solution)/shard_map/ppermute | solution.py:174
  101.5 4.3 %collective-permute-start.40 = (f32[64,256]{1,0:T(8,128)S(1)}, f32[64,256]{1,0:T(8,128)S(1)}, u32[]{:S(2)}, u32[]{:S(2)}) collective-permute-start(f32[64,256]{1,0:T(8,128)S(1)} %bitcast_add_fusion.6), channel_id=1, source_target_pairs={{0,4},{4,0},{8,12},{12,8},{16,20},{20,16},{24,28},{28,24},{1,5},{5... | collective-permute-start | bytes 196616 | tf_op jit(solution)/shard_map/ppermute | solution.py:184
  104.3 6.1 %collective-permute-start.34 = (f32[64,256]{1,0:T(8,128)S(1)}, f32[64,256]{1,0:T(8,128)S(1)}, u32[]{:S(2)}, u32[]{:S(2)}) collective-permute-start(f32[64,256]{1,0:T(8,128)S(1)} %bitcast_add_fusion.7), channel_id=1, source_target_pairs={{0,16},{4,20},{8,24},{12,28},{16,0},{20,4},{24,8},{28,12},{1,17},{... | collective-permute-start | bytes 196616 | tf_op jit(solution)/shard_map/ppermute | solution.py:184
  105.9 5.9 %collective-permute-start.41 = (f32[2,64,256]{2,1,0:T(8,128)S(1)}, f32[2,64,256]{2,1,0:T(8,128)S(1)}, u32[]{:S(2)}, u32[]{:S(2)}) collective-permute-start(f32[2,64,256]{2,1,0:T(8,128)S(1)} %maximum_select_fusion.6), channel_id=1, source_target_pairs={{0,16},{4,20},{8,24},{12,28},{16,0},{20,4},{24,8},{28,12},{1,17},{... | collective-permute-start | bytes 393224 | tf_op jit(solution)/shard_map/ppermute | solution.py:184
  110.3 5.7 %collective-permute-start.35 = (f32[2,64,256]{2,1,0:T(8,128)S(1)}, f32[2,64,256]{2,1,0:T(8,128)S(1)}, u32[]{:S(2)}, u32[]{:S(2)}) collective-permute-start(f32[2,64,256]{2,1,0:T(8,128)S(1)} %maximum_select_fusion.4), channel_id=1, source_target_pairs={{0,8},{4,12},{8,0},{12,4},{16,24},{20,28},{24,16},{28,20},{1,9},{5... | collective-permute-start | bytes 393224 | tf_op jit(solution)/shard_map/ppermute | solution.py:184
  111.8 7.7 %collective-permute-start.42 = (f32[2,2,64,256]{3,2,1,0:T(8,128)S(1)}, f32[2,2,64,256]{3,2,1,0:T(8,128)S(1)}, u32[]{:S(2)}, u32[]{:S(2)}) collective-permute-start(f32[2,2,64,256]{3,2,1,0:T(8,128)S(1)} %maximum_select_fusion.3), channel_id=1, source_target_pairs={{0,8},{4,12},{8,0},{12,4},{16,24},{20,28},{24,16},{28,20},{1,9},{5... | collective-permute-start | bytes 786440 | tf_op jit(solution)/shard_map/ppermute | solution.py:184
  116.1 6.4 %collective-permute-start.36 = (f32[2,2,64,256]{3,2,0,1:T(8,128)S(1)}, f32[2,2,64,256]{3,2,0,1:T(8,128)S(1)}, u32[]{:S(2)}, u32[]{:S(2)}) collective-permute-start(f32[2,2,64,256]{3,2,0,1:T(8,128)S(1)} %maximum_select_fusion.2), channel_id=1, source_target_pairs={{0,4},{4,0},{8,12},{12,8},{16,20},{20,16},{24,28},{28,24},{1,5},{5... | collective-permute-start | bytes 786440 | tf_op jit(solution)/shard_map/ppermute | solution.py:184

commit v4 on v1

--- a/solution.py
+++ b/solution.py
@@ -235,11 +235,11 @@
         switch - 1, [first_step(offset) for offset in range(1, count)], low, *sends
     )
     block_low = results[0]
-    outputs = []
-    for (order, gather_order), keep, got in zip(streams, keeps, results[1:]):
-        current = halving_steps(keep + got, order[1:])
-        outputs.append(doubling_steps(current, "bucket", gather_order))
-    return jnp.concatenate(outputs, axis=1), block_low
+    pieces = []
+    for (order, _), keep, got in zip(streams, keeps, results[1:]):
+        pieces.append(halving_steps(keep + got, order[1:]))
+    joined = jnp.concatenate(pieces, axis=1)
+    return doubling_steps(joined, "bucket", streams[0][1]), block_low
 
 
 def on_device(

time: 119 us -> 131 us (1.10)
  other arithmetic: 18.9 us -> 24.3 us
  waiting for transfers between devices: 61.9 us -> 65 us
  local copies, waits for them, and re-layouts: 5.73 us -> 8.25 us
    ppermute x6, waiting for transfers between devices: 14.1 us -> 16.9 us  [halving_steps(): got = lax.ppermute(send, name, [(k, k ^ bit) for k in range(count)])]
    dot_general x4, matrix products: 1.49 us -> 3.73 us  [one_round(): jnp.dot(carried, matrix.T, preferred_element_type=jnp.float32)]
    eq x3, other arithmetic: 4.55 us -> 6.32 us  [selected_term(): hit = (rel_ids[slot_index] == wanted)[:, :, None, None]]
    add x1, other arithmetic: 0.85 us -> 2.44 us  [reduce_gradients(): keep + lax.ppermute(send, 'rel', [(k, k ^ first) for k in range(rel_count)])]
    add x1, other arithmetic: 0.6 us -> 2.11 us  [selected_term(): total + jnp.where(hit, gradient[None, None, :, columns], jnp.float32(0.0))]
    dot_general x4, matrix products: 2.7 us -> 1.29 us  [one_round(): jnp.dot(left_half, matrix, preferred_element_type=jnp.float32)]
    ppermute x6 -> x3, waiting for transfers between devices: 16.8 us -> 17.8 us  [doubling_steps(): got = lax.ppermute(current, name, [(k, k ^ bit) for k in range(count)])]
    ppermute x6 -> x3, starting transfers between devices: 2.9 us -> 2.05 us  [doubling_steps(): got = lax.ppermute(current, name, [(k, k ^ bit) for k in range(count)])]
  transfers between devices with their start and end apart: 19 -> 16, of which waited for: 16 -> 13; matrix products, arithmetic and copies ran while one was open for 15% -> 18% of each run, Pallas kernels for 0% -> 0%
where the time goes in v4:
time: 131 us; the launch traced here: 132 us
  waiting for transfers between devices  65 us (50%)
  other arithmetic  24.3 us (19%)
  matrix products  16.1 us (12%)
  starting transfers between devices  15.6 us (12%)
  local copies, waits for them, and re-layouts  8.25 us (6%)
  between operations  2.17 us (2%)
    ppermute x3, waiting for transfers between devices, doubling_steps(): got = lax.ppermute(current, name, [(k, k ^ bit) for k in range(count)])  17.8 us
    ppermute x6, waiting for transfers between devices, halving_steps(): got = lax.ppermute(send, name, [(k, k ^ bit) for k in range(count)])  16.9 us
    ppermute x1, waiting for transfers between devices, run(): return (lax.ppermute(low_part, 'bucket', pairs),) + tuple(moved)  14.7 us
    ppermute x1, waiting for transfers between devices, run(): return tuple((lax.ppermute(array, 'bucket', pairs) for array in arrays))  12.7 us
    eq x3, other arithmetic, selected_term(): hit = (rel_ids[slot_index] == wanted)[:, :, None, None]  6.32 us
    ppermute x6, starting transfers between devices, halving_steps(): got = lax.ppermute(send, name, [(k, k ^ bit) for k in range(count)])  4.33 us
    dot_general x4, matrix products, one_round(): jnp.dot(carried, matrix.T, preferred_element_type=jnp.float32)  3.73 us
    ppermute x2, starting transfers between devices, run(): moved.append(lax.ppermute(part, name, [(k, k ^ bit) for k in range(size)]))  3.19 us
  transfers between devices with their start and end apart: 16, of which 13 were waited for; matrix products, arithmetic and copies ran while one was open for 18% of the time, Pallas kernels for 0%

profile of v4, /device:TPU:0, one launch (start us, length us, event | category | flops | bytes accessed | tf_op | source)
XLA Modules:
  0.0 131.5 jit_solution(12217348154349686748)
XLA Ops:
  0.6 3.1 %collective-permute-start.28 = (bf16[1,1,512,512]{3,2,1,0:T(8,128)(2,1)}, bf16[1,1,512,512]{3,2,1,0:T(8,128)(2,1)S(1)}, u32[]{:S(2)}, u32[]{:S(2)}) collective-permute-start(bf16[1,1,512,512]{3,2,1,0:T(8,128)(2,1)} %bitcast.255), channel_id=1, source_target_pairs={{0,2},{1,3},{2,0},{3,1},{4,6},{5,7},{6,4},{7,5},{8,10},{9,11},{10,... | collective-permute-start | bytes 1572872 | tf_op jit(solution)/shard_map/ppermute | solution.py:125
  3.7 0.8 compare_and_fusion
  4.5 1.5 %fusion.59 = (s32[1,1,1]{2,1,0:T(1,128)}, s32[1,1,1]{2,1,0:T(1,128)}, s32[1,1,1]{2,1,0:T(1,128)}, s32[1,1,1]{2,1,0:T(1,128)}) fusion(s32[1,1,4]{2,1,0:T(1,128)} %param.32), kind=kLoop, calls=%fused_computation.180 | loop fusion | bytes 32 | tf_op jit(solution)/shard_map/slice | solution.py:142
  6.0 1.2 compare_bitcast_fusion.7
  7.2 1.8 %convert_element_type.123 = bf16[256,512]{1,0:T(8,128)(2,1)} convert(f32[256,512]{1,0:T(8,128)} %param.27) | non-fusion elementwise | flops 131072 | bytes 786432 | tf_op jit(solution)/shard_map/convert_element_type | solution.py:44
  9.0 1.1 convert_element_type.125
  10.8 2.6 %compare_bitcast_fusion.2 = (pred[2]{0:T(512)(128)(4,1)}, pred[2]{0:T(512)(128)(4,1)}, pred[2]{0:T(512)(128)(4,1)}) fusion(s32[2,1,1]{0,2,1:T(1,128)S(1)} %get-tuple-element.171, s32[]{:T(128)} %bitcast.41, s32[]{:T(128)} %bitcast.45, s32[]{:T(128)} %bitcast.48), kind=kLoop, calls=%fused_computation.151 | loop fusion | flops 6 | bytes 26 | tf_op jit(solution)/shard_map/eq | solution.py:142
  13.4 2.4 %collective-permute-done.28 = bf16[1,1,512,512]{3,2,1,0:T(8,128)(2,1)S(1)} collective-permute-done((bf16[1,1,512,512]{3,2,1,0:T(8,128)(2,1)}, bf16[1,1,512,512]{3,2,1,0:T(8,128)(2,1)S(1)}, u32[]{:S(2)}, u32[]{:S(2)}) %collective-permute-start.28) | collective-permute-done | bytes 524320 | tf_op jit(solution)/shard_map/ppermute | solution.py:125
  17.2 0.6 compare_select_fusion
  18.7 0.6 gather_fusion.1
  19.3 1.6 %gather_fusion = bf16[2,512,512]{2,1,0:T(8,128)(2,1)} fusion(bf16[4,512,512]{2,1,0:T(8,128)(2,1)S(1)} %bitcast.228, s32[1024]{0:T(1024)S(1)} %pad_clamp_fusion.1), kind=kCustom, calls=%fused_computation.clone | custom fusion | bytes 2097160 | tf_op jit(solution)/shard_map/jit(_take)/gather | solution.py:270
  20.9 1.5 %broadcast_select_fusion = (bf16[2,512,512]{2,1,0:T(8,128)(2,1)S(1)}, bf16[2,512,512]{2,1,0:T(8,128)(2,1)S(1)}) fusion(bf16[2,512,512]{2,1,0:T(8,128)(2,1)S(1)} %gather_fusion.1, pred[2]{0:T(512)(128)(4,1)S(1)} %get-tuple-element.146, bf16[2,512,512]{2,1,0:T(8,128)(2,1)} %gather_fusion, pred[2]{0:T(512)(128)(4,1)S(1)} %get-tuple-element.182), kind=kLoop, calls=%fused_computation.61 | loop fusion | flops 1048576 | bytes 4194308 | tf_op jit(solution)/shard_map/jit(_take)/select_n | solution.py:270
  28.3 0.9 fusion.20
  29.2 15.6 %conditional.4 = (bf16[257,512]{1,0:T(8,128)(2,1)}) conditional(s32[]{:T(128)} %bitcast.31, bf16[257,512]{1,0:T(8,128)(2,1)S(1)} %maximum_maximum_fusion, bf16[257,512]{1,0:T(8,128)(2,1)S(1)} %maximum_maximum_fusion, bf16[257,512]{1,0:T(8,128)(2,1)S(1)} %maximum_maximum_fusion, ...), branch_computations={%region_2.4_spmd, %region_3.5_spmd, %region_4.6_spmd, %region_5.7_... | conditional | bytes 1052720 | solution.py:85
  29.2 2.9 %collective-permute-start.3 = (bf16[257,512]{1,0:T(8,128)(2,1)S(1)}, bf16[257,512]{1,0:T(8,128)(2,1)}, u32[]{:S(2)}, u32[]{:S(2)}) collective-permute-start(bf16[257,512]{1,0:T(8,128)(2,1)S(1)} %param.5), channel_id=1, source_target_pairs={{0,16},{4,20},{8,24},{12,28},{16,0},{20,4},{24,8},{28,12},{1,17},{... | collective-permute-start | bytes 789512 | tf_op jit(solution)/shard_map/cond/branch_3_fun/ppermute | solution.py:80
  32.1 12.7 %collective-permute-done.3 = bf16[257,512]{1,0:T(8,128)(2,1)} collective-permute-done((bf16[257,512]{1,0:T(8,128)(2,1)S(1)}, bf16[257,512]{1,0:T(8,128)(2,1)}, u32[]{:S(2)}, u32[]{:S(2)}) %collective-permute-start.3) | collective-permute-done | bytes 263200 | tf_op jit(solution)/shard_map/cond/branch_3_fun/ppermute | solution.py:80
  44.8 1.2 fusion.7
  46.6 1.2 convolution_convert_fusion.2
  47.8 1.2 fusion.3
  49.6 0.6 copy-done.13
  50.2 1.2 convolution_convert_fusion
  51.4 0.7 copy-done.7
  52.8 2.1 %select_add_fusion = f32[2,8,64,512]{3,2,1,0:T(8,128)} fusion(f32[8,64,512]{2,1,0:T(8,128)S(1)} %bitcast.223, f32[8,64,512]{2,1,0:T(8,128)S(1)} %bitcast.225, f32[8,64,512]{2,1,0:T(8,128)S(1)} %bitcast.219, f32[8,64,512]{2,1,0:T(8,128)S(1)} %bitcast.221, pred[2]{0:T(512)(128)(4,1)S(1)} %copy-done.29, pred[2]{0:T(512)(128)(4,1)S(1)} %copy-done.28, ...), kind=kLoop, calls=%fused_computation.16 | loop fusion | flops 3670016 | bytes 6291464 | tf_op jit(solution)/shard_map/add | solution.py:143
  55.0 2.6 %compare_bitcast_fusion.6 = (pred[2]{0:T(512)(128)(4,1)S(1)}, pred[2]{0:T(512)(128)(4,1)S(1)}, pred[2]{0:T(512)(128)(4,1)S(1)}) fusion(s32[2,1,1]{0,2,1:T(1,128)} %get-tuple-element.141, s32[]{:T(128)} %bitcast.41, s32[]{:T(128)} %bitcast.45, s32[]{:T(128)} %bitcast.48), kind=kLoop, calls=%fused_computation.155 | loop fusion | flops 6 | bytes 26 | tf_op jit(solution)/shard_map/eq | solution.py:142
  57.6 1.4 %fusion.22 = f32[256,512]{1,0:T(8,128)S(1)} fusion(bf16[256,512]{1,0:T(8,128)(2,1)S(1)} %convolution_convert_fusion.2, bf16[2,512,512]{2,1,0:T(8,128)(2,1)} %copy-done.6), kind=kOutput, calls=%fused_computation.97 | convolution fusion | flops 134217728 | bytes 1310720 | tf_op jit(solution)/shard_map/dot_general | solution.py:61
  59.0 1.6 %multiply_reduce_fusion.1 = (f32[256]{0:T(256)S(1)}, f32[256,512]{1,0:T(8,128)S(1)}) fusion(f32[256,512]{1,0:T(8,128)S(1)} %fusion.22, bf16[256,512]{1,0:T(8,128)(2,1)} %copy-done.7, bf16[2,512,512]{2,1,0:T(8,128)(2,1)} %copy-done.6), kind=kOutput, calls=%fused_computation.83 | convolution fusion | flops 134610688 | bytes 1836032 | tf_op jit(solution)/shard_map/dot_general | solution.py:61
  61.2 0.7 slice_convert_fusion
  62.1 1.0 multiply_reduce_fusion
  63.2 1.0 divide_subtract_fusion.1
  64.2 2.4 %add_add_fusion = f32[2,8,64,512]{3,2,1,0:T(8,128)S(1)} fusion(f32[2,8,64,512]{3,2,1,0:T(8,128)} %collective-permute-done.30, f32[8,64,512]{2,1,0:T(8,128)S(1)} %bitcast.224, f32[8,64,512]{2,1,0:T(8,128)S(1)} %bitcast.226, f32[8,64,512]{2,1,0:T(8,128)S(1)} %bitcast.220, f32[8,64,512]{2,1,0:T(8,128)S(1)} %bitcast.222, pred[2]{0:T(512)(128)(4,1)S(1)} %get-tuple-element.174, ...), kind=kLoop, calls=%fused_computation.17 | loop fusion | flops 4194304 | bytes 8388616 | tf_op jit(solution)/shard_map/add | solution.py:209
  67.0 0.8 copy-done.20
  67.8 18.1 %conditional.5 = (f32[256,512]{1,0:T(8,128)S(1)}, f32[2,2,2,64,256]{4,3,0,1,2:T(8,128)S(1)}, f32[2,2,2,64,256]{4,3,0,1,2:T(8,128)S(1)}) conditional(s32[]{:T(128)} %bitcast.31, (f32[1,2,2,2,64,256]{5,4,0,1,2,3:T(8,128)S(1)}, f32[1,2,2,2,64,256]{5,4,1,2,3,0:T(8,128)S(1)}, bf16[256,512]{1,0:T(8,128)(2,1)S(1)}) %tuple.166, ...), branch_computations={%region_10.12_spmd, %region_11.13_spmd, %region_12.14_spmd, %regio... | conditional | flops 131072 | bytes 10223760
  67.9 1.6 %collective-permute-start.16 = (f32[2,2,2,64,256]{4,3,2,1,0:T(8,128)S(1)}, f32[2,2,2,64,256]{4,3,2,1,0:T(8,128)S(1)}, u32[]{:S(2)}, u32[]{:S(2)}) collective-permute-start(f32[2,2,2,64,256]{4,3,2,1,0:T(8,128)S(1)} %bitcast.251), channel_id=1, source_target_pairs={{0,4},{4,0},{8,12},{12,8},{16,20},{20,16},{24,28},{28,24},{1,5},{5... | collective-permute-start | bytes 1572872 | tf_op jit(solution)/shard_map/cond/branch_3_fun/ppermute | solution.py:229
  69.5 1.6 %collective-permute-start.17 = (f32[2,2,2,64,256]{4,3,2,1,0:T(8,128)S(1)}, f32[2,2,2,64,256]{4,3,2,1,0:T(8,128)S(1)}, u32[]{:S(2)}, u32[]{:S(2)}) collective-permute-start(f32[2,2,2,64,256]{4,3,2,1,0:T(8,128)S(1)} %bitcast.244), channel_id=1, source_target_pairs={{0,2},{1,3},{2,0},{3,1},{4,6},{5,7},{6,4},{7,5},{8,10},{9,11},{10,... | collective-permute-start | bytes 1572872 | tf_op jit(solution)/shard_map/cond/branch_3_fun/ppermute | solution.py:229
  71.1 14.7 %collective-permute-done.18 = bf16[256,512]{1,0:T(8,128)(2,1)S(1)} collective-permute-done((bf16[256,512]{1,0:T(8,128)(2,1)S(1)}, bf16[256,512]{1,0:T(8,128)(2,1)S(1)}, u32[]{:S(2)}, u32[]{:S(2)}) %collective-permute-start.18) | collective-permute-done | bytes 262176 | tf_op jit(solution)/shard_map/cond/branch_3_fun/ppermute | solution.py:230
  86.9 6.7 %collective-permute-done.34 = f32[2,2,64,256]{3,2,0,1:T(8,128)S(1)} collective-permute-done((f32[2,2,64,256]{3,2,0,1:T(8,128)S(1)}, f32[2,2,64,256]{3,2,0,1:T(8,128)S(1)}, u32[]{:S(2)}, u32[]{:S(2)}) %collective-permute-start.34) | collective-permute-done | bytes 262176 | tf_op jit(solution)/shard_map/ppermute | solution.py:167
  94.0 2.4 %collective-permute-start.32 = (f32[2,64,256]{2,1,0:T(8,128)S(1)}, f32[2,64,256]{2,1,0:T(8,128)S(1)}, u32[]{:S(2)}, u32[]{:S(2)}) collective-permute-start(f32[2,64,256]{2,1,0:T(8,128)S(1)} %dynamic-slice_bitcast_fusion.5), channel_id=1, source_target_pairs={{0,16},{4,20},{8,24},{12,28},{16,0},{20,4},{24,8},{28,12},{1,17},{... | collective-permute-start | bytes 393224 | tf_op jit(solution)/shard_map/ppermute | solution.py:167
  96.4 2.9 %collective-permute-done.35 = f32[2,64,256]{2,1,0:T(8,128)S(1)} collective-permute-done((f32[2,64,256]{2,1,0:T(8,128)S(1)}, f32[2,64,256]{2,1,0:T(8,128)S(1)}, u32[]{:S(2)}, u32[]{:S(2)}) %collective-permute-start.35) | collective-permute-done | bytes 131104 | tf_op jit(solution)/shard_map/ppermute | solution.py:167
  99.4 1.2 collective-permute-start.36
  100.5 2.8 %collective-permute-done.32 = f32[2,64,256]{2,1,0:T(8,128)S(1)} collective-permute-done((f32[2,64,256]{2,1,0:T(8,128)S(1)}, f32[2,64,256]{2,1,0:T(8,128)S(1)}, u32[]{:S(2)}, u32[]{:S(2)}) %collective-permute-start.32) | collective-permute-done | bytes 131104 | tf_op jit(solution)/shard_map/ppermute | solution.py:167
  103.5 1.6 %collective-permute-done.36 = f32[64,256]{1,0:T(8,128)S(1)} collective-permute-done((f32[64,256]{1,0:T(8,128)S(1)}, f32[64,256]{1,0:T(8,128)S(1)}, u32[]{:S(2)}, u32[]{:S(2)}) %collective-permute-start.36) | collective-permute-done | bytes 65568 | tf_op jit(solution)/shard_map/ppermute | solution.py:167
  105.1 2.6 %collective-permute-done.33 = f32[64,256]{1,0:T(8,128)S(1)} collective-permute-done((f32[64,256]{1,0:T(8,128)S(1)}, f32[64,256]{1,0:T(8,128)S(1)}, u32[]{:S(2)}, u32[]{:S(2)}) %collective-permute-start.33) | collective-permute-done | bytes 65568 | tf_op jit(solution)/shard_map/ppermute | solution.py:167
  107.9 6.8 %collective-permute-done.37 = f32[64,512]{1,0:T(8,128)S(1)} collective-permute-done((f32[64,512]{1,0:T(8,128)S(1)}, f32[64,512]{1,0:T(8,128)S(1)}, u32[]{:S(2)}, u32[]{:S(2)}) %collective-permute-start.37) | collective-permute-done | bytes 131104 | tf_op jit(solution)/shard_map/ppermute | solution.py:177
  115.4 5.8 %collective-permute-done.38 = f32[2,64,512]{2,1,0:T(8,128)S(1)} collective-permute-done((f32[2,64,512]{2,1,0:T(8,128)S(1)}, f32[2,64,512]{2,1,0:T(8,128)S(1)}, u32[]{:S(2)}, u32[]{:S(2)}) %collective-permute-start.38) | collective-permute-done | bytes 262176 | tf_op jit(solution)/shard_map/ppermute | solution.py:177
  121.2 1.9 %collective-permute-start.39 = (f32[2,2,64,512]{3,2,0,1:T(8,128)S(1)}, f32[2,2,64,512]{3,2,0,1:T(8,128)S(1)}, u32[]{:S(2)}, u32[]{:S(2)}) collective-permute-start(f32[2,2,64,512]{3,2,0,1:T(8,128)S(1)} %maximum_select_fusion.1), channel_id=1, source_target_pairs={{0,4},{4,0},{8,12},{12,8},{16,20},{20,16},{24,28},{28,24},{1,5},{5... | collective-permute-start | bytes 1572872 | tf_op jit(solution)/shard_map/ppermute | solution.py:177
  123.1 1.9 %divide_subtract_fusion = f32[256,512]{1,0:T(8,128)} fusion(f32[256,512]{1,0:T(8,128)S(1)} %copy-done.11, f32[256,512]{1,0:T(8,128)S(1)} %get-tuple-element.114, f32[256]{0:T(256)S(1)} %get-tuple-element.138, bf16[257,512]{1,0:T(8,128)(2,1)} %get-tuple-element.215), kind=kLoop, calls=%fused_computation.78 | loop fusion | flops 655360 | bytes 1836032 | tf_op jit(solution)/shard_map/sub | solution.py:28
  125.2 5.2 %collective-permute-done.39 = f32[2,2,64,512]{3,2,0,1:T(8,128)S(1)} collective-permute-done((f32[2,2,64,512]{3,2,0,1:T(8,128)S(1)}, f32[2,2,64,512]{3,2,0,1:T(8,128)S(1)}, u32[]{:S(2)}, u32[]{:S(2)}) %collective-permute-start.39) | collective-permute-done | bytes 524320 | tf_op jit(solution)/shard_map/ppermute | solution.py:177
  130.4 1.1 maximum_select_fusion
  (151 shorter events, 13.5 us)
Async XLA Ops:
  0.6 12.8 %copy-start.15 = (bf16[1,512,512]{2,1,0:T(8,128)(2,1)S(1)}, bf16[1,512,512]{2,1,0:T(8,128)(2,1)}, u32[]{:S(2)}) copy-start(bf16[1,512,512]{2,1,0:T(8,128)(2,1)} %param.31) | copy-start | bytes 1572868
  0.6 15.2 %collective-permute-start.28 = (bf16[1,1,512,512]{3,2,1,0:T(8,128)(2,1)}, bf16[1,1,512,512]{3,2,1,0:T(8,128)(2,1)S(1)}, u32[]{:S(2)}, u32[]{:S(2)}) collective-permute-start(bf16[1,1,512,512]{3,2,1,0:T(8,128)(2,1)} %bitcast.255), channel_id=1, source_target_pairs={{0,2},{1,3},{2,0},{3,1},{4,6},{5,7},{6,4},{7,5},{8,10},{9,11},{10,... | collective-permute-start | bytes 1572872 | tf_op jit(solution)/shard_map/ppermute | solution.py:125
  9.0 7.0 %copy-start.22 = (s32[1,1,2,512]{3,2,1,0:T(2,128)S(1)}, s32[1,1,2,512]{3,2,1,0:T(2,128)}, u32[]{:S(2)}) copy-start(s32[1,1,2,512]{3,2,1,0:T(2,128)} %param.34) | copy-start | bytes 12292
  9.0 7.6 %copy-start.23 = (s32[1,1,2,512]{3,2,1,0:T(2,128)S(1)}, s32[1,1,2,512]{3,2,1,0:T(2,128)}, u32[]{:S(2)}) copy-start(s32[1,1,2,512]{3,2,1,0:T(2,128)} %param.33) | copy-start | bytes 12292
  9.0 8.2 %copy-start.24 = (s32[1,1,2,512]{3,2,1,0:T(2,128)S(1)}, s32[1,1,2,512]{3,2,1,0:T(2,128)}, u32[]{:S(2)}) copy-start(s32[1,1,2,512]{3,2,1,0:T(2,128)} %param.36) | copy-start | bytes 12292
  9.0 8.2 %copy-start.25 = (s32[1,1,2,512]{3,2,1,0:T(2,128)S(1)}, s32[1,1,2,512]{3,2,1,0:T(2,128)}, u32[]{:S(2)}) copy-start(s32[1,1,2,512]{3,2,1,0:T(2,128)} %param.35) | copy-start | bytes 12292
  15.9 2.7 %collective-permute-start.29 = (bf16[2,1,512,512]{3,2,0,1:T(8,128)(2,1)S(1)}, bf16[2,1,512,512]{3,2,0,1:T(8,128)(2,1)S(1)}, u32[]{:S(2)}, u32[]{:S(2)}) collective-permute-start(bf16[2,1,512,512]{3,2,0,1:T(8,128)(2,1)S(1)} %bitcast.229), channel_id=1, source_target_pairs={{0,1},{1,0},{2,3},{3,2},{4,5},{5,4},{6,7},{7,6},{8,9},{9,8},{10,11... | collective-permute-start | bytes 3145736 | tf_op jit(solution)/shard_map/ppermute | solution.py:125
  20.9 1.5 %copy-start.8 = (bf16[256,512]{1,0:T(8,128)(2,1)S(1)}, bf16[256,512]{1,0:T(8,128)(2,1)}, u32[]{:S(2)}) copy-start(bf16[256,512]{1,0:T(8,128)(2,1)} %convert_element_type.123) | copy-start | bytes 786436
  22.4 4.3 %copy-start.6 = (bf16[2,512,512]{2,1,0:T(8,128)(2,1)}, bf16[2,512,512]{2,1,0:T(8,128)(2,1)S(1)}, u32[]{:S(2)}) copy-start(bf16[2,512,512]{2,1,0:T(8,128)(2,1)S(1)} %get-tuple-element.192) | copy-start | bytes 3145732
  25.1 1.2 copy-start.21
  25.1 1.2 copy-start.4
  26.3 1.2 copy-start.2
  26.5 1.4 %copy-start.9 = (bf16[256,512]{1,0:T(8,128)(2,1)}, bf16[256,512]{1,0:T(8,128)(2,1)S(1)}, u32[]{:S(2)}) copy-start(bf16[256,512]{1,0:T(8,128)(2,1)S(1)} %fusion.53) | copy-start | bytes 786436
  26.8 18.0 %copy-start.18 = (bf16[256,512]{1,0:T(8,128)(2,1)}, bf16[256,512]{1,0:T(8,128)(2,1)S(1)}, u32[]{:S(2)}) copy-start(bf16[256,512]{1,0:T(8,128)(2,1)S(1)} %convolution_convert_fusion.3) | copy-start | bytes 786436
  27.1 20.7 %copy-start.16 = (bf16[256,512]{1,0:T(8,128)(2,1)}, bf16[256,512]{1,0:T(8,128)(2,1)S(1)}, u32[]{:S(2)}) copy-start(bf16[256,512]{1,0:T(8,128)(2,1)S(1)} %convolution_convert_fusion.1) | copy-start | bytes 786436
  27.1 1.1 copy-start.34
  27.1 1.2 copy-start.12
  28.2 17.8 %copy-start.30 = (s32[1,1,1,512]{3,2,1,0:T(1,128)S(1)}, s32[1,1,1,512]{3,2,1,0:T(1,128)}, u32[]{:S(2)}) copy-start(s32[1,1,1,512]{3,2,1,0:T(1,128)} %get-tuple-element.165) | copy-start | bytes 6148
  28.2 17.8 %copy-start.31 = (s32[1,1,1,512]{3,2,1,0:T(1,128)S(1)}, s32[1,1,1,512]{3,2,1,0:T(1,128)}, u32[]{:S(2)}) copy-start(s32[1,1,1,512]{3,2,1,0:T(1,128)} %get-tuple-element.163) | copy-start | bytes 6148
  28.2 17.8 %copy-start.33 = (f32[1,1,1,512]{3,2,1,0:T(1,128)S(1)}, f32[1,1,1,512]{3,2,1,0:T(1,128)}, u32[]{:S(2)}) copy-start(f32[1,1,1,512]{3,2,1,0:T(1,128)} %get-tuple-element.161) | copy-start | bytes 6148
  29.2 15.6 %collective-permute-start.3 = (bf16[257,512]{1,0:T(8,128)(2,1)S(1)}, bf16[257,512]{1,0:T(8,128)(2,1)}, u32[]{:S(2)}, u32[]{:S(2)}) collective-permute-start(bf16[257,512]{1,0:T(8,128)(2,1)S(1)} %param.5), channel_id=1, source_target_pairs={{0,16},{4,20},{8,24},{12,28},{16,0},{20,4},{24,8},{28,12},{1,17},{... | collective-permute-start | bytes 789512 | tf_op jit(solution)/shard_map/cond/branch_3_fun/ppermute | solution.py:80
  46.0 3.0 %copy-start.32 = (f32[1,1,1,512]{3,2,1,0:T(1,128)S(1)}, f32[1,1,1,512]{3,2,1,0:T(1,128)}, u32[]{:S(2)}) copy-start(f32[1,1,1,512]{3,2,1,0:T(1,128)} %get-tuple-element.159) | copy-start | bytes 6148
  46.6 5.5 %copy-start.10 = (bf16[256,512]{1,0:T(8,128)(2,1)S(1)}, bf16[256,512]{1,0:T(8,128)(2,1)}, u32[]{:S(2)}) copy-start(bf16[256,512]{1,0:T(8,128)(2,1)} %copy-done.9) | copy-start | bytes 786436
  50.2 2.6 %copy-start.26 = (pred[2]{0:T(512)(128)(4,1)S(1)}, pred[2]{0:T(512)(128)(4,1)}, u32[]{:S(2)}) copy-start(pred[2]{0:T(512)(128)(4,1)} %get-tuple-element.170) | copy-start | bytes 10
  50.2 2.6 %copy-start.27 = (pred[2]{0:T(512)(128)(4,1)S(1)}, pred[2]{0:T(512)(128)(4,1)}, u32[]{:S(2)}) copy-start(pred[2]{0:T(512)(128)(4,1)} %get-tuple-element.175) | copy-start | bytes 10
  50.2 2.6 %copy-start.28 = (pred[2]{0:T(512)(128)(4,1)S(1)}, pred[2]{0:T(512)(128)(4,1)}, u32[]{:S(2)}) copy-start(pred[2]{0:T(512)(128)(4,1)} %get-tuple-element.176) | copy-start | bytes 10
  50.2 2.6 %copy-start.29 = (pred[2]{0:T(512)(128)(4,1)S(1)}, pred[2]{0:T(512)(128)(4,1)}, u32[]{:S(2)}) copy-start(pred[2]{0:T(512)(128)(4,1)} %get-tuple-element.177) | copy-start | bytes 10
  52.8 2.2 %copy-start = (f32[512,512]{1,0:T(8,128)}, f32[512,512]{1,0:T(8,128)S(1)}, u32[]{:S(2)}) copy-start(f32[512,512]{1,0:T(8,128)S(1)} %fusion.63) | copy-start | bytes 3145732
  54.9 9.3 %collective-permute-start.30 = (f32[2,8,64,512]{3,2,1,0:T(8,128)}, f32[2,8,64,512]{3,2,1,0:T(8,128)}, u32[]{:S(2)}, u32[]{:S(2)}) collective-permute-start(f32[2,8,64,512]{3,2,1,0:T(8,128)} %select_add_fusion), channel_id=1, source_target_pairs={{0,1},{1,0},{2,3},{3,2},{4,5},{5,4},{6,7},{7,6},{8,9},{9,8},{10,11... | collective-permute-start | bytes 6291464 | tf_op jit(solution)/shard_map/ppermute | solution.py:209
  54.9 6.9 %copy-start.19 = (bf16[256,512]{1,0:T(8,128)(2,1)S(1)}, bf16[256,512]{1,0:T(8,128)(2,1)}, u32[]{:S(2)}) copy-start(bf16[256,512]{1,0:T(8,128)(2,1)} %copy-done.18) | copy-start | bytes 786436
  55.0 7.2 %copy-start.14 = (bf16[256,256]{1,0:T(8,128)(2,1)S(1)}, bf16[256,256]{1,0:T(8,128)(2,1)}, u32[]{:S(2)}) copy-start(bf16[256,256]{1,0:T(8,128)(2,1)} %copy-done.13) | copy-start | bytes 393220
  55.0 7.2 %copy-start.17 = (bf16[256,512]{1,0:T(8,128)(2,1)S(1)}, bf16[256,512]{1,0:T(8,128)(2,1)}, u32[]{:S(2)}) copy-start(bf16[256,512]{1,0:T(8,128)(2,1)} %copy-done.16) | copy-start | bytes 786436
  58.9 4.2 %copy-start.3 = (f32[256,512]{1,0:T(8,128)S(1)}, f32[256,512]{1,0:T(8,128)}, u32[]{:S(2)}) copy-start(f32[256,512]{1,0:T(8,128)} %copy-done.2) | copy-start | bytes 1572868
  58.9 4.2 %copy-start.5 = (f32[256,512]{1,0:T(8,128)S(1)}, f32[256,512]{1,0:T(8,128)}, u32[]{:S(2)}) copy-start(f32[256,512]{1,0:T(8,128)} %param.27) | copy-start | bytes 1572868
  61.9 2.3 %copy-start.1 = (f32[512,512]{1,0:T(8,128)S(1)}, f32[512,512]{1,0:T(8,128)}, u32[]{:S(2)}) copy-start(f32[512,512]{1,0:T(8,128)} %copy-done) | copy-start | bytes 3145732
  67.9 17.9 %collective-permute-start.16 = (f32[2,2,2,64,256]{4,3,2,1,0:T(8,128)S(1)}, f32[2,2,2,64,256]{4,3,2,1,0:T(8,128)S(1)}, u32[]{:S(2)}, u32[]{:S(2)}) collective-permute-start(f32[2,2,2,64,256]{4,3,2,1,0:T(8,128)S(1)} %bitcast.251), channel_id=1, source_target_pairs={{0,4},{4,0},{8,12},{12,8},{16,20},{20,16},{24,28},{28,24},{1,5},{5... | collective-permute-start | bytes 1572872 | tf_op jit(solution)/shard_map/cond/branch_3_fun/ppermute | solution.py:229
  69.5 16.4 %collective-permute-start.17 = (f32[2,2,2,64,256]{4,3,2,1,0:T(8,128)S(1)}, f32[2,2,2,64,256]{4,3,2,1,0:T(8,128)S(1)}, u32[]{:S(2)}, u32[]{:S(2)}) collective-permute-start(f32[2,2,2,64,256]{4,3,2,1,0:T(8,128)S(1)} %bitcast.244), channel_id=1, source_target_pairs={{0,2},{1,3},{2,0},{3,1},{4,6},{5,7},{6,4},{7,5},{8,10},{9,11},{10,... | collective-permute-start | bytes 1572872 | tf_op jit(solution)/shard_map/cond/branch_3_fun/ppermute | solution.py:229
  71.1 14.7 %collective-permute-start.18 = (bf16[256,512]{1,0:T(8,128)(2,1)S(1)}, bf16[256,512]{1,0:T(8,128)(2,1)S(1)}, u32[]{:S(2)}, u32[]{:S(2)}) collective-permute-start(bf16[256,512]{1,0:T(8,128)(2,1)S(1)} %get-tuple-element.93), channel_id=1, source_target_pairs={{0,16},{4,20},{8,24},{12,28},{16,0},{20,4},{24,8},{28,12},{1,17},{... | collective-permute-start | bytes 786440 | tf_op jit(solution)/shard_map/cond/branch_3_fun/ppermute | solution.py:230
  86.1 7.4 %collective-permute-start.34 = (f32[2,2,64,256]{3,2,0,1:T(8,128)S(1)}, f32[2,2,64,256]{3,2,0,1:T(8,128)S(1)}, u32[]{:S(2)}, u32[]{:S(2)}) collective-permute-start(f32[2,2,64,256]{3,2,0,1:T(8,128)S(1)} %dynamic-slice_bitcast_fusion.2), channel_id=1, source_target_pairs={{0,4},{4,0},{8,12},{12,8},{16,20},{20,16},{24,28},{28,24},{1,5},{5... | collective-permute-start | bytes 786440 | tf_op jit(solution)/shard_map/ppermute | solution.py:167
  86.8 7.2 %collective-permute-start.31 = (f32[2,2,64,256]{3,2,0,1:T(8,128)S(1)}, f32[2,2,64,256]{3,2,0,1:T(8,128)S(1)}, u32[]{:S(2)}, u32[]{:S(2)}) collective-permute-start(f32[2,2,64,256]{3,2,0,1:T(8,128)S(1)} %dynamic-slice_bitcast_fusion.3), channel_id=1, source_target_pairs={{0,8},{4,12},{8,0},{12,4},{16,24},{20,28},{24,16},{28,20},{1,9},{5... | collective-permute-start | bytes 786440 | tf_op jit(solution)/shard_map/ppermute | solution.py:167
  93.6 5.7 %collective-permute-start.35 = (f32[2,64,256]{2,1,0:T(8,128)S(1)}, f32[2,64,256]{2,1,0:T(8,128)S(1)}, u32[]{:S(2)}, u32[]{:S(2)}) collective-permute-start(f32[2,64,256]{2,1,0:T(8,128)S(1)} %dynamic-slice_bitcast_fusion.4), channel_id=1, source_target_pairs={{0,8},{4,12},{8,0},{12,4},{16,24},{20,28},{24,16},{28,20},{1,9},{5... | collective-permute-start | bytes 393224 | tf_op jit(solution)/shard_map/ppermute | solution.py:167
  94.0 29.1 %copy-start.11 = (f32[256,512]{1,0:T(8,128)S(1)}, f32[256,512]{1,0:T(8,128)}, u32[]{:S(2)}) copy-start(f32[256,512]{1,0:T(8,128)} %get-tuple-element.191) | copy-start | bytes 1572868
  94.0 9.3 %collective-permute-start.32 = (f32[2,64,256]{2,1,0:T(8,128)S(1)}, f32[2,64,256]{2,1,0:T(8,128)S(1)}, u32[]{:S(2)}, u32[]{:S(2)}) collective-permute-start(f32[2,64,256]{2,1,0:T(8,128)S(1)} %dynamic-slice_bitcast_fusion.5), channel_id=1, source_target_pairs={{0,16},{4,20},{8,24},{12,28},{16,0},{20,4},{24,8},{28,12},{1,17},{... | collective-permute-start | bytes 393224 | tf_op jit(solution)/shard_map/ppermute | solution.py:167
  99.4 5.7 %collective-permute-start.36 = (f32[64,256]{1,0:T(8,128)S(1)}, f32[64,256]{1,0:T(8,128)S(1)}, u32[]{:S(2)}, u32[]{:S(2)}) collective-permute-start(f32[64,256]{1,0:T(8,128)S(1)} %dynamic-slice_bitcast_fusion.6), channel_id=1, source_target_pairs={{0,16},{4,20},{8,24},{12,28},{16,0},{20,4},{24,8},{28,12},{1,17},{... | collective-permute-start | bytes 196616 | tf_op jit(solution)/shard_map/ppermute | solution.py:167
  103.4 4.3 %collective-permute-start.33 = (f32[64,256]{1,0:T(8,128)S(1)}, f32[64,256]{1,0:T(8,128)S(1)}, u32[]{:S(2)}, u32[]{:S(2)}) collective-permute-start(f32[64,256]{1,0:T(8,128)S(1)} %dynamic-slice_bitcast_fusion.7), channel_id=1, source_target_pairs={{0,2},{1,3},{2,0},{3,1},{4,6},{5,7},{6,4},{7,5},{8,10},{9,11},{10,... | collective-permute-start | bytes 196616 | tf_op jit(solution)/shard_map/ppermute | solution.py:167
  107.8 6.9 %collective-permute-start.37 = (f32[64,512]{1,0:T(8,128)S(1)}, f32[64,512]{1,0:T(8,128)S(1)}, u32[]{:S(2)}, u32[]{:S(2)}) collective-permute-start(f32[64,512]{1,0:T(8,128)S(1)} %get-tuple-element.158), channel_id=1, source_target_pairs={{0,16},{4,20},{8,24},{12,28},{16,0},{20,4},{24,8},{28,12},{1,17},{... | collective-permute-start | bytes 393224 | tf_op jit(solution)/shard_map/ppermute | solution.py:177
  114.7 6.4 %collective-permute-start.38 = (f32[2,64,512]{2,1,0:T(8,128)S(1)}, f32[2,64,512]{2,1,0:T(8,128)S(1)}, u32[]{:S(2)}, u32[]{:S(2)}) collective-permute-start(f32[2,64,512]{2,1,0:T(8,128)S(1)} %maximum_select_fusion.2), channel_id=1, source_target_pairs={{0,8},{4,12},{8,0},{12,4},{16,24},{20,28},{24,16},{28,20},{1,9},{5... | collective-permute-start | bytes 786440 | tf_op jit(solution)/shard_map/ppermute | solution.py:177
  121.2 9.2 %collective-permute-start.39 = (f32[2,2,64,512]{3,2,0,1:T(8,128)S(1)}, f32[2,2,64,512]{3,2,0,1:T(8,128)S(1)}, u32[]{:S(2)}, u32[]{:S(2)}) collective-permute-start(f32[2,2,64,512]{3,2,0,1:T(8,128)S(1)} %maximum_select_fusion.1), channel_id=1, source_target_pairs={{0,4},{4,0},{8,12},{12,8},{16,20},{20,16},{24,28},{28,24},{1,5},{5... | collective-permute-start | bytes 1572872 | tf_op jit(solution)/shard_map/ppermute | solution.py:177
  (3 other events, 2.3 us)

commit v5 on v1

--- a/solution.py
+++ b/solution.py
@@ -199,7 +199,7 @@
     rel_steps = [("rel", bit) for bit in rest]
     bucket_steps = [("bucket", bit) for bit in bucket_bits]
     streams = [
-        (bucket_steps + rel_steps, bucket_bits[::-1]),
+        (bucket_steps[:2] + rel_steps + bucket_steps[2:], bucket_bits[::-1]),
         (rel_steps + bucket_steps, bucket_bits[:1] + bucket_bits[1:][::-1]),
     ]
     band = width // len(streams)

time: 119 us -> 123 us (1.034); the launches traced: 121 us -> 122 us
  starting transfers between devices: 16.5 us -> 38.3 us
  waiting for transfers between devices: 61.9 us -> 41.8 us
    ppermute x6, starting transfers between devices: 4.35 us -> 17.3 us  [halving_steps(): got = lax.ppermute(send, name, [(k, k ^ bit) for k in range(count)])]
    ppermute x6, waiting for transfers between devices: 14.1 us -> 5 us  [halving_steps(): got = lax.ppermute(send, name, [(k, k ^ bit) for k in range(count)])]
    ppermute x1, waiting for transfers between devices: 14.6 us -> 7.29 us  [run(): return (lax.ppermute(low_part, 'bucket', pairs),) + tuple(moved)]
    ppermute x2, waiting for transfers between devices: 0.01 us -> 5.93 us  [run(): moved.append(lax.ppermute(part, name, [(k, k ^ bit) for k in range(size)]))]
    ppermute x1, waiting for transfers between devices: 12.7 us -> 7 us  [run(): return tuple((lax.ppermute(array, 'bucket', pairs) for array in arrays))]
    ppermute x6, waiting for transfers between devices: 16.8 us -> 12.9 us  [doubling_steps(): got = lax.ppermute(current, name, [(k, k ^ bit) for k in range(count)])]
    ppermute x1, starting transfers between devices: 0.01 us -> 3.59 us  [run(): return (lax.ppermute(low_part, 'bucket', pairs),) + tuple(moved)]
    ppermute x6, starting transfers between devices: 2.9 us -> 6.35 us  [doubling_steps(): got = lax.ppermute(current, name, [(k, k ^ bit) for k in range(count)])]
  transfers between devices with their start and end apart: 19 -> 19, of which waited for: 16 -> 14; matrix products, arithmetic and copies ran while one was open for 15% -> 14% of each run, Pallas kernels for 0% -> 0%
where the time goes in v5:
time: 123 us; the launch traced here: 122 us
  waiting for transfers between devices  41.8 us (34%)
  starting transfers between devices  38.3 us (31%)
  other arithmetic  18.9 us (15%)
  matrix products  15.4 us (13%)
  local copies, waits for them, and re-layouts  5.6 us (5%)
  between operations  2.16 us (2%)
    ppermute x6, starting transfers between devices, halving_steps(): got = lax.ppermute(send, name, [(k, k ^ bit) for k in range(count)])  17.3 us
    ppermute x6, waiting for transfers between devices, doubling_steps(): got = lax.ppermute(current, name, [(k, k ^ bit) for k in range(count)])  12.9 us
    ppermute x1, waiting for transfers between devices, run(): return (lax.ppermute(low_part, 'bucket', pairs),) + tuple(moved)  7.29 us
    ppermute x1, waiting for transfers between devices, run(): return tuple((lax.ppermute(array, 'bucket', pairs) for array in arrays))  7 us
    ppermute x6, starting transfers between devices, doubling_steps(): got = lax.ppermute(current, name, [(k, k ^ bit) for k in range(count)])  6.35 us
    ppermute x2, waiting for transfers between devices, run(): moved.append(lax.ppermute(part, name, [(k, k ^ bit) for k in range(size)]))  5.93 us
    ppermute x6, waiting for transfers between devices, halving_steps(): got = lax.ppermute(send, name, [(k, k ^ bit) for k in range(count)])  5 us
    ppermute x1, starting transfers between devices, run(): return tuple((lax.ppermute(array, 'bucket', pairs) for array in arrays))  4.81 us
  transfers between devices with their start and end apart: 19, of which 14 were waited for; matrix products, arithmetic and copies ran while one was open for 14% of the time, Pallas kernels for 0%

profile of v5, /device:TPU:0, one launch (start us, length us, event | category | flops | bytes accessed | tf_op | source)
XLA Modules:
  0.0 122.2 jit_solution(15825973728266122905)
XLA Ops:
  0.6 3.1 %collective-permute-start.28 = (bf16[1,1,512,512]{3,2,1,0:T(8,128)(2,1)}, bf16[1,1,512,512]{3,2,1,0:T(8,128)(2,1)S(1)}, u32[]{:S(2)}, u32[]{:S(2)}) collective-permute-start(bf16[1,1,512,512]{3,2,1,0:T(8,128)(2,1)} %bitcast.286), channel_id=1, source_target_pairs={{0,2},{1,3},{2,0},{3,1},{4,6},{5,7},{6,4},{7,5},{8,10},{9,11},{10,... | collective-permute-start | bytes 1572872 | tf_op jit(solution)/shard_map/ppermute | solution.py:125
  4.5 1.4 %fusion.58 = (s32[1,1,1]{2,1,0:T(1,128)}, s32[1,1,1]{2,1,0:T(1,128)}, s32[1,1,1]{2,1,0:T(1,128)}, s32[1,1,1]{2,1,0:T(1,128)}) fusion(s32[1,1,4]{2,1,0:T(1,128)} %param.32), kind=kLoop, calls=%fused_computation.185 | loop fusion | bytes 32 | tf_op jit(solution)/shard_map/slice | solution.py:142
  6.6 1.9 %compare_bitcast_fusion.2 = (pred[2]{0:T(512)(128)(4,1)S(1)}, pred[2]{0:T(512)(128)(4,1)S(1)}, pred[2]{0:T(512)(128)(4,1)S(1)}) fusion(s32[2,1,1]{0,2,1:T(1,128)S(1)} %get-tuple-element.168, s32[]{:T(128)} %bitcast.41, s32[]{:T(128)} %bitcast.45, s32[]{:T(128)} %bitcast.48), kind=kLoop, calls=%fused_computation.158 | loop fusion | flops 6 | bytes 26 | tf_op jit(solution)/shard_map/eq | solution.py:142
  8.7 1.8 %convert_element_type.123 = bf16[256,512]{1,0:T(8,128)(2,1)} convert(f32[256,512]{1,0:T(8,128)} %param.27) | non-fusion elementwise | flops 131072 | bytes 786432 | tf_op jit(solution)/shard_map/convert_element_type | solution.py:44
  10.5 1.1 convert_element_type.125
  12.3 1.9 %compare_bitcast_fusion.6 = (pred[2]{0:T(512)(128)(4,1)S(1)}, pred[2]{0:T(512)(128)(4,1)S(1)}, pred[2]{0:T(512)(128)(4,1)S(1)}) fusion(s32[2,1,1]{0,2,1:T(1,128)S(1)} %get-tuple-element.141, s32[]{:T(128)} %bitcast.41, s32[]{:T(128)} %bitcast.45, s32[]{:T(128)} %bitcast.48), kind=kLoop, calls=%fused_computation.162 | loop fusion | flops 6 | bytes 26 | tf_op jit(solution)/shard_map/eq | solution.py:142
  14.4 1.5 %collective-permute-done.28 = bf16[1,1,512,512]{3,2,1,0:T(8,128)(2,1)S(1)} collective-permute-done((bf16[1,1,512,512]{3,2,1,0:T(8,128)(2,1)}, bf16[1,1,512,512]{3,2,1,0:T(8,128)(2,1)S(1)}, u32[]{:S(2)}, u32[]{:S(2)}) %collective-permute-start.28) | collective-permute-done | bytes 524320 | tf_op jit(solution)/shard_map/ppermute | solution.py:125
  16.3 2.3 %collective-permute-done.29 = bf16[2,1,512,512]{3,2,0,1:T(8,128)(2,1)S(1)} collective-permute-done((bf16[2,1,512,512]{3,2,0,1:T(8,128)(2,1)S(1)}, bf16[2,1,512,512]{3,2,0,1:T(8,128)(2,1)S(1)}, u32[]{:S(2)}, u32[]{:S(2)}) %collective-permute-start.29) | collective-permute-done | bytes 1048608 | tf_op jit(solution)/shard_map/ppermute | solution.py:125
  19.3 1.6 %gather_fusion = bf16[2,512,512]{2,1,0:T(8,128)(2,1)} fusion(bf16[4,512,512]{2,1,0:T(8,128)(2,1)S(1)} %bitcast.248, s32[1024]{0:T(1024)S(1)} %pad_clamp_fusion.1), kind=kCustom, calls=%fused_computation.clone | custom fusion | bytes 2097160 | tf_op jit(solution)/shard_map/jit(_take)/gather | solution.py:270
  20.9 1.5 %broadcast_select_fusion = (bf16[2,512,512]{2,1,0:T(8,128)(2,1)S(1)}, bf16[2,512,512]{2,1,0:T(8,128)(2,1)S(1)}) fusion(bf16[2,512,512]{2,1,0:T(8,128)(2,1)S(1)} %gather_fusion.1, pred[2]{0:T(512)(128)(4,1)S(1)} %get-tuple-element.146, bf16[2,512,512]{2,1,0:T(8,128)(2,1)} %gather_fusion, pred[2]{0:T(512)(128)(4,1)S(1)} %get-tuple-element.179), kind=kLoop, calls=%fused_computation.61 | loop fusion | flops 1048576 | bytes 4194308 | tf_op jit(solution)/shard_map/jit(_take)/select_n | solution.py:270
  26.5 1.0 convolution_convert_fusion.3
  27.5 1.0 convolution_convert_fusion.1
  29.6 0.9 fusion.20
  30.5 11.8 %conditional.4 = (bf16[257,512]{1,0:T(8,128)(2,1)}) conditional(s32[]{:T(128)} %bitcast.31, bf16[257,512]{1,0:T(8,128)(2,1)S(1)} %maximum_maximum_fusion, bf16[257,512]{1,0:T(8,128)(2,1)S(1)} %maximum_maximum_fusion, bf16[257,512]{1,0:T(8,128)(2,1)S(1)} %maximum_maximum_fusion, ...), branch_computations={%region_2.4_spmd, %region_3.5_spmd, %region_4.6_spmd, %region_5.7_... | conditional | bytes 1052720 | solution.py:85
  30.5 4.8 %collective-permute-start.6 = (bf16[257,512]{1,0:T(8,128)(2,1)S(1)}, bf16[257,512]{1,0:T(8,128)(2,1)}, u32[]{:S(2)}, u32[]{:S(2)}) collective-permute-start(bf16[257,512]{1,0:T(8,128)(2,1)S(1)} %param.8), channel_id=1, source_target_pairs={{0,28},{4,24},{8,20},{12,16},{16,12},{20,8},{24,4},{28,0},{1,29},{... | collective-permute-start | bytes 789512 | tf_op jit(solution)/shard_map/cond/branch_6_fun/ppermute | solution.py:80
  35.3 7.0 %collective-permute-done.6 = bf16[257,512]{1,0:T(8,128)(2,1)} collective-permute-done((bf16[257,512]{1,0:T(8,128)(2,1)S(1)}, bf16[257,512]{1,0:T(8,128)(2,1)}, u32[]{:S(2)}, u32[]{:S(2)}) %collective-permute-start.6) | collective-permute-done | bytes 263200 | tf_op jit(solution)/shard_map/cond/branch_6_fun/ppermute | solution.py:80
  42.3 1.3 %fusion.7 = f32[256,256]{1,0:T(8,128)S(1)} fusion(bf16[256,512]{1,0:T(8,128)(2,1)} %convolution_convert_fusion.3, bf16[257,512]{1,0:T(8,128)(2,1)} %get-tuple-element.212), kind=kOutput, calls=%fused_computation.41 | convolution fusion | flops 67305472 | bytes 786432 | tf_op jit(solution)/shard_map/dot_general | solution.py:54
  44.2 1.2 convolution_convert_fusion.2
  45.4 1.2 %fusion.3 = f32[256,256]{1,0:T(8,128)S(1)} fusion(bf16[256,512]{1,0:T(8,128)(2,1)S(1)} %copy-done.7, bf16[257,512]{1,0:T(8,128)(2,1)} %get-tuple-element.212), kind=kOutput, calls=%fused_computation.35 | convolution fusion | flops 67305472 | bytes 786432 | tf_op jit(solution)/shard_map/dot_general | solution.py:54
  47.2 1.2 convolution_convert_fusion
  50.7 1.1 multiply_reduce_fusion
  53.7 1.0 divide_subtract_fusion.1
  54.7 0.8 add_add_fusion
  56.7 20.1 %conditional.5 = (f32[256,512]{1,0:T(8,128)S(1)}, f32[2,2,2,64,256]{4,3,0,2,1:T(8,128)S(1)}, f32[2,2,2,64,256]{4,3,0,1,2:T(8,128)S(1)}) conditional(s32[]{:T(128)} %bitcast.31, (f32[1,2,2,2,64,256]{5,4,0,1,3,2:T(8,128)S(1)}, f32[1,2,2,2,64,256]{5,4,1,2,3,0:T(8,128)S(1)}, bf16[256,512]{1,0:T(8,128)(2,1)S(1)}) %tuple.164, ...), branch_computations={%region_10.12_spmd, %region_11.13_spmd, %region_12.14_spmd, %regio... | conditional | flops 131072 | bytes 10223760
  56.8 1.4 %collective-permute-start.25 = (f32[2,2,2,64,256]{4,3,2,1,0:T(8,128)S(1)}, f32[2,2,2,64,256]{4,3,2,1,0:T(8,128)S(1)}, u32[]{:S(2)}, u32[]{:S(2)}) collective-permute-start(f32[2,2,2,64,256]{4,3,2,1,0:T(8,128)S(1)} %bitcast.283), channel_id=1, source_target_pairs={{0,4},{4,0},{8,12},{12,8},{16,20},{20,16},{24,28},{28,24},{1,5},{5... | collective-permute-start | bytes 1572872 | tf_op jit(solution)/shard_map/cond/branch_6_fun/ppermute | solution.py:229
  58.3 1.6 %collective-permute-start.26 = (f32[2,2,2,64,256]{4,3,2,1,0:T(8,128)S(1)}, f32[2,2,2,64,256]{4,3,2,1,0:T(8,128)S(1)}, u32[]{:S(2)}, u32[]{:S(2)}) collective-permute-start(f32[2,2,2,64,256]{4,3,2,1,0:T(8,128)S(1)} %bitcast.276), channel_id=1, source_target_pairs={{0,2},{1,3},{2,0},{3,1},{4,6},{5,7},{6,4},{7,5},{8,10},{9,11},{10,... | collective-permute-start | bytes 1572872 | tf_op jit(solution)/shard_map/cond/branch_6_fun/ppermute | solution.py:229
  59.9 3.6 %collective-permute-start.27 = (bf16[256,512]{1,0:T(8,128)(2,1)S(1)}, bf16[256,512]{1,0:T(8,128)(2,1)S(1)}, u32[]{:S(2)}, u32[]{:S(2)}) collective-permute-start(bf16[256,512]{1,0:T(8,128)(2,1)S(1)} %get-tuple-element.102), channel_id=1, source_target_pairs={{0,28},{4,24},{8,20},{12,16},{16,12},{20,8},{24,4},{28,0},{1,29},{... | collective-permute-start | bytes 786440 | tf_op jit(solution)/shard_map/cond/branch_6_fun/ppermute | solution.py:230
  63.4 7.3 %collective-permute-done.27 = bf16[256,512]{1,0:T(8,128)(2,1)S(1)} collective-permute-done((bf16[256,512]{1,0:T(8,128)(2,1)S(1)}, bf16[256,512]{1,0:T(8,128)(2,1)S(1)}, u32[]{:S(2)}, u32[]{:S(2)}) %collective-permute-start.27) | collective-permute-done | bytes 262176 | tf_op jit(solution)/shard_map/cond/branch_6_fun/ppermute | solution.py:230
  70.8 5.9 %collective-permute-done.25 = f32[2,2,2,64,256]{4,3,2,1,0:T(8,128)S(1)} collective-permute-done((f32[2,2,2,64,256]{4,3,2,1,0:T(8,128)S(1)}, f32[2,2,2,64,256]{4,3,2,1,0:T(8,128)S(1)}, u32[]{:S(2)}, u32[]{:S(2)}) %collective-permute-start.25) | collective-permute-done | bytes 524320 | tf_op jit(solution)/shard_map/cond/branch_6_fun/ppermute | solution.py:229
  76.9 1.5 %collective-permute-start.37 = (f32[2,2,64,256]{3,2,0,1:T(8,128)S(1)}, f32[2,2,64,256]{3,2,0,1:T(8,128)S(1)}, u32[]{:S(2)}, u32[]{:S(2)}) collective-permute-start(f32[2,2,64,256]{3,2,0,1:T(8,128)S(1)} %dynamic-slice_bitcast_fusion.2), channel_id=1, source_target_pairs={{0,4},{4,0},{8,12},{12,8},{16,20},{20,16},{24,28},{28,24},{1,5},{5... | collective-permute-start | bytes 786440 | tf_op jit(solution)/shard_map/ppermute | solution.py:167
  78.5 5.5 %collective-permute-start.31 = (f32[2,2,64,256]{3,2,1,0:T(8,128)S(1)}, f32[2,2,64,256]{3,2,1,0:T(8,128)S(1)}, u32[]{:S(2)}, u32[]{:S(2)}) collective-permute-start(f32[2,2,64,256]{3,2,1,0:T(8,128)S(1)} %dynamic-slice_bitcast_fusion.3), channel_id=1, source_target_pairs={{0,8},{4,12},{8,0},{12,4},{16,24},{20,28},{24,16},{28,20},{1,9},{5... | collective-permute-start | bytes 786440 | tf_op jit(solution)/shard_map/ppermute | solution.py:167
  84.0 1.9 %divide_subtract_fusion = f32[256,512]{1,0:T(8,128)} fusion(f32[256,512]{1,0:T(8,128)S(1)} %copy-done.4, f32[256,512]{1,0:T(8,128)S(1)} %get-tuple-element.114, f32[256]{0:T(256)S(1)} %get-tuple-element.138, bf16[257,512]{1,0:T(8,128)(2,1)} %get-tuple-element.212), kind=kLoop, calls=%fused_computation.76 | loop fusion | flops 655360 | bytes 1836032 | tf_op jit(solution)/shard_map/sub | solution.py:28
  86.0 4.3 %collective-permute-start.38 = (f32[2,64,256]{2,1,0:T(8,128)S(1)}, f32[2,64,256]{2,1,0:T(8,128)S(1)}, u32[]{:S(2)}, u32[]{:S(2)}) collective-permute-start(f32[2,64,256]{2,1,0:T(8,128)S(1)} %dynamic-slice_bitcast_fusion.4), channel_id=1, source_target_pairs={{0,8},{4,12},{8,0},{12,4},{16,24},{20,28},{24,16},{28,20},{1,9},{5... | collective-permute-start | bytes 393224 | tf_op jit(solution)/shard_map/ppermute | solution.py:167
  90.3 1.6 %collective-permute-start.32 = (f32[2,64,256]{2,1,0:T(8,128)S(1)}, f32[2,64,256]{2,1,0:T(8,128)S(1)}, u32[]{:S(2)}, u32[]{:S(2)}) collective-permute-start(f32[2,64,256]{2,1,0:T(8,128)S(1)} %dynamic-slice_bitcast_fusion.5), channel_id=1, source_target_pairs={{0,2},{1,3},{2,0},{3,1},{4,6},{5,7},{6,4},{7,5},{8,10},{9,11},{10,... | collective-permute-start | bytes 393224 | tf_op jit(solution)/shard_map/ppermute | solution.py:167
  91.9 1.3 %collective-permute-done.38 = f32[2,64,256]{2,1,0:T(8,128)S(1)} collective-permute-done((f32[2,64,256]{2,1,0:T(8,128)S(1)}, f32[2,64,256]{2,1,0:T(8,128)S(1)}, u32[]{:S(2)}, u32[]{:S(2)}) %collective-permute-start.38) | collective-permute-done | bytes 131104 | tf_op jit(solution)/shard_map/ppermute | solution.py:167
  93.3 3.1 %collective-permute-start.39 = (f32[64,256]{1,0:T(8,128)S(1)}, f32[64,256]{1,0:T(8,128)S(1)}, u32[]{:S(2)}, u32[]{:S(2)}) collective-permute-start(f32[64,256]{1,0:T(8,128)S(1)} %dynamic-slice_bitcast_fusion.6), channel_id=1, source_target_pairs={{0,16},{4,20},{8,24},{12,28},{16,0},{20,4},{24,8},{28,12},{1,17},{... | collective-permute-start | bytes 196616 | tf_op jit(solution)/shard_map/ppermute | solution.py:167
  96.4 1.3 %collective-permute-start.33 = (f32[64,256]{1,0:T(8,128)S(1)}, f32[64,256]{1,0:T(8,128)S(1)}, u32[]{:S(2)}, u32[]{:S(2)}) collective-permute-start(f32[64,256]{1,0:T(8,128)S(1)} %dynamic-slice_bitcast_fusion.7), channel_id=1, source_target_pairs={{0,16},{4,20},{8,24},{12,28},{16,0},{20,4},{24,8},{28,12},{1,17},{... | collective-permute-start | bytes 196616 | tf_op jit(solution)/shard_map/ppermute | solution.py:167
  97.7 1.6 %collective-permute-done.39 = f32[64,256]{1,0:T(8,128)S(1)} collective-permute-done((f32[64,256]{1,0:T(8,128)S(1)}, f32[64,256]{1,0:T(8,128)S(1)}, u32[]{:S(2)}, u32[]{:S(2)}) %collective-permute-start.39) | collective-permute-done | bytes 65568 | tf_op jit(solution)/shard_map/ppermute | solution.py:167
  99.4 1.3 %collective-permute-start.40 = (f32[64,256]{1,0:T(8,128)S(1)}, f32[64,256]{1,0:T(8,128)S(1)}, u32[]{:S(2)}, u32[]{:S(2)}) collective-permute-start(f32[64,256]{1,0:T(8,128)S(1)} %bitcast_add_fusion.6), channel_id=1, source_target_pairs={{0,4},{4,0},{8,12},{12,8},{16,20},{20,16},{24,28},{28,24},{1,5},{5... | collective-permute-start | bytes 196616 | tf_op jit(solution)/shard_map/ppermute | solution.py:177
  100.6 2.1 %collective-permute-done.33 = f32[64,256]{1,0:T(8,128)S(1)} collective-permute-done((f32[64,256]{1,0:T(8,128)S(1)}, f32[64,256]{1,0:T(8,128)S(1)}, u32[]{:S(2)}, u32[]{:S(2)}) %collective-permute-start.33) | collective-permute-done | bytes 65568 | tf_op jit(solution)/shard_map/ppermute | solution.py:167
  103.7 2.2 %collective-permute-start.41 = (f32[2,64,256]{2,1,0:T(8,128)S(1)}, f32[2,64,256]{2,1,0:T(8,128)S(1)}, u32[]{:S(2)}, u32[]{:S(2)}) collective-permute-start(f32[2,64,256]{2,1,0:T(8,128)S(1)} %maximum_select_fusion.6), channel_id=1, source_target_pairs={{0,16},{4,20},{8,24},{12,28},{16,0},{20,4},{24,8},{28,12},{1,17},{... | collective-permute-start | bytes 393224 | tf_op jit(solution)/shard_map/ppermute | solution.py:177
  106.0 2.1 %collective-permute-done.34 = f32[64,256]{1,0:T(8,128)S(1)} collective-permute-done((f32[64,256]{1,0:T(8,128)S(1)}, f32[64,256]{1,0:T(8,128)S(1)}, u32[]{:S(2)}, u32[]{:S(2)}) %collective-permute-start.34) | collective-permute-done | bytes 65568 | tf_op jit(solution)/shard_map/ppermute | solution.py:177
  108.3 2.3 %collective-permute-done.41 = f32[2,64,256]{2,1,0:T(8,128)S(1)} collective-permute-done((f32[2,64,256]{2,1,0:T(8,128)S(1)}, f32[2,64,256]{2,1,0:T(8,128)S(1)}, u32[]{:S(2)}, u32[]{:S(2)}) %collective-permute-start.41) | collective-permute-done | bytes 131104 | tf_op jit(solution)/shard_map/ppermute | solution.py:177
  110.6 1.6 %collective-permute-start.42 = (f32[2,2,64,256]{3,2,1,0:T(8,128)S(1)}, f32[2,2,64,256]{3,2,1,0:T(8,128)S(1)}, u32[]{:S(2)}, u32[]{:S(2)}) collective-permute-start(f32[2,2,64,256]{3,2,1,0:T(8,128)S(1)} %maximum_select_fusion.3), channel_id=1, source_target_pairs={{0,8},{4,12},{8,0},{12,4},{16,24},{20,28},{24,16},{28,20},{1,9},{5... | collective-permute-start | bytes 786440 | tf_op jit(solution)/shard_map/ppermute | solution.py:177
  112.2 2.4 %collective-permute-done.35 = f32[2,64,256]{2,1,0:T(8,128)S(1)} collective-permute-done((f32[2,64,256]{2,1,0:T(8,128)S(1)}, f32[2,64,256]{2,1,0:T(8,128)S(1)}, u32[]{:S(2)}, u32[]{:S(2)}) %collective-permute-start.35) | collective-permute-done | bytes 131104 | tf_op jit(solution)/shard_map/ppermute | solution.py:177
  115.5 2.5 %collective-permute-done.42 = f32[2,2,64,256]{3,2,1,0:T(8,128)S(1)} collective-permute-done((f32[2,2,64,256]{3,2,1,0:T(8,128)S(1)}, f32[2,2,64,256]{3,2,1,0:T(8,128)S(1)}, u32[]{:S(2)}, u32[]{:S(2)}) %collective-permute-start.42) | collective-permute-done | bytes 262176 | tf_op jit(solution)/shard_map/ppermute | solution.py:177
  118.0 3.1 %collective-permute-done.36 = f32[2,2,64,256]{3,2,0,1:T(8,128)S(1)} collective-permute-done((f32[2,2,64,256]{3,2,0,1:T(8,128)S(1)}, f32[2,2,64,256]{3,2,0,1:T(8,128)S(1)}, u32[]{:S(2)}, u32[]{:S(2)}) %collective-permute-start.36) | collective-permute-done | bytes 262176 | tf_op jit(solution)/shard_map/ppermute | solution.py:177
  121.1 1.1 maximum_bitcast_fusion
  (125 shorter events, 16.7 us)
Async XLA Ops:
  0.6 13.7 %copy-start.6 = (bf16[1,512,512]{2,1,0:T(8,128)(2,1)S(1)}, bf16[1,512,512]{2,1,0:T(8,128)(2,1)}, u32[]{:S(2)}) copy-start(bf16[1,512,512]{2,1,0:T(8,128)(2,1)} %param.31) | copy-start | bytes 1572868
  0.6 15.2 %collective-permute-start.28 = (bf16[1,1,512,512]{3,2,1,0:T(8,128)(2,1)}, bf16[1,1,512,512]{3,2,1,0:T(8,128)(2,1)S(1)}, u32[]{:S(2)}, u32[]{:S(2)}) collective-permute-start(bf16[1,1,512,512]{3,2,1,0:T(8,128)(2,1)} %bitcast.286), channel_id=1, source_target_pairs={{0,2},{1,3},{2,0},{3,1},{4,6},{5,7},{6,4},{7,5},{8,10},{9,11},{10,... | collective-permute-start | bytes 1572872 | tf_op jit(solution)/shard_map/ppermute | solution.py:125
  10.4 5.5 %copy-start.11 = (s32[1,1,2,512]{3,2,1,0:T(2,128)S(1)}, s32[1,1,2,512]{3,2,1,0:T(2,128)}, u32[]{:S(2)}) copy-start(s32[1,1,2,512]{3,2,1,0:T(2,128)} %param.34) | copy-start | bytes 12292
  10.4 5.6 %copy-start.12 = (s32[1,1,2,512]{3,2,1,0:T(2,128)S(1)}, s32[1,1,2,512]{3,2,1,0:T(2,128)}, u32[]{:S(2)}) copy-start(s32[1,1,2,512]{3,2,1,0:T(2,128)} %param.33) | copy-start | bytes 12292
  10.4 5.6 %copy-start.13 = (s32[1,1,2,512]{3,2,1,0:T(2,128)S(1)}, s32[1,1,2,512]{3,2,1,0:T(2,128)}, u32[]{:S(2)}) copy-start(s32[1,1,2,512]{3,2,1,0:T(2,128)} %param.36) | copy-start | bytes 12292
  10.4 5.6 %copy-start.14 = (s32[1,1,2,512]{3,2,1,0:T(2,128)S(1)}, s32[1,1,2,512]{3,2,1,0:T(2,128)}, u32[]{:S(2)}) copy-start(s32[1,1,2,512]{3,2,1,0:T(2,128)} %param.35) | copy-start | bytes 12292
  15.9 2.7 %collective-permute-start.29 = (bf16[2,1,512,512]{3,2,0,1:T(8,128)(2,1)S(1)}, bf16[2,1,512,512]{3,2,0,1:T(8,128)(2,1)S(1)}, u32[]{:S(2)}, u32[]{:S(2)}) collective-permute-start(bf16[2,1,512,512]{3,2,0,1:T(8,128)(2,1)S(1)} %bitcast.249), channel_id=1, source_target_pairs={{0,1},{1,0},{2,3},{3,2},{4,5},{5,4},{6,7},{7,6},{8,9},{9,8},{10,11... | collective-permute-start | bytes 3145736 | tf_op jit(solution)/shard_map/ppermute | solution.py:125
  20.9 1.5 %copy-start.3 = (bf16[256,512]{1,0:T(8,128)(2,1)S(1)}, bf16[256,512]{1,0:T(8,128)(2,1)}, u32[]{:S(2)}) copy-start(bf16[256,512]{1,0:T(8,128)(2,1)} %convert_element_type.123) | copy-start | bytes 786436
  22.4 5.0 %copy-start.1 = (bf16[2,512,512]{2,1,0:T(8,128)(2,1)}, bf16[2,512,512]{2,1,0:T(8,128)(2,1)S(1)}, u32[]{:S(2)}) copy-start(bf16[2,512,512]{2,1,0:T(8,128)(2,1)S(1)} %get-tuple-element.189) | copy-start | bytes 3145732
  25.1 1.2 copy-start.10
  25.1 1.2 copy-start
  28.5 1.1 copy-start.15
  28.5 1.1 copy-start.5
  30.5 11.8 %collective-permute-start.6 = (bf16[257,512]{1,0:T(8,128)(2,1)S(1)}, bf16[257,512]{1,0:T(8,128)(2,1)}, u32[]{:S(2)}, u32[]{:S(2)}) collective-permute-start(bf16[257,512]{1,0:T(8,128)(2,1)S(1)} %param.8), channel_id=1, source_target_pairs={{0,28},{4,24},{8,20},{12,16},{16,12},{20,8},{24,4},{28,0},{1,29},{... | collective-permute-start | bytes 789512 | tf_op jit(solution)/shard_map/cond/branch_6_fun/ppermute | solution.py:80
  42.3 3.1 %copy-start.7 = (bf16[256,512]{1,0:T(8,128)(2,1)S(1)}, bf16[256,512]{1,0:T(8,128)(2,1)}, u32[]{:S(2)}) copy-start(bf16[256,512]{1,0:T(8,128)(2,1)} %convolution_convert_fusion.1) | copy-start | bytes 786436
  49.0 1.5 %copy-start.8 = (bf16[256,512]{1,0:T(8,128)(2,1)S(1)}, bf16[256,512]{1,0:T(8,128)(2,1)}, u32[]{:S(2)}) copy-start(bf16[256,512]{1,0:T(8,128)(2,1)} %convolution_convert_fusion.3) | copy-start | bytes 786436
  49.6 2.7 %copy-start.2 = (bf16[2,512,512]{2,1,0:T(8,128)(2,1)S(1)}, bf16[2,512,512]{2,1,0:T(8,128)(2,1)}, u32[]{:S(2)}) copy-start(bf16[2,512,512]{2,1,0:T(8,128)(2,1)} %copy-done.1) | copy-start | bytes 3145732
  49.6 5.1 %collective-permute-start.30 = (f32[2,8,64,512]{3,2,1,0:T(8,128)S(1)}, f32[2,8,64,512]{3,2,1,0:T(8,128)S(1)}, u32[]{:S(2)}, u32[]{:S(2)}) collective-permute-start(f32[2,8,64,512]{3,2,1,0:T(8,128)S(1)} %select_add_fusion), channel_id=1, source_target_pairs={{0,1},{1,0},{2,3},{3,2},{4,5},{5,4},{6,7},{7,6},{8,9},{9,8},{10,11... | collective-permute-start | bytes 6291464 | tf_op jit(solution)/shard_map/ppermute | solution.py:209
  55.8 1.0 copy-start.9
  56.8 19.9 %collective-permute-start.25 = (f32[2,2,2,64,256]{4,3,2,1,0:T(8,128)S(1)}, f32[2,2,2,64,256]{4,3,2,1,0:T(8,128)S(1)}, u32[]{:S(2)}, u32[]{:S(2)}) collective-permute-start(f32[2,2,2,64,256]{4,3,2,1,0:T(8,128)S(1)} %bitcast.283), channel_id=1, source_target_pairs={{0,4},{4,0},{8,12},{12,8},{16,20},{20,16},{24,28},{28,24},{1,5},{5... | collective-permute-start | bytes 1572872 | tf_op jit(solution)/shard_map/cond/branch_6_fun/ppermute | solution.py:229
  58.3 18.5 %collective-permute-start.26 = (f32[2,2,2,64,256]{4,3,2,1,0:T(8,128)S(1)}, f32[2,2,2,64,256]{4,3,2,1,0:T(8,128)S(1)}, u32[]{:S(2)}, u32[]{:S(2)}) collective-permute-start(f32[2,2,2,64,256]{4,3,2,1,0:T(8,128)S(1)} %bitcast.276), channel_id=1, source_target_pairs={{0,2},{1,3},{2,0},{3,1},{4,6},{5,7},{6,4},{7,5},{8,10},{9,11},{10,... | collective-permute-start | bytes 1572872 | tf_op jit(solution)/shard_map/cond/branch_6_fun/ppermute | solution.py:229
  59.9 10.9 %collective-permute-start.27 = (bf16[256,512]{1,0:T(8,128)(2,1)S(1)}, bf16[256,512]{1,0:T(8,128)(2,1)S(1)}, u32[]{:S(2)}, u32[]{:S(2)}) collective-permute-start(bf16[256,512]{1,0:T(8,128)(2,1)S(1)} %get-tuple-element.102), channel_id=1, source_target_pairs={{0,28},{4,24},{8,20},{12,16},{16,12},{20,8},{24,4},{28,0},{1,29},{... | collective-permute-start | bytes 786440 | tf_op jit(solution)/shard_map/cond/branch_6_fun/ppermute | solution.py:230
  76.8 7.2 %copy-start.4 = (f32[256,512]{1,0:T(8,128)S(1)}, f32[256,512]{1,0:T(8,128)}, u32[]{:S(2)}) copy-start(f32[256,512]{1,0:T(8,128)} %get-tuple-element.188) | copy-start | bytes 1572868
  76.9 9.0 %collective-permute-start.37 = (f32[2,2,64,256]{3,2,0,1:T(8,128)S(1)}, f32[2,2,64,256]{3,2,0,1:T(8,128)S(1)}, u32[]{:S(2)}, u32[]{:S(2)}) collective-permute-start(f32[2,2,64,256]{3,2,0,1:T(8,128)S(1)} %dynamic-slice_bitcast_fusion.2), channel_id=1, source_target_pairs={{0,4},{4,0},{8,12},{12,8},{16,20},{20,16},{24,28},{28,24},{1,5},{5... | collective-permute-start | bytes 786440 | tf_op jit(solution)/shard_map/ppermute | solution.py:167
  78.5 11.8 %collective-permute-start.31 = (f32[2,2,64,256]{3,2,1,0:T(8,128)S(1)}, f32[2,2,64,256]{3,2,1,0:T(8,128)S(1)}, u32[]{:S(2)}, u32[]{:S(2)}) collective-permute-start(f32[2,2,64,256]{3,2,1,0:T(8,128)S(1)} %dynamic-slice_bitcast_fusion.3), channel_id=1, source_target_pairs={{0,8},{4,12},{8,0},{12,4},{16,24},{20,28},{24,16},{28,20},{1,9},{5... | collective-permute-start | bytes 786440 | tf_op jit(solution)/shard_map/ppermute | solution.py:167
  86.0 7.2 %collective-permute-start.38 = (f32[2,64,256]{2,1,0:T(8,128)S(1)}, f32[2,64,256]{2,1,0:T(8,128)S(1)}, u32[]{:S(2)}, u32[]{:S(2)}) collective-permute-start(f32[2,64,256]{2,1,0:T(8,128)S(1)} %dynamic-slice_bitcast_fusion.4), channel_id=1, source_target_pairs={{0,8},{4,12},{8,0},{12,4},{16,24},{20,28},{24,16},{28,20},{1,9},{5... | collective-permute-start | bytes 393224 | tf_op jit(solution)/shard_map/ppermute | solution.py:167
  90.3 6.0 %collective-permute-start.32 = (f32[2,64,256]{2,1,0:T(8,128)S(1)}, f32[2,64,256]{2,1,0:T(8,128)S(1)}, u32[]{:S(2)}, u32[]{:S(2)}) collective-permute-start(f32[2,64,256]{2,1,0:T(8,128)S(1)} %dynamic-slice_bitcast_fusion.5), channel_id=1, source_target_pairs={{0,2},{1,3},{2,0},{3,1},{4,6},{5,7},{6,4},{7,5},{8,10},{9,11},{10,... | collective-permute-start | bytes 393224 | tf_op jit(solution)/shard_map/ppermute | solution.py:167
  93.3 6.1 %collective-permute-start.39 = (f32[64,256]{1,0:T(8,128)S(1)}, f32[64,256]{1,0:T(8,128)S(1)}, u32[]{:S(2)}, u32[]{:S(2)}) collective-permute-start(f32[64,256]{1,0:T(8,128)S(1)} %dynamic-slice_bitcast_fusion.6), channel_id=1, source_target_pairs={{0,16},{4,20},{8,24},{12,28},{16,0},{20,4},{24,8},{28,12},{1,17},{... | collective-permute-start | bytes 196616 | tf_op jit(solution)/shard_map/ppermute | solution.py:167
  96.4 6.3 %collective-permute-start.33 = (f32[64,256]{1,0:T(8,128)S(1)}, f32[64,256]{1,0:T(8,128)S(1)}, u32[]{:S(2)}, u32[]{:S(2)}) collective-permute-start(f32[64,256]{1,0:T(8,128)S(1)} %dynamic-slice_bitcast_fusion.7), channel_id=1, source_target_pairs={{0,16},{4,20},{8,24},{12,28},{16,0},{20,4},{24,8},{28,12},{1,17},{... | collective-permute-start | bytes 196616 | tf_op jit(solution)/shard_map/ppermute | solution.py:167
  99.4 4.3 %collective-permute-start.40 = (f32[64,256]{1,0:T(8,128)S(1)}, f32[64,256]{1,0:T(8,128)S(1)}, u32[]{:S(2)}, u32[]{:S(2)}) collective-permute-start(f32[64,256]{1,0:T(8,128)S(1)} %bitcast_add_fusion.6), channel_id=1, source_target_pairs={{0,4},{4,0},{8,12},{12,8},{16,20},{20,16},{24,28},{28,24},{1,5},{5... | collective-permute-start | bytes 196616 | tf_op jit(solution)/shard_map/ppermute | solution.py:177
  102.8 5.4 %collective-permute-start.34 = (f32[64,256]{1,0:T(8,128)S(1)}, f32[64,256]{1,0:T(8,128)S(1)}, u32[]{:S(2)}, u32[]{:S(2)}) collective-permute-start(f32[64,256]{1,0:T(8,128)S(1)} %bitcast_add_fusion.7), channel_id=1, source_target_pairs={{0,16},{4,20},{8,24},{12,28},{16,0},{20,4},{24,8},{28,12},{1,17},{... | collective-permute-start | bytes 196616 | tf_op jit(solution)/shard_map/ppermute | solution.py:177
  103.7 6.8 %collective-permute-start.41 = (f32[2,64,256]{2,1,0:T(8,128)S(1)}, f32[2,64,256]{2,1,0:T(8,128)S(1)}, u32[]{:S(2)}, u32[]{:S(2)}) collective-permute-start(f32[2,64,256]{2,1,0:T(8,128)S(1)} %maximum_select_fusion.6), channel_id=1, source_target_pairs={{0,16},{4,20},{8,24},{12,28},{16,0},{20,4},{24,8},{28,12},{1,17},{... | collective-permute-start | bytes 393224 | tf_op jit(solution)/shard_map/ppermute | solution.py:177
  108.1 6.4 %collective-permute-start.35 = (f32[2,64,256]{2,1,0:T(8,128)S(1)}, f32[2,64,256]{2,1,0:T(8,128)S(1)}, u32[]{:S(2)}, u32[]{:S(2)}) collective-permute-start(f32[2,64,256]{2,1,0:T(8,128)S(1)} %maximum_select_fusion.4), channel_id=1, source_target_pairs={{0,8},{4,12},{8,0},{12,4},{16,24},{20,28},{24,16},{28,20},{1,9},{5... | collective-permute-start | bytes 393224 | tf_op jit(solution)/shard_map/ppermute | solution.py:177
  110.6 7.3 %collective-permute-start.42 = (f32[2,2,64,256]{3,2,1,0:T(8,128)S(1)}, f32[2,2,64,256]{3,2,1,0:T(8,128)S(1)}, u32[]{:S(2)}, u32[]{:S(2)}) collective-permute-start(f32[2,2,64,256]{3,2,1,0:T(8,128)S(1)} %maximum_select_fusion.3), channel_id=1, source_target_pairs={{0,8},{4,12},{8,0},{12,4},{16,24},{20,28},{24,16},{28,20},{1,9},{5... | collective-permute-start | bytes 786440 | tf_op jit(solution)/shard_map/ppermute | solution.py:177
  114.6 6.4 %collective-permute-start.36 = (f32[2,2,64,256]{3,2,0,1:T(8,128)S(1)}, f32[2,2,64,256]{3,2,0,1:T(8,128)S(1)}, u32[]{:S(2)}, u32[]{:S(2)}) collective-permute-start(f32[2,2,64,256]{3,2,0,1:T(8,128)S(1)} %maximum_select_fusion.2), channel_id=1, source_target_pairs={{0,4},{4,0},{8,12},{12,8},{16,20},{20,16},{24,28},{28,24},{1,5},{5... | collective-permute-start | bytes 786440 | tf_op jit(solution)/shard_map/ppermute | solution.py:177
